TPU v7x, 256 devices: a whole 4x4x8 slice. The times are simulated.
256 devices in a mesh: seg: 4 (over x_lo, core), utt: 64 (over y, x_hi, z).
Axes of the slice: x: 4 (x_hi: 2, x_lo: 2; x = x_hi * 2 + x_lo), y: 4, z: 8, core: 2. Of those that a mesh axis runs over, the one named last changes fastest.
Arguments:
- audio_waves: float32 [64, 4096], P('utt', 'seg'), may hold values from -6 to 6
- lengths: int32 [64], P('utt'), may hold values from 1024 to 4096
- target_ids: int32 [64, 32], P('utt', 'seg'), may hold values from 0 to 255
- input_weight: float32 [128], replicated, may hold values from -4 to 4
- conv_weight: bfloat16 [10, 256, 512], replicated, may hold values from -0.375 to 0.375
- res_weight: bfloat16 [9, 256, 128], replicated, may hold values from -0.375 to 0.375
- skip_weight: bfloat16 [2560, 1024], replicated, may hold values from -0.375 to 0.375
Outputs:
- gram: float32 [1024, 1024], P(('seg', 'utt'))
- cross: float32 [1024, 256], P(('seg', 'utt'))
All inputs are finite; a program needn't handle non-finite values.
Results may differ from a plain program's by a relative error of at most 0.0023.
Values may be sent and summed in bfloat16 or wider, within the bound.
No kernel may reach another device: no remote copies, remote signals or barrier semaphores. Data moves between devices by JAX's collectives and lax.ppermute only.
A program may use at most 64 MiB of HBM per device.

v0:
```python
import jax
import jax.numpy as jnp
from jax import lax
from jax.sharding import PartitionSpec as P

CLASSES = 256
FRAME = 128


HALF_ROOT = 0.7071067811865476


def shifted(value, axis, by):
    length = lax.axis_size(axis)
    pairs = [(i, i + by) for i in range(length) if 0 <= i + by < length]
    return lax.ppermute(value, axis, pairs)


def layer_math(delayed, current, conv_one, res_one):
    batch_rows, time_rows, channels = current.shape
    paired = jnp.concatenate([delayed, current], 2).reshape(batch_rows * time_rows, 2 * channels)
    preact = jnp.dot(paired, conv_one, preferred_element_type=jnp.float32)
    gate_width = preact.shape[1] // 2
    gated = (jnp.tanh(preact[:, :gate_width]) * jax.nn.sigmoid(preact[:, gate_width:])).astype(
        jnp.bfloat16
    )
    following = None
    if res_one is not None:
        residual_term = jnp.dot(gated, res_one, preferred_element_type=jnp.float32)
        flat_current = current.reshape(batch_rows * time_rows, channels).astype(jnp.float32)
        following = (
            ((flat_current + residual_term) * HALF_ROOT)
            .astype(jnp.bfloat16)
            .reshape(batch_rows, time_rows, channels)
        )
    return (gated.reshape(batch_rows, time_rows, gate_width), following)


def per_device(
    audio_waves, lengths, target_ids, input_weight, conv_weight, res_weight, skip_weight
):
    batch_rows, seg_len = audio_waves.shape
    layer_total = conv_weight.shape[0]
    gated_list = []
    hidden = (audio_waves[:, :, None] * input_weight[None, None, :]).astype(jnp.bfloat16)
    for layer_num in range(layer_total):
        dilation = 2**layer_num
        tail_rows = hidden[:, seg_len - dilation :, :]
        earlier = shifted(tail_rows, "seg", 1)
        delayed = jnp.concatenate([earlier, hidden[:, : seg_len - dilation, :]], 1)
        res_one = res_weight[layer_num] if layer_num < layer_total - 1 else None
        gated, hidden = layer_math(delayed, hidden, conv_weight[layer_num], res_one)
        gated_list.append(gated)
    stacked = jnp.concatenate(gated_list, 2).reshape(batch_rows * seg_len, skip_weight.shape[0])
    skip_sum = jnp.dot(stacked, skip_weight, preferred_element_type=jnp.float32)
    features = jnp.maximum(skip_sum, 0.0).astype(jnp.bfloat16)
    skip_width = features.shape[1]
    position = lax.axis_index("seg") * seg_len + jnp.arange(seg_len, dtype=jnp.int32)
    valid = (position[None, :] < lengths[:, None]).reshape(batch_rows * seg_len)
    masked = jnp.where(valid[:, None], features, jnp.zeros_like(features))
    frame_ids = jnp.repeat(target_ids, FRAME, axis=1).reshape(batch_rows * seg_len)
    onehot = (frame_ids[:, None] == jnp.arange(CLASSES, dtype=jnp.int32)[None, :]).astype(
        jnp.bfloat16
    )
    paired = jnp.concatenate([masked, onehot], 1)
    valid_total = lax.psum(jnp.sum(valid.astype(jnp.float32)), ("seg", "utt"))
    owned_rows = lax.psum_scatter(
        lax.dot_general(
            masked, paired, (((0,), (0,)), ((), ())), preferred_element_type=jnp.float32
        ),
        ("seg", "utt"),
        scatter_dimension=0,
        tiled=True,
    )
    gram_rows = owned_rows[:, :skip_width] / valid_total
    cross_rows = owned_rows[:, skip_width:] * (CLASSES / valid_total)
    return (gram_rows, cross_rows)


def solution(mesh):
    in_specs = (P("utt", "seg"), P("utt"), P("utt", "seg"), P(), P(), P(), P())
    out_specs = (P(("seg", "utt"), None), P(("seg", "utt"), None))
    return jax.shard_map(
        per_device, mesh=mesh, in_specs=in_specs, out_specs=out_specs, check_vma=False
    )
```

profile of v0, /device:TPU:28, one launch (start us, length us, event | category | flops | bytes accessed | tf_op | source)
XLA Modules:
  0.0 382.8 jit_solution(8602478082041737052)
XLA Ops:
  8.1 1.7 collective-permute-start
  10.7 1.5 fusion.80
  12.2 1.2 bitcast_dynamic-update-slice_fusion.9
  13.8 3.3 collective-permute-start.1
  18.4 1.2 bitcast_dynamic-update-slice_fusion.8
  20.0 4.1 %collective-permute-start.2 = (bf16[1,4,128]{2,1,0:T(4,128)(2,1)S(1)}, bf16[1,4,128]{2,1,0:T(4,128)(2,1)S(1)}, u32[]{:S(2)}, u32[]{:S(2)}) collective-permute-start(bf16[1,4,128]{2,1,0:T(4,128)(2,1)S(1)} %slice.252), channel_id=1, source_target_pairs={{0,64},{64,128},{128,192},{1,65},{65,129},{129,193},{2,66},{66,130... | collective-permute-start | bytes 3080 | tf_op jit(solution)/shard_map/ppermute | solution.py:16
  25.4 1.2 bitcast_dynamic-update-slice_fusion.7
  27.0 4.1 %collective-permute-start.3 = (bf16[1,8,128]{2,1,0:T(8,128)(2,1)S(1)}, bf16[1,8,128]{2,1,0:T(8,128)(2,1)S(1)}, u32[]{:S(2)}, u32[]{:S(2)}) collective-permute-start(bf16[1,8,128]{2,1,0:T(8,128)(2,1)S(1)} %slice.256), channel_id=1, source_target_pairs={{0,64},{64,128},{128,192},{1,65},{65,129},{129,193},{2,66},{66,130... | collective-permute-start | bytes 6152 | tf_op jit(solution)/shard_map/ppermute | solution.py:16
  32.4 1.2 bitcast_dynamic-update-slice_fusion.6
  34.0 4.1 %collective-permute-start.4 = (bf16[1,16,128]{2,1,0:T(8,128)(2,1)S(1)}, bf16[1,16,128]{2,1,0:T(8,128)(2,1)S(1)}, u32[]{:S(2)}, u32[]{:S(2)}) collective-permute-start(bf16[1,16,128]{2,1,0:T(8,128)(2,1)S(1)} %slice.260), channel_id=1, source_target_pairs={{0,64},{64,128},{128,192},{1,65},{65,129},{129,193},{2,66},{66,130... | collective-permute-start | bytes 12296 | tf_op jit(solution)/shard_map/ppermute | solution.py:16
  39.4 1.2 bitcast_dynamic-update-slice_fusion.5
  41.0 4.1 %collective-permute-start.5 = (bf16[1,32,128]{2,1,0:T(8,128)(2,1)S(1)}, bf16[1,32,128]{2,1,0:T(8,128)(2,1)S(1)}, u32[]{:S(2)}, u32[]{:S(2)}) collective-permute-start(bf16[1,32,128]{2,1,0:T(8,128)(2,1)S(1)} %slice.264), channel_id=1, source_target_pairs={{0,64},{64,128},{128,192},{1,65},{65,129},{129,193},{2,66},{66,130... | collective-permute-start | bytes 24584 | tf_op jit(solution)/shard_map/ppermute | solution.py:16
  48.0 4.2 %collective-permute-start.6 = (bf16[1,64,128]{2,1,0:T(8,128)(2,1)S(1)}, bf16[1,64,128]{2,1,0:T(8,128)(2,1)S(1)}, u32[]{:S(2)}, u32[]{:S(2)}) collective-permute-start(bf16[1,64,128]{2,1,0:T(8,128)(2,1)S(1)} %slice.268), channel_id=1, source_target_pairs={{0,64},{64,128},{128,192},{1,65},{65,129},{129,193},{2,66},{66,130... | collective-permute-start | bytes 49160 | tf_op jit(solution)/shard_map/ppermute | solution.py:16
  55.0 4.2 %collective-permute-start.7 = (bf16[1,128,128]{2,1,0:T(8,128)(2,1)S(1)}, bf16[1,128,128]{2,1,0:T(8,128)(2,1)S(1)}, u32[]{:S(2)}, u32[]{:S(2)}) collective-permute-start(bf16[1,128,128]{2,1,0:T(8,128)(2,1)S(1)} %slice.272), channel_id=1, source_target_pairs={{0,64},{64,128},{128,192},{1,65},{65,129},{129,193},{2,66},{66,130... | collective-permute-start | bytes 98312 | tf_op jit(solution)/shard_map/ppermute | solution.py:16
  62.2 4.4 %collective-permute-start.8 = (bf16[1,256,128]{2,1,0:T(8,128)(2,1)S(1)}, bf16[1,256,128]{2,1,0:T(8,128)(2,1)S(1)}, u32[]{:S(2)}, u32[]{:S(2)}) collective-permute-start(bf16[1,256,128]{2,1,0:T(8,128)(2,1)S(1)} %slice.276), channel_id=1, source_target_pairs={{0,64},{64,128},{128,192},{1,65},{65,129},{129,193},{2,66},{66,130... | collective-permute-start | bytes 196616 | tf_op jit(solution)/shard_map/ppermute | solution.py:16
  70.2 5.3 %collective-permute-start.9 = (bf16[1,512,128]{2,1,0:T(8,128)(2,1)}, bf16[1,512,128]{2,1,0:T(8,128)(2,1)}, u32[]{:S(2)}, u32[]{:S(2)}) collective-permute-start(bf16[1,512,128]{2,1,0:T(8,128)(2,1)} %get-tuple-element.20), channel_id=1, source_target_pairs={{0,64},{64,128},{128,192},{1,65},{65,129},{129,193},{2,66},{66,130... | collective-permute-start | bytes 393224 | tf_op jit(solution)/shard_map/ppermute | solution.py:16
  76.3 1.4 fusion.125
  77.7 1.2 bitcast_dynamic-update-slice_fusion
  78.9 9.1 %broadcast_select_fusion = bf16[1024,1024]{0,1:T(8,128)(2,1)S(1)} fusion(pred[1024]{0:T(1024)(128)(4,1)S(1)} %add_compare_fusion, bf16[2560,1024]{1,0:T(8,128)(2,1)} %param.13, bf16[1,1024,2560]{1,2,0:T(8,128)(2,1)} %bitcast_dynamic-update-slice_fusion), kind=kOutput, calls=%fused_computation.7 | convolution fusion | flops 5371854848 | bytes 12583936 | tf_op jit(solution)/shard_map/dot_general | solution.py:55
  88.0 4.7 %fusion.2 = f32[1024,1280]{1,0:T(8,128)} fusion(bf16[1024,1024]{0,1:T(8,128)(2,1)S(1)} %broadcast_select_fusion, bf16[1024,256]{0,1:T(8,128)(2,1)S(1)} %fusion.79), kind=kOutput, calls=%fused_computation.3 | convolution fusion | flops 2689597440 | bytes 7864320 | tf_op jit(solution)/shard_map/dot_general | solution.py:68
  93.4 80.7 %psum.7 = f32[]{:T(128)} all-reduce(f32[]{:T(128)} %convert_reduce_fusion), channel_id=1, replica_groups=mesh['seg'=4,'utt'=64] {'seg','utt'}, use_global_device_ids=true, to_apply=%region_2.3 | all-reduce | flops 1 | bytes 8 | tf_op jit(solution)/shard_map/psum | solution.py:66
  174.8 197.8 %all-reduce.3.cloned.1.call-done = f32[1024,1280]{1,0:T(8,128)} async-done(((f32[1024,1280]{1,0:T(8,128)}), f32[1024,1280]{1,0:T(8,128)}) %all-reduce.3.cloned.1.call-update) | async-done | bytes 5242896
  372.6 2.0 dynamic-slice_divide_fusion
  374.6 1.4 dynamic-slice_multiply_fusion
  (64 shorter events, 21.6 us)
Async XLA Ops:
  7.2 59.4 %copy-start = (s32[1,8]{1,0:T(1,128)S(1)}, s32[1,8]{1,0:T(1,128)}, u32[]{:S(2)}) copy-start(s32[1,8]{1,0:T(1,128)} %param.9) | copy-start | bytes 100
  7.2 365.4 %all-reduce.3.cloned.1.call-start = ((), (), s32[]{:S(2)}) async-start(), calls=%async_computation | async-start | bytes 10485760
  8.1 2.5 collective-permute-start
  10.7 2.7 copy-start.2
  10.7 2.7 copy-start.3
  10.7 2.7 copy-start.4
  12.2 5.7 %copy-start.1 = (bf16[10,256,512]{2,1,0:T(8,128)(2,1)S(1)}, bf16[10,256,512]{2,1,0:T(8,128)(2,1)}, u32[]{:S(2)}) copy-start(bf16[10,256,512]{2,1,0:T(8,128)(2,1)} %param.11) | copy-start | bytes 7864324
  13.8 4.1 %collective-permute-start.1 = (bf16[1,2,128]{2,1,0:T(2,128)(2,1)S(1)}, bf16[1,2,128]{2,1,0:T(2,128)(2,1)S(1)}, u32[]{:S(2)}, u32[]{:S(2)}) collective-permute-start(bf16[1,2,128]{2,1,0:T(2,128)(2,1)S(1)} %slice.248), channel_id=1, source_target_pairs={{0,64},{64,128},{128,192},{1,65},{65,129},{129,193},{2,66},{66,130... | collective-permute-start | bytes 1544 | tf_op jit(solution)/shard_map/ppermute | solution.py:16
  20.0 4.9 %collective-permute-start.2 = (bf16[1,4,128]{2,1,0:T(4,128)(2,1)S(1)}, bf16[1,4,128]{2,1,0:T(4,128)(2,1)S(1)}, u32[]{:S(2)}, u32[]{:S(2)}) collective-permute-start(bf16[1,4,128]{2,1,0:T(4,128)(2,1)S(1)} %slice.252), channel_id=1, source_target_pairs={{0,64},{64,128},{128,192},{1,65},{65,129},{129,193},{2,66},{66,130... | collective-permute-start | bytes 3080 | tf_op jit(solution)/shard_map/ppermute | solution.py:16
  27.0 4.9 %collective-permute-start.3 = (bf16[1,8,128]{2,1,0:T(8,128)(2,1)S(1)}, bf16[1,8,128]{2,1,0:T(8,128)(2,1)S(1)}, u32[]{:S(2)}, u32[]{:S(2)}) collective-permute-start(bf16[1,8,128]{2,1,0:T(8,128)(2,1)S(1)} %slice.256), channel_id=1, source_target_pairs={{0,64},{64,128},{128,192},{1,65},{65,129},{129,193},{2,66},{66,130... | collective-permute-start | bytes 6152 | tf_op jit(solution)/shard_map/ppermute | solution.py:16
  34.0 4.9 %collective-permute-start.4 = (bf16[1,16,128]{2,1,0:T(8,128)(2,1)S(1)}, bf16[1,16,128]{2,1,0:T(8,128)(2,1)S(1)}, u32[]{:S(2)}, u32[]{:S(2)}) collective-permute-start(bf16[1,16,128]{2,1,0:T(8,128)(2,1)S(1)} %slice.260), channel_id=1, source_target_pairs={{0,64},{64,128},{128,192},{1,65},{65,129},{129,193},{2,66},{66,130... | collective-permute-start | bytes 12296 | tf_op jit(solution)/shard_map/ppermute | solution.py:16
  41.0 4.9 %collective-permute-start.5 = (bf16[1,32,128]{2,1,0:T(8,128)(2,1)S(1)}, bf16[1,32,128]{2,1,0:T(8,128)(2,1)S(1)}, u32[]{:S(2)}, u32[]{:S(2)}) collective-permute-start(bf16[1,32,128]{2,1,0:T(8,128)(2,1)S(1)} %slice.264), channel_id=1, source_target_pairs={{0,64},{64,128},{128,192},{1,65},{65,129},{129,193},{2,66},{66,130... | collective-permute-start | bytes 24584 | tf_op jit(solution)/shard_map/ppermute | solution.py:16
  48.0 5.0 %collective-permute-start.6 = (bf16[1,64,128]{2,1,0:T(8,128)(2,1)S(1)}, bf16[1,64,128]{2,1,0:T(8,128)(2,1)S(1)}, u32[]{:S(2)}, u32[]{:S(2)}) collective-permute-start(bf16[1,64,128]{2,1,0:T(8,128)(2,1)S(1)} %slice.268), channel_id=1, source_target_pairs={{0,64},{64,128},{128,192},{1,65},{65,129},{129,193},{2,66},{66,130... | collective-permute-start | bytes 49160 | tf_op jit(solution)/shard_map/ppermute | solution.py:16
  55.0 5.1 %collective-permute-start.7 = (bf16[1,128,128]{2,1,0:T(8,128)(2,1)S(1)}, bf16[1,128,128]{2,1,0:T(8,128)(2,1)S(1)}, u32[]{:S(2)}, u32[]{:S(2)}) collective-permute-start(bf16[1,128,128]{2,1,0:T(8,128)(2,1)S(1)} %slice.272), channel_id=1, source_target_pairs={{0,64},{64,128},{128,192},{1,65},{65,129},{129,193},{2,66},{66,130... | collective-permute-start | bytes 98312 | tf_op jit(solution)/shard_map/ppermute | solution.py:16
  62.2 5.2 %collective-permute-start.8 = (bf16[1,256,128]{2,1,0:T(8,128)(2,1)S(1)}, bf16[1,256,128]{2,1,0:T(8,128)(2,1)S(1)}, u32[]{:S(2)}, u32[]{:S(2)}) collective-permute-start(bf16[1,256,128]{2,1,0:T(8,128)(2,1)S(1)} %slice.276), channel_id=1, source_target_pairs={{0,64},{64,128},{128,192},{1,65},{65,129},{129,193},{2,66},{66,130... | collective-permute-start | bytes 196616 | tf_op jit(solution)/shard_map/ppermute | solution.py:16
  70.2 6.1 %collective-permute-start.9 = (bf16[1,512,128]{2,1,0:T(8,128)(2,1)}, bf16[1,512,128]{2,1,0:T(8,128)(2,1)}, u32[]{:S(2)}, u32[]{:S(2)}) collective-permute-start(bf16[1,512,128]{2,1,0:T(8,128)(2,1)} %get-tuple-element.20), channel_id=1, source_target_pairs={{0,64},{64,128},{128,192},{1,65},{65,129},{129,193},{2,66},{66,130... | collective-permute-start | bytes 393224 | tf_op jit(solution)/shard_map/ppermute | solution.py:16
Sparse Core Ops, SparseCore 0:
  92.9 279.6 all-reduce.2
where the time goes:
time: 384 us; the launch traced here: 383 us
  waiting for transfers between devices  205 us (53%)
  blocking collectives  80.7 us (21%)
  starting transfers between devices  39.5 us (10%)
  matrix products  23.8 us (6%)
  other arithmetic  17.2 us (4%)
  between operations  15.8 us (4%)
    unnamed x2, waiting for transfers between devices  198 us
    psum x1, blocking collectives, per_device(): valid_total = lax.psum(jnp.sum(valid.astype(jnp.float32)), ('seg', 'utt'))  80.7 us
    ppermute x10, starting transfers between devices, shifted(): return lax.ppermute(value, axis, pairs)  39.4 us
    unnamed x9, other arithmetic  11 us
    dot_general x1, matrix products, per_device(): skip_sum = jnp.dot(stacked, skip_weight, preferred_element_type=jnp.float32)  9.14 us
  transfers between devices with their start and end apart: 11, of which 10 were waited for; matrix products, arithmetic and copies ran while one was open for 0% of the time, Pallas kernels for 0%

commit v1 on v0

v1 whole, which is shorter than its diff:
```python
import jax
import jax.numpy as jnp
from jax import lax
from jax.sharding import PartitionSpec as P

CLASSES = 256
FRAME = 128


HALF_ROOT = 0.7071067811865476


def shifted(value, axis, by):
    length = lax.axis_size(axis)
    pairs = [(i, i + by) for i in range(length) if 0 <= i + by < length]
    return lax.ppermute(value, axis, pairs)


def round_up(value, step):
    return -(-value // step) * step


def layer_math(delayed, current, conv_one, res_one):
    channels = current.shape[1]
    paired = jnp.concatenate([delayed, current], 1)
    preact = jnp.dot(paired, conv_one, preferred_element_type=jnp.float32)
    gate_width = preact.shape[1] // 2
    gated = (jnp.tanh(preact[:, :gate_width]) * jax.nn.sigmoid(preact[:, gate_width:])).astype(
        jnp.bfloat16
    )
    following = None
    if res_one is not None:
        residual_term = jnp.dot(gated, res_one, preferred_element_type=jnp.float32)
        following = ((current.astype(jnp.float32) + residual_term) * HALF_ROOT).astype(
            jnp.bfloat16
        )
    return gated, following


def per_device(
    audio_waves, lengths, target_ids, input_weight, conv_weight, res_weight, skip_weight
):
    batch_rows, seg_len = audio_waves.shape
    layer_total = conv_weight.shape[0]
    reach = 2**layer_total - 1
    earlier = shifted(audio_waves, "seg", 1)
    window = round_up(seg_len + reach, 16)
    extended = jnp.concatenate([earlier, audio_waves], 1)[0, 2 * seg_len - window :]
    hidden = (extended[:, None] * input_weight[None, :]).astype(jnp.bfloat16)
    gated_list = []
    for layer_num in range(layer_total):
        dilation = 2**layer_num
        later_reach = 2**layer_total - 2 ** (layer_num + 1)
        in_len = hidden.shape[0]
        out_len = min(in_len, round_up(seg_len + later_reach, 16))
        if in_len - dilation >= out_len:
            delayed = hidden[in_len - out_len - dilation : in_len - dilation]
        else:
            delayed = jnp.concatenate(
                [jnp.zeros((dilation, hidden.shape[1]), hidden.dtype), hidden[: in_len - dilation]],
                0,
            )
        current = hidden[in_len - out_len :]
        res_one = res_weight[layer_num] if layer_num < layer_total - 1 else None
        gated, hidden = layer_math(delayed, current, conv_weight[layer_num], res_one)
        gated_list.append(gated[out_len - seg_len :])
    stacked = jnp.concatenate(gated_list, 1)
    skip_sum = jnp.dot(stacked, skip_weight, preferred_element_type=jnp.float32)
    features = jnp.maximum(skip_sum, 0.0).astype(jnp.bfloat16)
    skip_width = features.shape[1]
    position = lax.axis_index("seg") * seg_len + jnp.arange(seg_len, dtype=jnp.int32)
    valid = (position[None, :] < lengths[:, None]).reshape(batch_rows * seg_len)
    masked = jnp.where(valid[:, None], features, jnp.zeros_like(features))
    frame_ids = jnp.repeat(target_ids, FRAME, axis=1).reshape(batch_rows * seg_len)
    onehot = (frame_ids[:, None] == jnp.arange(CLASSES, dtype=jnp.int32)[None, :]).astype(
        jnp.bfloat16
    )
    paired = jnp.concatenate([masked, onehot], 1)
    valid_total = lax.psum(jnp.sum(lengths), "utt").astype(jnp.float32)
    partial = lax.dot_general(
        masked, paired, (((0,), (0,)), ((), ())), preferred_element_type=jnp.float32
    )
    owners = lax.axis_size("seg") * lax.axis_size("utt")
    row_count = partial.shape[0] // owners
    width = partial.shape[1]
    slab = partial.reshape(owners, 8, row_count * width // 8)
    owned = lax.psum_scatter(slab, ("seg", "utt"), scatter_dimension=0, tiled=True)
    owned_rows = owned.reshape(row_count, width)
    gram_rows = owned_rows[:, :skip_width] / valid_total
    cross_rows = owned_rows[:, skip_width:] * (CLASSES / valid_total)
    return (gram_rows, cross_rows)


def solution(mesh):
    in_specs = (P("utt", "seg"), P("utt"), P("utt", "seg"), P(), P(), P(), P())
    out_specs = (P(("seg", "utt"), None), P(("seg", "utt"), None))
    return jax.shard_map(
        per_device, mesh=mesh, in_specs=in_specs, out_specs=out_specs, check_vma=False
    )
```

time: 384 us -> 1400 us (3.65); the launches traced: 383 us -> 1380 us
  waiting for transfers between devices: 205 us -> 1300 us
  blocking collectives: 80.7 us -> 23.8 us
  starting transfers between devices: 39.5 us -> 1.78 us
    unnamed x2, waiting for transfers between devices: 198 us -> 1300 us
    psum x1, blocking collectives: 80.7 us -> 23.8 us  [per_device(): valid_total = lax.psum(jnp.sum(lengths), 'utt').astype(jnp.float32)]
    ppermute x10 -> x1, starting transfers between devices: 39.4 us -> 1.74 us  [shifted(): return lax.ppermute(value, axis, pairs)]
  transfers between devices with their start and end apart: 11 -> 2, of which waited for: 10 -> 2; matrix products, arithmetic and copies ran while one was open for 0% -> 0% of each run, Pallas kernels for 0% -> 0%
where the time goes in v1:
time: 1400 us; the launch traced here: 1380 us
  waiting for transfers between devices  1300 us (93%)
  blocking collectives  23.8 us (2%)
  matrix products  23.3 us (2%)
  between operations  15.7 us (1%)
    unnamed x2, waiting for transfers between devices  1300 us
  transfers between devices with their start and end apart: 2, of which 2 were waited for; matrix products, arithmetic and copies ran while one was open for 0% of the time, Pallas kernels for 0%

profile of v1, /device:TPU:28, one launch (start us, length us, event | category | flops | bytes accessed | tf_op | source)
XLA Modules:
  0.0 1382.5 jit_solution(6084020557514572608)
XLA Ops:
  7.2 1.7 collective-permute-start
  10.7 1.0 multiply_convert_fusion
  11.7 1.7 fusion.71
  13.4 0.8 fusion.49
  15.1 0.9 copy-done.2
  16.0 0.8 fusion.74
  16.8 0.8 fusion.50
  18.2 0.8 fusion.77
  18.9 0.8 fusion.51
  20.4 0.8 fusion.94
  21.2 0.8 fusion.52
  22.8 0.8 fusion.98
  23.5 0.8 fusion.53
  25.2 1.0 fusion.102
  26.1 0.8 fusion.54
  27.8 0.8 fusion.106
  28.5 0.8 fusion.59
  30.6 0.7 fusion.64
  35.3 5.9 broadcast_select_fusion
  41.2 4.7 fusion
  45.9 6.8 reshape.27
  52.7 23.8 %psum.7 = s32[]{:T(128)} all-reduce(s32[]{:T(128)} %bitcast), channel_id=1, replica_groups=mesh['seg'=4,'utt'=64] {'utt'}, use_global_device_ids=true, to_apply=%region_1.2 | all-reduce | flops 1 | bytes 8 | tf_op jit(solution)/shard_map/psum | solution.py:79
  77.1 1296.6 %reduce-scatter.5.cloned.1.call-done = f32[1,8,640]{2,1,0:T(8,128)} async-done(((f32[256,8,640]{2,1,0:T(8,128)}), f32[1,8,640]{2,1,0:T(8,128)}) %reduce-scatter.5.cloned.1.call-update) | async-done | bytes 20496
  1373.7 0.7 reshape.28
  (53 shorter events, 11.8 us)
Async XLA Ops:
  7.2 2.5 copy-start
  7.2 1366.5 %reduce-scatter.5.cloned.1.call-start = ((), (), s32[]{:S(2)}) async-start(), calls=%async_computation.1 | async-start | bytes 5263360
  7.2 2.8 collective-permute-start
  13.4 1.1 copy-start.3
  13.4 1.1 copy-start.4
  14.2 1.8 copy-start.2
  32.5 2.2 slice-start
  33.6 1.7 slice-start.1
  52.6 1323.0 %copy-start.1 = (s32[1,8]{1,0:T(1,128)S(1)}, s32[1,8]{1,0:T(1,128)}, u32[]{:S(2)}) copy-start(s32[1,8]{1,0:T(1,128)} %param.9) | copy-start | bytes 100
Sparse Core Ops, SparseCore 0:
  52.8 1320.8 reduce-scatter.4

commit v2 on v1

--- a/solution.py
+++ b/solution.py
@@ -1,7 +1,7 @@
 import jax
 import jax.numpy as jnp
 from jax import lax
-from jax.sharding import PartitionSpec as P
+from jax.sharding import Mesh, PartitionSpec as P
 
 CLASSES = 256
 FRAME = 128
@@ -10,8 +10,22 @@
 HALF_ROOT = 0.7071067811865476
 
 
+SEG = ("xl", "core")
+UTT = ("y", "xh", "z")
+FINE = SEG + UTT
+STAGES = ("core", "z", "y", "xh", "xl")
+
+
+def fine_sizes(seg_size, utt_size):
+    z = 8 if utt_size % 8 == 0 else utt_size
+    xh = 2 if (utt_size // z) % 2 == 0 else 1
+    return {"xl": seg_size // 2, "core": 2, "y": utt_size // (z * xh), "xh": xh, "z": z}
+
+
 def shifted(value, axis, by):
-    length = lax.axis_size(axis)
+    length = 1
+    for name in axis:
+        length *= lax.axis_size(name)
     pairs = [(i, i + by) for i in range(length) if 0 <= i + by < length]
     return lax.ppermute(value, axis, pairs)
 
@@ -43,7 +57,7 @@
     batch_rows, seg_len = audio_waves.shape
     layer_total = conv_weight.shape[0]
     reach = 2**layer_total - 1
-    earlier = shifted(audio_waves, "seg", 1)
+    earlier = shifted(audio_waves, SEG, 1)
     window = round_up(seg_len + reach, 16)
     extended = jnp.concatenate([earlier, audio_waves], 1)[0, 2 * seg_len - window :]
     hidden = (extended[:, None] * input_weight[None, :]).astype(jnp.bfloat16)
@@ -68,7 +82,7 @@
     skip_sum = jnp.dot(stacked, skip_weight, preferred_element_type=jnp.float32)
     features = jnp.maximum(skip_sum, 0.0).astype(jnp.bfloat16)
     skip_width = features.shape[1]
-    position = lax.axis_index("seg") * seg_len + jnp.arange(seg_len, dtype=jnp.int32)
+    position = lax.axis_index(SEG) * seg_len + jnp.arange(seg_len, dtype=jnp.int32)
     valid = (position[None, :] < lengths[:, None]).reshape(batch_rows * seg_len)
     masked = jnp.where(valid[:, None], features, jnp.zeros_like(features))
     frame_ids = jnp.repeat(target_ids, FRAME, axis=1).reshape(batch_rows * seg_len)
@@ -76,24 +90,34 @@
         jnp.bfloat16
     )
     paired = jnp.concatenate([masked, onehot], 1)
-    valid_total = lax.psum(jnp.sum(lengths), "utt").astype(jnp.float32)
+    valid_total = lax.psum(lengths.astype(jnp.float32), UTT)[0]
     partial = lax.dot_general(
         masked, paired, (((0,), (0,)), ((), ())), preferred_element_type=jnp.float32
     )
-    owners = lax.axis_size("seg") * lax.axis_size("utt")
+    sizes = {name: lax.axis_size(name) for name in FINE}
+    owners = 1
+    for name in FINE:
+        owners *= sizes[name]
     row_count = partial.shape[0] // owners
     width = partial.shape[1]
-    slab = partial.reshape(owners, 8, row_count * width // 8)
-    owned = lax.psum_scatter(slab, ("seg", "utt"), scatter_dimension=0, tiled=True)
-    owned_rows = owned.reshape(row_count, width)
+    blocks = partial.reshape(tuple(sizes[n] for n in FINE) + (row_count, width))
+    order = tuple(FINE.index(n) for n in STAGES) + (len(FINE), len(FINE) + 1)
+    slab = blocks.transpose(order).reshape(
+        tuple(sizes[n] for n in STAGES) + (8, row_count * width // 8)
+    )
+    for stage, name in enumerate(STAGES):
+        slab = lax.psum_scatter(slab, name, scatter_dimension=stage, tiled=True)
+    owned_rows = slab.reshape(row_count, width)
     gram_rows = owned_rows[:, :skip_width] / valid_total
     cross_rows = owned_rows[:, skip_width:] * (CLASSES / valid_total)
     return (gram_rows, cross_rows)
 
 
 def solution(mesh):
-    in_specs = (P("utt", "seg"), P("utt"), P("utt", "seg"), P(), P(), P(), P())
-    out_specs = (P(("seg", "utt"), None), P(("seg", "utt"), None))
+    sizes = fine_sizes(mesh.shape["seg"], mesh.shape["utt"])
+    fine = Mesh(mesh.devices.reshape(tuple(sizes[n] for n in FINE)), FINE)
+    in_specs = (P(UTT, SEG), P(UTT), P(UTT, SEG), P(), P(), P(), P())
+    out_specs = (P(FINE, None), P(FINE, None))
     return jax.shard_map(
-        per_device, mesh=mesh, in_specs=in_specs, out_specs=out_specs, check_vma=False
+        per_device, mesh=fine, in_specs=in_specs, out_specs=out_specs, check_vma=False
     )

time: 1400 us -> 376 us (0.27)
  the two profiles are of different devices: /device:TPU:28 before, /device:TPU:2 now
where the time goes in v2:
time: 376 us; the launch traced here: 375 us
  blocking collectives  184 us (49%)
  waiting for transfers between devices  115 us (31%)
  local copies, waits for them, and re-layouts  24 us (6%)
  matrix products  23.3 us (6%)
  between operations  15.5 us (4%)
  other arithmetic  11.1 us (3%)
    psum x1, blocking collectives, per_device(): valid_total = lax.psum(lengths.astype(jnp.float32), UTT)[0]  184 us
    reduce_scatter x4, waiting for transfers between devices, per_device(): slab = lax.psum_scatter(slab, name, scatter_dimension=stage, tiled=True)  113 us
    reshape x2, local copies, waits for them, and re-layouts, per_device(): blocks.transpose(order)  13 us
    dot_general x10, matrix products, layer_math(): preact = jnp.dot(paired, conv_one, preferred_element_type=jnp.float32)  8.26 us
  transfers between devices with their start and end apart: 6, of which 5 were waited for; matrix products, arithmetic and copies ran while one was open for 0% of the time, Pallas kernels for 0%

profile of v2, /device:TPU:2, one launch (start us, length us, event | category | flops | bytes accessed | tf_op | source)
XLA Modules:
  0.0 374.9 jit_solution(3123613729911916969)
XLA Ops:
  7.2 1.9 collective-permute-start
  10.0 2.3 collective-permute-done
  13.1 1.0 multiply_convert_fusion
  14.1 1.7 fusion.71
  15.8 0.8 fusion.49
  17.5 0.9 copy-done.2
  19.2 0.8 fusion.50
  21.3 0.8 fusion.51
  23.5 0.8 fusion.52
  25.9 0.8 fusion.53
  27.6 1.0 fusion.102
  28.5 0.8 fusion.54
  30.9 0.8 fusion.59
  37.7 5.9 %broadcast_select_fusion = bf16[1024,1024]{0,1:T(8,128)(2,1)S(1)} fusion(pred[1024]{0:T(1024)(128)(4,1)S(1)} %add_compare_fusion, bf16[1024,2560]{0,1:T(8,128)(2,1)S(1)} %fusion.118, bf16[2560,1024]{1,0:T(8,128)(2,1)S(1)} %bitcast.95), kind=kOutput, calls=%fused_computation.78 | convolution fusion | flops 5371854848 | bytes 12583936 | tf_op jit(solution)/shard_map/dot_general | solution.py:82
  43.6 4.7 %fusion = f32[1024,1280]{1,0:T(8,128)} fusion(bf16[1024,1024]{0,1:T(8,128)(2,1)S(1)} %broadcast_select_fusion, bf16[1024,256]{0,1:T(8,128)(2,1)S(1)} %fusion.93), kind=kOutput, calls=%fused_computation.1 | convolution fusion | flops 2689597440 | bytes 7864320 | tf_op jit(solution)/shard_map/dot_general | solution.py:94
  48.3 7.1 %reshape.29 = f32[2,2,4,2,8,4,1280]{6,5,4,3,2,1,0:T(4,128)} reshape(f32[1024,1280]{1,0:T(8,128)} %fusion) | data formatting | bytes 10485760 | tf_op jit(solution)/shard_map/reshape | solution.py:103
  55.4 7.5 %reshape.32 = f32[2,8,4,2,2,8,640]{6,5,1,3,2,0,4:T(8,128)} reshape(f32[2,8,4,2,2,4,1280]{6,5,1,3,2,0,4:T(4,128)} %bitcast.88) | data formatting | bytes 10485760 | tf_op jit(solution)/shard_map/reshape | solution.py:105
  62.9 5.5 %copy.35 = f32[2,8,4,2,2,8,640]{6,5,4,3,2,1,0:T(8,128)} copy(f32[2,8,4,2,2,8,640]{6,5,1,3,2,0,4:T(8,128)} %reshape.32) | data formatting | bytes 10485760 | tf_op jit(solution)/shard_map/reshape | solution.py:105
  68.4 21.3 %reduce-scatter.10.cloned.1.call-done = f32[1,8,4,2,2,8,640]{6,5,4,3,2,1,0:T(8,128)} async-done(((f32[2,8,4,2,2,8,640]{6,5,4,3,2,1,0:T(8,128)}), f32[1,8,4,2,2,8,640]{6,5,4,3,2,1,0:T(8,128)}) %reduce-scatter.10.cloned.1.call-update) | async-done | bytes 2621456 | tf_op jit(solution)/shard_map/reduce_scatter | solution.py:109
  89.8 48.0 %reduce-scatter.12.cloned.1.call-done = f32[1,1,4,2,2,8,640]{6,5,4,3,2,1,0:T(8,128)} async-done(((f32[1,8,4,2,2,8,640]{6,5,4,3,2,1,0:T(8,128)}), f32[1,1,4,2,2,8,640]{6,5,4,3,2,1,0:T(8,128)}) %reduce-scatter.12.cloned.1.call-update) | async-done | bytes 327696 | tf_op jit(solution)/shard_map/reduce_scatter | solution.py:109
  137.9 25.4 %reduce-scatter.14.cloned.1.call-done = f32[1,1,1,2,2,8,640]{6,5,4,3,2,1,0:T(8,128)} async-done(((f32[1,1,4,2,2,8,640]{6,5,4,3,2,1,0:T(8,128)}), f32[1,1,1,2,2,8,640]{6,5,4,3,2,1,0:T(8,128)}) %reduce-scatter.14.cloned.1.call-update) | async-done | bytes 81936 | tf_op jit(solution)/shard_map/reduce_scatter | solution.py:109
  163.3 17.9 %reduce-scatter.16.cloned.1.call-done = f32[1,1,1,1,2,8,640]{6,5,4,3,2,1,0:T(8,128)} async-done(((f32[1,1,1,2,2,8,640]{6,5,4,3,2,1,0:T(8,128)}), f32[1,1,1,1,2,8,640]{6,5,4,3,2,1,0:T(8,128)}) %reduce-scatter.16.cloned.1.call-update) | async-done | bytes 40976 | tf_op jit(solution)/shard_map/reduce_scatter | solution.py:109
  181.2 183.8 %psum.7 = f32[]{:T(128)} all-reduce(f32[]{:T(128)} %bitcast.24), channel_id=1, replica_groups=mesh['xl'=2,'core'=2,'y'=4,'xh'=2,'z'=8] {'y','xh','z'}, use_global_device_ids=true, to_apply=%region_5.6 | all-reduce | flops 1 | bytes 8 | tf_op jit(solution)/shard_map/psum | solution.py:93
  366.5 1.3 slice_divide_fusion
  (67 shorter events, 16.5 us)
Async XLA Ops:
  7.2 2.6 copy-start
  7.2 82.5 %reduce-scatter.10.cloned.1.call-start = ((), (), s32[]{:S(2)}) async-start(), calls=%async_computation.5 | async-start | bytes 7864320 | tf_op jit(solution)/shard_map/reduce_scatter | solution.py:109
  7.2 5.1 %collective-permute-start = (f32[1,1024]{1,0:T(1,128)}, f32[1,1024]{1,0:T(1,128)S(1)}, u32[]{:S(2)}, u32[]{:S(2)}) collective-permute-start(f32[1,1024]{1,0:T(1,128)} %param.7), channel_id=1, source_target_pairs={{0,64},{64,128},{128,192},{1,65},{65,129},{129,193},{2,66},{66,130... | collective-permute-start | bytes 12296 | tf_op jit(solution)/shard_map/ppermute | solution.py:30
  15.8 1.1 copy-start.3
  15.8 1.1 copy-start.4
  16.6 1.8 copy-start.2
  35.0 2.2 slice-start
  36.0 1.7 slice-start.1
  68.4 299.9 %copy-start.1 = (s32[1,8]{1,0:T(1,128)S(1)}, s32[1,8]{1,0:T(1,128)}, u32[]{:S(2)}) copy-start(s32[1,8]{1,0:T(1,128)} %param.9) | copy-start | bytes 100
  68.4 69.4 %reduce-scatter.12.cloned.1.call-start = ((), (), s32[]{:S(2)}) async-start(), calls=%async_computation.6 | async-start | bytes 2949120 | tf_op jit(solution)/shard_map/reduce_scatter | solution.py:109
  89.7 73.5 %reduce-scatter.14.cloned.1.call-start = ((), (), s32[]{:S(2)}) async-start(), calls=%async_computation.7 | async-start | bytes 409600 | tf_op jit(solution)/shard_map/reduce_scatter | solution.py:109
  137.8 43.3 %reduce-scatter.16.cloned.1.call-start = ((), (), s32[]{:S(2)}) async-start(), calls=%async_computation.8 | async-start | bytes 122880 | tf_op jit(solution)/shard_map/reduce_scatter | solution.py:109
  163.3 202.5 %reduce-scatter.18.cloned.1.call-start = ((), (), s32[]{:S(2)}) async-start(), calls=%async_computation.9 | async-start | bytes 61440
Sparse Core Ops, SparseCore 0:
  68.5 21.1 reduce-scatter.9
  92.3 45.4 reduce-scatter.11
  140.3 22.8 reduce-scatter.13
  165.5 15.5 reduce-scatter.15
  183.4 14.7 reduce-scatter.17

commit v3 on v2

--- a/solution.py
+++ b/solution.py
@@ -13,7 +13,30 @@
 SEG = ("xl", "core")
 UTT = ("y", "xh", "z")
 FINE = SEG + UTT
-STAGES = ("core", "z", "y", "xh", "xl")
+GROUPS = (("core",), ("z",), ("y", "xh", "xl"))
+
+
+def linear(index, names, sizes):
+    value = 0
+    for name in names:
+        value = value * sizes[name] + index[name]
+    return value
+
+
+def owner_pairs(sizes):
+    import itertools
+
+    pairs = []
+    for digits in itertools.product(*(range(sizes[n]) for n in FINE)):
+        index = dict(zip(FINE, digits))
+        block = 0
+        for group in GROUPS:
+            size = 1
+            for name in group:
+                size *= sizes[name]
+            block = block * size + linear(index, group, sizes)
+        pairs.append((linear(index, FINE, sizes), block))
+    return pairs
 
 
 def fine_sizes(seg_size, utt_size):
@@ -90,7 +113,6 @@
         jnp.bfloat16
     )
     paired = jnp.concatenate([masked, onehot], 1)
-    valid_total = lax.psum(lengths.astype(jnp.float32), UTT)[0]
     partial = lax.dot_general(
         masked, paired, (((0,), (0,)), ((), ())), preferred_element_type=jnp.float32
     )
@@ -100,13 +122,25 @@
         owners *= sizes[name]
     row_count = partial.shape[0] // owners
     width = partial.shape[1]
-    blocks = partial.reshape(tuple(sizes[n] for n in FINE) + (row_count, width))
-    order = tuple(FINE.index(n) for n in STAGES) + (len(FINE), len(FINE) + 1)
-    slab = blocks.transpose(order).reshape(
-        tuple(sizes[n] for n in STAGES) + (8, row_count * width // 8)
-    )
-    for stage, name in enumerate(STAGES):
-        slab = lax.psum_scatter(slab, name, scatter_dimension=stage, tiled=True)
+    group_sizes = []
+    for group in GROUPS:
+        size = 1
+        for name in group:
+            size *= sizes[name]
+        group_sizes.append(size)
+    chunk = (8, row_count * width // 8)
+    slab = partial.reshape(tuple(group_sizes) + chunk)
+    local_count = jnp.sum(valid.astype(jnp.float32))
+    count_block = jnp.broadcast_to(local_count, tuple(group_sizes[:-1]) + (1,) + chunk)
+    slab = jnp.concatenate([slab, count_block], len(GROUPS) - 1)
+    for stage, group in enumerate(GROUPS[:-1]):
+        slab = lax.psum_scatter(slab, group, scatter_dimension=stage, tiled=True)
+    last = GROUPS[-1]
+    slab = lax.psum(slab, last)
+    flat = slab.reshape((group_sizes[-1] + 1,) + chunk)
+    valid_total = flat[group_sizes[-1], 0, 0]
+    mine = lax.dynamic_index_in_dim(flat, lax.axis_index(last), 0, keepdims=True)
+    slab = lax.ppermute(mine, FINE, owner_pairs(sizes))
     owned_rows = slab.reshape(row_count, width)
     gram_rows = owned_rows[:, :skip_width] / valid_total
     cross_rows = owned_rows[:, skip_width:] * (CLASSES / valid_total)

time: 376 us -> 250 us (0.66)
  the two profiles are of different devices: /device:TPU:2 before, /device:TPU:28 now
where the time goes in v3:
time: 250 us; the launch traced here: 247 us
  waiting for transfers between devices  170 us (68%)
  matrix products  23.3 us (9%)
  local copies, waits for them, and re-layouts  17.8 us (7%)
  between operations  15.5 us (6%)
  other arithmetic  11.7 us (5%)
  starting transfers between devices  8.93 us (4%)
    psum x1, waiting for transfers between devices, per_device(): slab = lax.psum(slab, last)  95.5 us
    unnamed x4, waiting for transfers between devices  48.9 us
    reduce_scatter x1, waiting for transfers between devices, per_device(): slab = lax.psum_scatter(slab, group, scatter_dimension=stage, tiled=True)  23.2 us
    dot_general x10, matrix products, layer_math(): preact = jnp.dot(paired, conv_one, preferred_element_type=jnp.float32)  8.26 us
    ppermute x1, starting transfers between devices, per_device(): slab = lax.ppermute(mine, FINE, owner_pairs(sizes))  7.07 us
    convert_element_type x9, other arithmetic, layer_math(): (jnp.tanh(preact[:, :gate_width]) * jax.nn.sigmoid(preact[:, gate_width:]...  7.07 us
    reshape x1, local copies, waits for them, and re-layouts, per_device(): slab = partial.reshape(tuple(group_sizes) + chunk)  6.77 us
    concatenate x1, local copies, waits for them, and re-layouts, per_device(): slab = jnp.concatenate([slab, count_block], len(GROUPS) - 1)  5.94 us
  transfers between devices with their start and end apart: 5, of which 4 were waited for; matrix products, arithmetic and copies ran while one was open for 1% of the time, Pallas kernels for 0%

profile of v3, /device:TPU:28, one launch (start us, length us, event | category | flops | bytes accessed | tf_op | source)
XLA Modules:
  0.0 246.8 jit_solution(17150045885127726668)
XLA Ops:
  7.2 1.7 collective-permute-start
  11.2 1.0 multiply_convert_fusion
  12.1 1.7 fusion.71
  13.9 0.8 fusion.49
  15.6 0.9 copy-done.2
  17.3 0.8 fusion.50
  19.4 0.8 fusion.51
  20.9 0.8 fusion.94
  21.6 0.8 fusion.52
  24.0 0.8 fusion.53
  25.6 1.0 fusion.102
  26.6 0.8 fusion.54
  29.0 0.8 fusion.59
  35.8 5.9 %broadcast_select_fusion = bf16[1024,1024]{0,1:T(8,128)(2,1)S(1)} fusion(pred[1024]{0:T(1024)(128)(4,1)S(1)} %add_compare_fusion, bf16[1024,2560]{0,1:T(8,128)(2,1)S(1)} %fusion.118, bf16[2560,1024]{1,0:T(8,128)(2,1)S(1)} %bitcast.94), kind=kOutput, calls=%fused_computation.78 | convolution fusion | flops 5371854848 | bytes 12583936 | tf_op jit(solution)/shard_map/dot_general | solution.py:105
  41.7 4.7 %fusion = f32[1024,1280]{1,0:T(8,128)} fusion(bf16[1024,1024]{0,1:T(8,128)(2,1)S(1)} %broadcast_select_fusion, bf16[1024,256]{0,1:T(8,128)(2,1)S(1)} %fusion.93), kind=kOutput, calls=%fused_computation.1 | convolution fusion | flops 2689597440 | bytes 7864320 | tf_op jit(solution)/shard_map/dot_general | solution.py:116
  46.3 6.8 %reshape.31 = f32[2,8,16,8,640]{4,3,2,1,0:T(8,128)} reshape(f32[1024,1280]{1,0:T(8,128)} %fusion) | data formatting | bytes 10485760 | tf_op jit(solution)/shard_map/reshape | solution.py:132
  53.1 5.9 %concatenate.67 = f32[2,8,17,8,640]{4,3,2,1,0:T(8,128)} pad(f32[2,8,16,8,640]{4,3,2,1,0:T(8,128)} %reshape.31, f32[]{:T(128)} %convert_reduce_fusion), padding=0_0x0_0x0_1x0_0x0_0 | pad | bytes 10813444 | tf_op jit(solution)/shard_map/concatenate | solution.py:135
  59.1 23.2 %reduce-scatter.6.cloned.1.call-done = f32[1,8,17,8,640]{4,3,2,1,0:T(8,128)} async-done(((f32[2,8,17,8,640]{4,3,2,1,0:T(8,128)}), f32[1,8,17,8,640]{4,3,2,1,0:T(8,128)}) %reduce-scatter.6.cloned.1.call-update) | async-done | bytes 2785296 | tf_op jit(solution)/shard_map/reduce_scatter | solution.py:137
  82.4 48.8 %reduce-scatter.8.cloned.1.call-done = f32[1,1,17,8,640]{4,3,2,1,0:T(8,128)} async-done(((f32[1,8,17,8,640]{4,3,2,1,0:T(8,128)}), f32[1,1,17,8,640]{4,3,2,1,0:T(8,128)}) %reduce-scatter.8.cloned.1.call-update) | async-done | bytes 348176
  131.2 95.5 %all-reduce.7.cloned.1.call-done = f32[1,1,17,8,640]{4,3,2,1,0:T(8,128)} async-done(((f32[1,1,17,8,640]{4,3,2,1,0:T(8,128)}), f32[1,1,17,8,640]{4,3,2,1,0:T(8,128)}) %all-reduce.7.cloned.1.call-update) | async-done | bytes 348176 | tf_op jit(solution)/shard_map/psum | solution.py:139
  227.5 7.1 %collective-permute-start.1 = (f32[1,8,640]{2,1,0:T(8,128)S(1)}, f32[1,8,640]{2,1,0:T(8,128)S(1)}, u32[]{:S(2)}, u32[]{:S(2)}) collective-permute-start(f32[1,8,640]{2,1,0:T(8,128)S(1)} %dynamic-slice_bitcast_fusion), channel_id=1, source_target_pairs={{0,0},{1,16},{2,32},{3,48},{4,64},{5,80},{6,96},{7,112},{8,2},{9,1... | collective-permute-start | bytes 61448 | tf_op jit(solution)/shard_map/ppermute | solution.py:143
  234.5 1.2 slice.319
  236.4 2.0 collective-permute-done.1
  238.4 1.3 slice_divide_fusion
  (64 shorter events, 16.2 us)
Async XLA Ops:
  7.2 2.5 copy-start
  7.2 75.1 %reduce-scatter.6.cloned.1.call-start = ((), (), s32[]{:S(2)}) async-start(), calls=%async_computation.2 | async-start | bytes 8355840 | tf_op jit(solution)/shard_map/reduce_scatter | solution.py:137
  7.2 3.2 %collective-permute-start = (f32[1,1024]{1,0:T(1,128)}, f32[1,1024]{1,0:T(1,128)S(1)}, u32[]{:S(2)}, u32[]{:S(2)}) collective-permute-start(f32[1,1024]{1,0:T(1,128)} %param.7), channel_id=1, source_target_pairs={{0,64},{64,128},{128,192},{1,65},{65,129},{129,193},{2,66},{66,130... | collective-permute-start | bytes 12296 | tf_op jit(solution)/shard_map/ppermute | solution.py:53
  13.9 1.1 copy-start.3
  13.9 1.1 copy-start.4
  14.7 1.8 copy-start.2
  33.0 2.2 slice-start
  34.1 1.7 slice-start.1
  59.1 181.2 %copy-start.1 = (s32[1,8]{1,0:T(1,128)S(1)}, s32[1,8]{1,0:T(1,128)}, u32[]{:S(2)}) copy-start(s32[1,8]{1,0:T(1,128)} %param.9) | copy-start | bytes 100
  59.1 72.1 %reduce-scatter.8.cloned.1.call-start = ((), (), s32[]{:S(2)}) async-start(), calls=%async_computation.4 | async-start | bytes 3133440
  82.3 144.4 %all-reduce.7.cloned.1.call-start = ((), (), s32[]{:S(2)}) async-start(), calls=%async_computation.3 | async-start | bytes 696320 | tf_op jit(solution)/shard_map/psum | solution.py:139
  227.5 10.9 %collective-permute-start.1 = (f32[1,8,640]{2,1,0:T(8,128)S(1)}, f32[1,8,640]{2,1,0:T(8,128)S(1)}, u32[]{:S(2)}, u32[]{:S(2)}) collective-permute-start(f32[1,8,640]{2,1,0:T(8,128)S(1)} %dynamic-slice_bitcast_fusion), channel_id=1, source_target_pairs={{0,0},{1,16},{2,32},{3,48},{4,64},{5,80},{6,96},{7,112},{8,2},{9,1... | collective-permute-start | bytes 61448 | tf_op jit(solution)/shard_map/ppermute | solution.py:143
Sparse Core Ops, SparseCore 0:
  59.2 23.0 reduce-scatter.5
  84.9 46.2 reduce-scatter.7
  134.5 92.2 all-reduce.6

commit v4 on v3

--- a/solution.py
+++ b/solution.py
@@ -13,7 +13,7 @@
 SEG = ("xl", "core")
 UTT = ("y", "xh", "z")
 FINE = SEG + UTT
-GROUPS = (("core",), ("z",), ("y", "xh", "xl"))
+GROUPS = (("core",), ("z",), ("y",), ("xh",), ("xl",))
 
 
 def linear(index, names, sizes):
@@ -128,20 +128,23 @@
         for name in group:
             size *= sizes[name]
         group_sizes.append(size)
+    local_count = jnp.sum(valid.astype(jnp.float32))
+    rows = lax.broadcasted_iota(jnp.int32, partial.shape, 0)
+    cols = lax.broadcasted_iota(jnp.int32, partial.shape, 1)
+    slot = (rows % row_count == 1) & (cols == rows - 1)
+    partial = jnp.where(slot, local_count, partial)
     chunk = (8, row_count * width // 8)
     slab = partial.reshape(tuple(group_sizes) + chunk)
-    local_count = jnp.sum(valid.astype(jnp.float32))
-    count_block = jnp.broadcast_to(local_count, tuple(group_sizes[:-1]) + (1,) + chunk)
-    slab = jnp.concatenate([slab, count_block], len(GROUPS) - 1)
-    for stage, group in enumerate(GROUPS[:-1]):
+    for stage, group in enumerate(GROUPS):
         slab = lax.psum_scatter(slab, group, scatter_dimension=stage, tiled=True)
-    last = GROUPS[-1]
-    slab = lax.psum(slab, last)
-    flat = slab.reshape((group_sizes[-1] + 1,) + chunk)
-    valid_total = flat[group_sizes[-1], 0, 0]
-    mine = lax.dynamic_index_in_dim(flat, lax.axis_index(last), 0, keepdims=True)
-    slab = lax.ppermute(mine, FINE, owner_pairs(sizes))
+    slab = lax.ppermute(slab, FINE, owner_pairs(sizes))
     owned_rows = slab.reshape(row_count, width)
+    first_col = lax.axis_index(FINE) * row_count
+    valid_total = lax.dynamic_slice(owned_rows, (1, first_col), (1, 1))[0, 0]
+    mirror = lax.dynamic_slice(owned_rows, (0, first_col + 1), (1, 1))[0, 0]
+    own_rows = lax.broadcasted_iota(jnp.int32, owned_rows.shape, 0)
+    own_cols = lax.broadcasted_iota(jnp.int32, owned_rows.shape, 1)
+    owned_rows = jnp.where((own_rows == 1) & (own_cols == first_col), mirror, owned_rows)
     gram_rows = owned_rows[:, :skip_width] / valid_total
     cross_rows = owned_rows[:, skip_width:] * (CLASSES / valid_total)
     return (gram_rows, cross_rows)

time: 250 us -> 211 us (0.84)
  waiting for transfers between devices: 170 us -> 137 us
  local copies, waits for them, and re-layouts: 17.8 us -> 10.6 us
    psum x1 -> x0, waiting for transfers between devices: 95.5 us -> none  [per_device(): slab = lax.psum(slab, last)]
    reduce_scatter x1 -> x4, waiting for transfers between devices: 23.2 us -> 113 us  [per_device(): slab = lax.psum_scatter(slab, group, scatter_dimension=stage, tiled=True)]
    unnamed x4 -> x6, waiting for transfers between devices: 48.9 us -> 19 us
    concatenate x1 -> x0, local copies, waits for them, and re-layouts: 5.94 us -> none  [per_device(): slab = jnp.concatenate([slab, count_block], len(GROUPS) - 1)]
    ppermute x1, waiting for transfers between devices: 1.95 us -> 5 us  [per_device(): slab = lax.ppermute(slab, FINE, owner_pairs(sizes))]
  transfers between devices with their start and end apart: 5 -> 7, of which waited for: 4 -> 6; matrix products, arithmetic and copies ran while one was open for 1% -> 0% of each run, Pallas kernels for 0% -> 0%
where the time goes in v4:
time: 211 us; the launch traced here: 208 us
  waiting for transfers between devices  137 us (65%)
  matrix products  24.6 us (12%)
  between operations  15.6 us (7%)
  other arithmetic  12.5 us (6%)
  local copies, waits for them, and re-layouts  10.6 us (5%)
  starting transfers between devices  7.89 us (4%)
    reduce_scatter x4, waiting for transfers between devices, per_device(): slab = lax.psum_scatter(slab, group, scatter_dimension=stage, tiled=True)  113 us
    unnamed x6, waiting for transfers between devices  19 us
    dot_general x10, matrix products, layer_math(): preact = jnp.dot(paired, conv_one, preferred_element_type=jnp.float32)  8.26 us
    convert_element_type x9, other arithmetic, layer_math(): (jnp.tanh(preact[:, :gate_width]) * jax.nn.sigmoid(preact[:, gate_width:]...  7.07 us
    reshape x1, local copies, waits for them, and re-layouts, per_device(): slab = partial.reshape(tuple(group_sizes) + chunk)  6.76 us
    dot_general x1, matrix products, per_device(): lax.dot_general(masked, paired, (((0,), (0,)), ((), ())), preferred_eleme...  6.01 us
    ppermute x1, starting transfers between devices, per_device(): slab = lax.ppermute(slab, FINE, owner_pairs(sizes))  5.95 us
    dot_general x1, matrix products, per_device(): skip_sum = jnp.dot(stacked, skip_weight, preferred_element_type=jnp.float32)  5.88 us
  transfers between devices with their start and end apart: 7, of which 6 were waited for; matrix products, arithmetic and copies ran while one was open for 0% of the time, Pallas kernels for 0%

profile of v4, /device:TPU:28, one launch (start us, length us, event | category | flops | bytes accessed | tf_op | source)
XLA Modules:
  0.0 207.8 jit_solution(3260899174963551212)
XLA Ops:
  7.2 1.7 collective-permute-start
  11.2 1.0 multiply_convert_fusion
  12.2 1.7 fusion.72
  13.9 0.8 fusion.50
  15.6 0.9 copy-done.2
  17.3 0.8 fusion.51
  19.4 0.8 fusion.52
  20.9 0.8 fusion.95
  21.7 0.8 fusion.53
  24.0 0.8 fusion.54
  25.7 1.0 fusion.103
  26.6 0.8 fusion.55
  29.0 0.8 fusion.60
  35.8 5.9 %broadcast_select_fusion = bf16[1024,1024]{0,1:T(8,128)(2,1)S(1)} fusion(pred[1024]{0:T(1024)(128)(4,1)S(1)} %add_compare_fusion, bf16[1024,2560]{0,1:T(8,128)(2,1)S(1)} %fusion.119, bf16[2560,1024]{1,0:T(8,128)(2,1)S(1)} %bitcast.93), kind=kOutput, calls=%fused_computation.81 | convolution fusion | flops 5371854848 | bytes 12583936 | tf_op jit(solution)/shard_map/dot_general | solution.py:105
  41.7 6.0 %fusion.1 = f32[1024,1280]{1,0:T(8,128)} fusion(bf16[1024,1024]{0,1:T(8,128)(2,1)S(1)} %broadcast_select_fusion, bf16[1024,256]{0,1:T(8,128)(2,1)S(1)} %fusion.94, f32[]{:T(128)} %convert_reduce_fusion, s32[1024]{0:T(1024)S(1)} %get-tuple-element.18, s32[1024]{0:T(1024)S(1)} %get-tuple-element.19, s32[1024]{0:T(1024)S(1)} %fusion.165, ...), kind=kOutput, calls=%fused_computation.3 | convolution fusion | flops 2696151040 | bytes 7877636 | tf_op jit(solution)/shard_map/dot_general | solution.py:116
  47.7 6.8 %reshape.27 = f32[2,8,4,2,2,8,640]{6,5,4,3,2,1,0:T(8,128)} reshape(f32[1024,1280]{1,0:T(8,128)} %fusion.1) | data formatting | bytes 10485760 | tf_op jit(solution)/shard_map/reshape | solution.py:137
  54.5 22.8 %reduce-scatter.10.cloned.1.call-done = f32[1,8,4,2,2,8,640]{6,5,4,3,2,1,0:T(8,128)} async-done(((f32[2,8,4,2,2,8,640]{6,5,4,3,2,1,0:T(8,128)}), f32[1,8,4,2,2,8,640]{6,5,4,3,2,1,0:T(8,128)}) %reduce-scatter.10.cloned.1.call-update) | async-done | bytes 2621456 | tf_op jit(solution)/shard_map/reduce_scatter | solution.py:139
  77.4 48.3 %reduce-scatter.12.cloned.1.call-done = f32[1,1,4,2,2,8,640]{6,5,4,3,2,1,0:T(8,128)} async-done(((f32[1,8,4,2,2,8,640]{6,5,4,3,2,1,0:T(8,128)}), f32[1,1,4,2,2,8,640]{6,5,4,3,2,1,0:T(8,128)}) %reduce-scatter.12.cloned.1.call-update) | async-done | bytes 327696 | tf_op jit(solution)/shard_map/reduce_scatter | solution.py:139
  125.8 23.3 %reduce-scatter.14.cloned.1.call-done = f32[1,1,1,2,2,8,640]{6,5,4,3,2,1,0:T(8,128)} async-done(((f32[1,1,4,2,2,8,640]{6,5,4,3,2,1,0:T(8,128)}), f32[1,1,1,2,2,8,640]{6,5,4,3,2,1,0:T(8,128)}) %reduce-scatter.14.cloned.1.call-update) | async-done | bytes 81936 | tf_op jit(solution)/shard_map/reduce_scatter | solution.py:139
  149.2 18.2 %reduce-scatter.16.cloned.1.call-done = f32[1,1,1,1,2,8,640]{6,5,4,3,2,1,0:T(8,128)} async-done(((f32[1,1,1,2,2,8,640]{6,5,4,3,2,1,0:T(8,128)}), f32[1,1,1,1,2,8,640]{6,5,4,3,2,1,0:T(8,128)}) %reduce-scatter.16.cloned.1.call-update) | async-done | bytes 40976 | tf_op jit(solution)/shard_map/reduce_scatter | solution.py:139
  167.4 18.9 %reduce-scatter.18.cloned.1.call-done = f32[1,1,1,1,1,8,640]{6,5,4,3,2,1,0:T(8,128)} async-done(((f32[1,1,1,1,2,8,640]{6,5,4,3,2,1,0:T(8,128)}), f32[1,1,1,1,1,8,640]{6,5,4,3,2,1,0:T(8,128)}) %reduce-scatter.18.cloned.1.call-update) | async-done | bytes 20496
  186.4 6.0 %collective-permute-start.1 = (f32[1,1,1,1,1,8,640]{6,5,4,3,2,1,0:T(8,128)}, f32[1,1,1,1,1,8,640]{6,5,4,3,2,1,0:T(8,128)S(1)}, u32[]{:S(2)}, u32[]{:S(2)}) collective-permute-start(f32[1,1,1,1,1,8,640]{6,5,4,3,2,1,0:T(8,128)} %reduce-scatter.18.cloned.1.call-done), channel_id=1, source_target_pairs={{0,0},{1,16},{2,32},{3,48},{4,64},{5,80},{6,96},{7,112},{8,2},{9,1... | collective-permute-start | bytes 61448 | tf_op jit(solution)/shard_map/ppermute | solution.py:140
  192.4 5.0 %collective-permute-done.1 = f32[1,1,1,1,1,8,640]{6,5,4,3,2,1,0:T(8,128)S(1)} collective-permute-done((f32[1,1,1,1,1,8,640]{6,5,4,3,2,1,0:T(8,128)}, f32[1,1,1,1,1,8,640]{6,5,4,3,2,1,0:T(8,128)S(1)}, u32[]{:S(2)}, u32[]{:S(2)}) %collective-permute-start.1) | collective-permute-done | bytes 20512 | tf_op jit(solution)/shard_map/ppermute | solution.py:140
  198.7 1.3 slice_divide_fusion
  (74 shorter events, 17.0 us)
Async XLA Ops:
  7.2 2.5 %copy-start = (s32[1,8]{1,0:T(1,128)S(1)}, s32[1,8]{1,0:T(1,128)}, u32[]{:S(2)}) copy-start(s32[1,8]{1,0:T(1,128)} %param.9) | copy-start | bytes 100
  7.2 70.2 %reduce-scatter.10.cloned.1.call-start = ((), (), s32[]{:S(2)}) async-start(), calls=%async_computation.5 | async-start | bytes 7864320 | tf_op jit(solution)/shard_map/reduce_scatter | solution.py:139
  7.2 3.3 %collective-permute-start = (f32[1,1024]{1,0:T(1,128)}, f32[1,1024]{1,0:T(1,128)S(1)}, u32[]{:S(2)}, u32[]{:S(2)}) collective-permute-start(f32[1,1024]{1,0:T(1,128)} %param.7), channel_id=1, source_target_pairs={{0,64},{64,128},{128,192},{1,65},{65,129},{129,193},{2,66},{66,130... | collective-permute-start | bytes 12296 | tf_op jit(solution)/shard_map/ppermute | solution.py:53
  13.9 1.1 copy-start.3
  13.9 1.1 copy-start.4
  14.7 1.8 copy-start.2
  33.1 2.2 %slice-start = ((s8[5242880]{0:T(1024)(128)(4,1)}), s8[4194304]{0:T(1024)(128)(4,1)S(1)}, s32[]{:S(2)}) async-start(s8[5242880]{0:T(1024)(128)(4,1)} %bitcast.92), calls=%async_computation.10 | async-start | bytes 8388608
  34.1 1.7 slice-start.1
  54.5 146.8 %copy-start.1 = (s32[1,8]{1,0:T(1,128)S(1)}, s32[1,8]{1,0:T(1,128)}, u32[]{:S(2)}) copy-start(s32[1,8]{1,0:T(1,128)} %param.9) | copy-start | bytes 100
  54.5 71.2 %reduce-scatter.12.cloned.1.call-start = ((), (), s32[]{:S(2)}) async-start(), calls=%async_computation.6 | async-start | bytes 2949120 | tf_op jit(solution)/shard_map/reduce_scatter | solution.py:139
  77.4 71.7 %reduce-scatter.14.cloned.1.call-start = ((), (), s32[]{:S(2)}) async-start(), calls=%async_computation.7 | async-start | bytes 409600 | tf_op jit(solution)/shard_map/reduce_scatter | solution.py:139
  125.7 41.7 %reduce-scatter.16.cloned.1.call-start = ((), (), s32[]{:S(2)}) async-start(), calls=%async_computation.8 | async-start | bytes 122880 | tf_op jit(solution)/shard_map/reduce_scatter | solution.py:139
  149.1 37.3 %reduce-scatter.18.cloned.1.call-start = ((), (), s32[]{:S(2)}) async-start(), calls=%async_computation.9 | async-start | bytes 61440
  186.4 11.0 %collective-permute-start.1 = (f32[1,1,1,1,1,8,640]{6,5,4,3,2,1,0:T(8,128)}, f32[1,1,1,1,1,8,640]{6,5,4,3,2,1,0:T(8,128)S(1)}, u32[]{:S(2)}, u32[]{:S(2)}) collective-permute-start(f32[1,1,1,1,1,8,640]{6,5,4,3,2,1,0:T(8,128)} %reduce-scatter.18.cloned.1.call-done), channel_id=1, source_target_pairs={{0,0},{1,16},{2,32},{3,48},{4,64},{5,80},{6,96},{7,112},{8,2},{9,1... | collective-permute-start | bytes 61448 | tf_op jit(solution)/shard_map/ppermute | solution.py:140
Sparse Core Ops, SparseCore 0:
  54.6 22.7 reduce-scatter.9
  79.9 45.7 reduce-scatter.11
  128.2 20.7 reduce-scatter.13
  151.4 15.9 reduce-scatter.15
  169.7 16.6 reduce-scatter.17

commit v5 on v4

--- a/solution.py
+++ b/solution.py
@@ -14,6 +14,7 @@
 UTT = ("y", "xh", "z")
 FINE = SEG + UTT
 GROUPS = (("core",), ("z",), ("y",), ("xh",), ("xl",))
+EXCHANGED = ("core", "y", "xh", "xl")
 
 
 def linear(index, names, sizes):
@@ -51,6 +52,23 @@
         length *= lax.axis_size(name)
     pairs = [(i, i + by) for i in range(length) if 0 <= i + by < length]
     return lax.ppermute(value, axis, pairs)
+
+
+def exchange_scatter(slab, axis, dim):
+    size = slab.shape[dim]
+    index = lax.axis_index(axis)
+    bit = size // 2
+    while bit >= 1:
+        shape = slab.shape
+        split = shape[:dim] + (2, shape[dim] // 2) + shape[dim + 1 :]
+        halves = slab.reshape(split)
+        side = (index // bit) % 2
+        mine = lax.dynamic_index_in_dim(halves, side, dim, keepdims=False)
+        other = lax.dynamic_index_in_dim(halves, 1 - side, dim, keepdims=False)
+        pairs = [(i, i ^ bit) for i in range(size)]
+        slab = mine + lax.ppermute(other, axis, pairs)
+        bit //= 2
+    return slab
 
 
 def round_up(value, step):
@@ -136,7 +154,10 @@
     chunk = (8, row_count * width // 8)
     slab = partial.reshape(tuple(group_sizes) + chunk)
     for stage, group in enumerate(GROUPS):
-        slab = lax.psum_scatter(slab, group, scatter_dimension=stage, tiled=True)
+        if group[0] in EXCHANGED and len(group) == 1:
+            slab = exchange_scatter(slab, group[0], stage)
+        else:
+            slab = lax.psum_scatter(slab, group, scatter_dimension=stage, tiled=True)
     slab = lax.ppermute(slab, FINE, owner_pairs(sizes))
     owned_rows = slab.reshape(row_count, width)
     first_col = lax.axis_index(FINE) * row_count

time: 211 us -> 161 us (0.76); the launches traced: 208 us -> 160 us
  waiting for transfers between devices: 137 us -> 77.1 us
  other arithmetic: 12.5 us -> 17.2 us
  local copies, waits for them, and re-layouts: 10.6 us -> 15 us
  starting transfers between devices: 7.89 us -> 10.7 us
    reduce_scatter x4 -> x1, waiting for transfers between devices: 113 us -> 47.3 us  [per_device(): slab = lax.psum_scatter(slab, group, scatter_dimension=stage, tiled=True)]
    ppermute x0 -> x5, waiting for transfers between devices: none -> 22.2 us  [exchange_scatter(): slab = mine + lax.ppermute(other, axis, pairs)]
    unnamed x6 -> x1, waiting for transfers between devices: 19 us -> 0.02 us
    another operation x0 -> x1, local copies, waits for them, and re-layouts: none -> 6.77 us  [exchange_scatter(): halves = slab.reshape(split)]
    reshape x1 -> x0, local copies, waits for them, and re-layouts: 6.76 us -> none  [per_device(): slab = partial.reshape(tuple(group_sizes) + chunk)]
    ppermute x0 -> x5, starting transfers between devices: none -> 5.77 us  [exchange_scatter(): slab = mine + lax.ppermute(other, axis, pairs)]
    add x0 -> x5, other arithmetic: none -> 4.7 us  [exchange_scatter(): slab = mine + lax.ppermute(other, axis, pairs)]
    squeeze x0 -> x5, local copies, waits for them, and re-layouts: none -> 4.39 us  [exchange_scatter(): other = lax.dynamic_index_in_dim(halves, 1 - side, dim, keepdims=False)]
  transfers between devices with their start and end apart: 7 -> 8, of which waited for: 6 -> 7; matrix products, arithmetic and copies ran while one was open for 0% -> 1% of each run, Pallas kernels for 0% -> 0%
where the time goes in v5:
time: 161 us; the launch traced here: 160 us
  waiting for transfers between devices  77.1 us (48%)
  matrix products  24.6 us (15%)
  other arithmetic  17.2 us (11%)
  between operations  15.9 us (10%)
  local copies, waits for them, and re-layouts  15 us (9%)
  starting transfers between devices  10.7 us (7%)
    reduce_scatter x1, waiting for transfers between devices, per_device(): slab = lax.psum_scatter(slab, group, scatter_dimension=stage, tiled=True)  47.3 us
    ppermute x5, waiting for transfers between devices, exchange_scatter(): slab = mine + lax.ppermute(other, axis, pairs)  22.2 us
    dot_general x10, matrix products, layer_math(): preact = jnp.dot(paired, conv_one, preferred_element_type=jnp.float32)  8.25 us
    ppermute x1, waiting for transfers between devices, per_device(): slab = lax.ppermute(slab, FINE, owner_pairs(sizes))  7.6 us
    convert_element_type x9, other arithmetic, layer_math(): (jnp.tanh(preact[:, :gate_width]) * jax.nn.sigmoid(preact[:, gate_width:]...  7.06 us
    another operation x1, local copies, waits for them, and re-layouts, exchange_scatter(): halves = slab.reshape(split)  6.77 us
    dot_general x1, matrix products, per_device(): lax.dot_general(masked, paired, (((0,), (0,)), ((), ())), preferred_eleme...  6.03 us
    dot_general x1, matrix products, per_device(): skip_sum = jnp.dot(stacked, skip_weight, preferred_element_type=jnp.float32)  5.88 us
  transfers between devices with their start and end apart: 8, of which 7 were waited for; matrix products, arithmetic and copies ran while one was open for 1% of the time, Pallas kernels for 0%

profile of v5, /device:TPU:28, one launch (start us, length us, event | category | flops | bytes accessed | tf_op | source)
XLA Modules:
  0.0 160.4 jit_solution(159014840094162092)
XLA Ops:
  7.2 1.7 %collective-permute-start = (f32[1,1024]{1,0:T(1,128)}, f32[1,1024]{1,0:T(1,128)S(1)}, u32[]{:S(2)}, u32[]{:S(2)}) collective-permute-start(f32[1,1024]{1,0:T(1,128)} %param.7), channel_id=1, source_target_pairs={{0,64},{64,128},{128,192},{1,65},{65,129},{129,193},{2,66},{66,130... | collective-permute-start | bytes 12296 | tf_op jit(solution)/shard_map/ppermute | solution.py:54
  11.2 1.0 multiply_convert_fusion
  12.2 1.7 %fusion.72 = f32[2048,512]{0,1:T(8,128)S(1)} fusion(bf16[2047,128]{1,0:T(8,128)(2,1)S(1)} %bitcast.94, bf16[2048,128]{1,0:T(8,128)(2,1)S(1)} %multiply_convert_fusion, bf16[10,256,512]{2,1,0:T(8,128)(2,1)} %param.11), kind=kOutput, calls=%fused_computation.106 | convolution fusion | flops 540016640 | bytes 5504768 | tf_op jit(solution)/shard_map/dot_general | solution.py:81
  25.7 1.0 fusion.103
  35.8 5.9 %broadcast_select_fusion = bf16[1024,1024]{0,1:T(8,128)(2,1)S(1)} fusion(pred[1024]{0:T(1024)(128)(4,1)S(1)} %add_compare_fusion, bf16[1024,2560]{0,1:T(8,128)(2,1)S(1)} %fusion.119, bf16[2560,1024]{1,0:T(8,128)(2,1)S(1)} %bitcast.101), kind=kOutput, calls=%fused_computation.83 | convolution fusion | flops 5371854848 | bytes 12583936 | tf_op jit(solution)/shard_map/dot_general | solution.py:123
  41.7 6.0 %fusion.1 = f32[1024,1280]{1,0:T(8,128)} fusion(bf16[1024,1024]{0,1:T(8,128)(2,1)S(1)} %broadcast_select_fusion, bf16[1024,256]{0,1:T(8,128)(2,1)S(1)} %fusion.94, f32[]{:T(128)} %convert_reduce_fusion, s32[1024]{0:T(1024)S(1)} %get-tuple-element.18, s32[1024]{0:T(1024)S(1)} %get-tuple-element.19, s32[1024]{0:T(1024)S(1)} %fusion.165, ...), kind=kOutput, calls=%fused_computation.3 | convolution fusion | flops 2696151040 | bytes 7877636 | tf_op jit(solution)/shard_map/dot_general | solution.py:134
  47.7 6.8 %reshape_reshape.3 = f32[2,1,8,4,2,2,8,640]{7,6,5,4,3,2,0,1:T(8,128)} reshape(f32[1024,1280]{1,0:T(8,128)} %fusion.1) | data formatting | bytes 10485760 | tf_op jit(solution)/shard_map/reshape;reshape | solution.py:64
  54.5 3.4 %dynamic-slice_bitcast_fusion = f32[1,8,4,2,2,8,640]{6,5,4,3,2,1,0:T(8,128)} fusion(f32[2,1,8,4,2,2,8,640]{7,6,5,4,3,2,0,1:T(8,128)} %reshape_reshape.3, s32[]{:T(128)S(6)} %select_n.95), kind=kLoop, calls=%fused_computation.9 | loop fusion | bytes 5242884 | tf_op jit(solution)/shard_map/jit(dynamic_index_in_dim)/squeeze | solution.py:67
  57.9 1.5 collective-permute-start.1
  59.4 4.7 %collective-permute-done.1 = f32[1,8,4,2,2,8,640]{6,5,4,3,2,1,0:T(8,128)S(1)} collective-permute-done((f32[1,8,4,2,2,8,640]{6,5,4,3,2,1,0:T(8,128)}, f32[1,8,4,2,2,8,640]{6,5,4,3,2,1,0:T(8,128)S(1)}, u32[]{:S(2)}, u32[]{:S(2)}) %collective-permute-start.1) | collective-permute-done | bytes 2621472 | tf_op jit(solution)/shard_map/ppermute | solution.py:69
  64.1 3.7 %bitcast_add_fusion = f32[1,8,4,2,2,8,640]{6,5,4,3,2,1,0:T(8,128)} fusion(f32[1,8,4,2,2,8,640]{6,5,4,3,2,1,0:T(8,128)S(1)} %collective-permute-done.1, f32[2,1,8,4,2,2,8,640]{7,6,5,4,3,2,0,1:T(8,128)} %reshape_reshape.3, s32[]{:T(128)S(6)} %select_n.94), kind=kLoop, calls=%fused_computation.8 | loop fusion | flops 655360 | bytes 7864324 | tf_op jit(solution)/shard_map/add | solution.py:69
  67.9 47.3 %reduce-scatter.2.cloned.1.call-done = f32[1,1,4,2,2,8,640]{6,5,4,3,2,1,0:T(8,128)} async-done(((f32[1,8,4,2,2,8,640]{6,5,4,3,2,1,0:T(8,128)}), f32[1,1,4,2,2,8,640]{6,5,4,3,2,1,0:T(8,128)}) %reduce-scatter.2.cloned.1.call-update) | async-done | bytes 327696 | tf_op jit(solution)/shard_map/reduce_scatter | solution.py:160
  115.2 0.9 dynamic-slice_bitcast_fusion.1
  116.1 1.5 collective-permute-start.2
  117.6 6.3 %collective-permute-done.2 = f32[1,1,2,2,2,8,640]{6,5,4,3,2,1,0:T(8,128)S(1)} collective-permute-done((f32[1,1,2,2,2,8,640]{6,5,4,3,2,1,0:T(8,128)S(1)}, f32[1,1,2,2,2,8,640]{6,5,4,3,2,1,0:T(8,128)S(1)}, u32[]{:S(2)}, u32[]{:S(2)}) %collective-permute-start.2) | collective-permute-done | bytes 163872 | tf_op jit(solution)/shard_map/ppermute | solution.py:69
  123.9 0.9 bitcast_add_fusion.1
  124.9 0.9 collective-permute-start.3
  125.8 3.6 %collective-permute-done.3 = f32[1,1,1,2,2,8,640]{6,5,4,3,2,1,0:T(8,128)S(1)} collective-permute-done((f32[1,1,1,2,2,8,640]{6,5,4,3,2,1,0:T(8,128)S(1)}, f32[1,1,1,2,2,8,640]{6,5,4,3,2,1,0:T(8,128)S(1)}, u32[]{:S(2)}, u32[]{:S(2)}) %collective-permute-start.3) | collective-permute-done | bytes 81952 | tf_op jit(solution)/shard_map/ppermute | solution.py:69
  130.1 5.0 %collective-permute-done.4 = f32[1,1,1,1,2,8,640]{6,5,4,3,2,1,0:T(8,128)S(1)} collective-permute-done((f32[1,1,1,1,2,8,640]{6,5,4,3,2,1,0:T(8,128)S(1)}, f32[1,1,1,1,2,8,640]{6,5,4,3,2,1,0:T(8,128)S(1)}, u32[]{:S(2)}, u32[]{:S(2)}) %collective-permute-start.4) | collective-permute-done | bytes 40992 | tf_op jit(solution)/shard_map/ppermute | solution.py:69
  135.0 1.2 collective-permute-start.5
  136.3 2.6 %collective-permute-done.5 = f32[1,1,1,1,1,8,640]{6,5,4,3,2,1,0:T(8,128)S(1)} collective-permute-done((f32[1,1,1,1,1,8,640]{6,5,4,3,2,1,0:T(8,128)S(1)}, f32[1,1,1,1,1,8,640]{6,5,4,3,2,1,0:T(8,128)S(1)}, u32[]{:S(2)}, u32[]{:S(2)}) %collective-permute-start.5) | collective-permute-done | bytes 20512 | tf_op jit(solution)/shard_map/ppermute | solution.py:69
  138.9 3.1 %collective-permute-start.6 = (f32[1,1,1,1,1,8,640]{6,5,4,3,2,1,0:T(8,128)S(1)}, f32[1,1,1,1,1,8,640]{6,5,4,3,2,1,0:T(8,128)S(1)}, u32[]{:S(2)}, u32[]{:S(2)}) collective-permute-start(f32[1,1,1,1,1,8,640]{6,5,4,3,2,1,0:T(8,128)S(1)} %dynamic-slice_add_fusion.2), channel_id=1, source_target_pairs={{0,0},{1,16},{2,32},{3,48},{4,64},{5,80},{6,96},{7,112},{8,2},{9,1... | collective-permute-start | bytes 61448 | tf_op jit(solution)/shard_map/ppermute | solution.py:161
  142.1 7.6 %collective-permute-done.6 = f32[1,1,1,1,1,8,640]{6,5,4,3,2,1,0:T(8,128)S(1)} collective-permute-done((f32[1,1,1,1,1,8,640]{6,5,4,3,2,1,0:T(8,128)S(1)}, f32[1,1,1,1,1,8,640]{6,5,4,3,2,1,0:T(8,128)S(1)}, u32[]{:S(2)}, u32[]{:S(2)}) %collective-permute-start.6) | collective-permute-done | bytes 20512 | tf_op jit(solution)/shard_map/ppermute | solution.py:161
  151.0 1.3 slice_divide_fusion
  (82 shorter events, 24.8 us)
Async XLA Ops:
  7.2 2.5 %copy-start = (s32[1,8]{1,0:T(1,128)S(1)}, s32[1,8]{1,0:T(1,128)}, u32[]{:S(2)}) copy-start(s32[1,8]{1,0:T(1,128)} %param.9) | copy-start | bytes 100
  7.2 108.0 %reduce-scatter.2.cloned.1.call-start = ((), (), s32[]{:S(2)}) async-start(), calls=%async_computation.1 | async-start | bytes 2949120 | tf_op jit(solution)/shard_map/reduce_scatter | solution.py:160
  7.2 3.3 %collective-permute-start = (f32[1,1024]{1,0:T(1,128)}, f32[1,1024]{1,0:T(1,128)S(1)}, u32[]{:S(2)}, u32[]{:S(2)}) collective-permute-start(f32[1,1024]{1,0:T(1,128)} %param.7), channel_id=1, source_target_pairs={{0,64},{64,128},{128,192},{1,65},{65,129},{129,193},{2,66},{66,130... | collective-permute-start | bytes 12296 | tf_op jit(solution)/shard_map/ppermute | solution.py:54
  13.9 1.1 copy-start.3
  13.9 1.1 copy-start.4
  14.8 1.8 %copy-start.2 = (bf16[10,256,512]{2,1,0:T(8,128)(2,1)S(1)}, bf16[10,256,512]{2,1,0:T(8,128)(2,1)}, u32[]{:S(2)}) copy-start(bf16[10,256,512]{2,1,0:T(8,128)(2,1)} %param.11) | copy-start | bytes 7864324
  33.1 2.2 %slice-start = ((s8[5242880]{0:T(1024)(128)(4,1)}), s8[4194304]{0:T(1024)(128)(4,1)S(1)}, s32[]{:S(2)}) async-start(s8[5242880]{0:T(1024)(128)(4,1)} %bitcast.100), calls=%async_computation.2 | async-start | bytes 8388608
  34.1 1.7 %slice-start.1 = ((s8[5242880]{0:T(1024)(128)(4,1)}), s8[1048576]{0:T(1024)(128)(4,1)S(1)}, s32[]{:S(2)}) async-start(s8[5242880]{0:T(1024)(128)(4,1)} %bitcast.100), calls=%async_computation.3 | async-start | bytes 2097152
  57.9 6.2 %collective-permute-start.1 = (f32[1,8,4,2,2,8,640]{6,5,4,3,2,1,0:T(8,128)}, f32[1,8,4,2,2,8,640]{6,5,4,3,2,1,0:T(8,128)S(1)}, u32[]{:S(2)}, u32[]{:S(2)}) collective-permute-start(f32[1,8,4,2,2,8,640]{6,5,4,3,2,1,0:T(8,128)} %dynamic-slice_bitcast_fusion), channel_id=1, source_target_pairs={{0,64},{64,0},{1,65},{65,1},{2,66},{66,2},{3,67},{67,3},{4,68},{68... | collective-permute-start | bytes 7864328 | tf_op jit(solution)/shard_map/ppermute | solution.py:69
  67.9 85.7 %copy-start.1 = (s32[1,8]{1,0:T(1,128)S(1)}, s32[1,8]{1,0:T(1,128)}, u32[]{:S(2)}) copy-start(s32[1,8]{1,0:T(1,128)} %param.9) | copy-start | bytes 100
  116.1 7.8 %collective-permute-start.2 = (f32[1,1,2,2,2,8,640]{6,5,4,3,2,1,0:T(8,128)S(1)}, f32[1,1,2,2,2,8,640]{6,5,4,3,2,1,0:T(8,128)S(1)}, u32[]{:S(2)}, u32[]{:S(2)}) collective-permute-start(f32[1,1,2,2,2,8,640]{6,5,4,3,2,1,0:T(8,128)S(1)} %dynamic-slice_bitcast_fusion.1), channel_id=1, source_target_pairs={{0,32},{16,48},{32,0},{48,16},{1,33},{17,49},{33,1},{49,17},{2,34}... | collective-permute-start | bytes 491528 | tf_op jit(solution)/shard_map/ppermute | solution.py:69
  124.9 4.5 %collective-permute-start.3 = (f32[1,1,1,2,2,8,640]{6,5,4,3,2,1,0:T(8,128)S(1)}, f32[1,1,1,2,2,8,640]{6,5,4,3,2,1,0:T(8,128)S(1)}, u32[]{:S(2)}, u32[]{:S(2)}) collective-permute-start(f32[1,1,1,2,2,8,640]{6,5,4,3,2,1,0:T(8,128)S(1)} %constant_dynamic-slice_fusion.3), channel_id=1, source_target_pairs={{0,16},{16,0},{32,48},{48,32},{1,17},{17,1},{33,49},{49,33},{2,18}... | collective-permute-start | bytes 245768 | tf_op jit(solution)/shard_map/ppermute | solution.py:69
  129.4 5.6 %collective-permute-start.4 = (f32[1,1,1,1,2,8,640]{6,5,4,3,2,1,0:T(8,128)S(1)}, f32[1,1,1,1,2,8,640]{6,5,4,3,2,1,0:T(8,128)S(1)}, u32[]{:S(2)}, u32[]{:S(2)}) collective-permute-start(f32[1,1,1,1,2,8,640]{6,5,4,3,2,1,0:T(8,128)S(1)} %constant_dynamic-slice_fusion.2), channel_id=1, source_target_pairs={{0,8},{8,0},{1,9},{9,1},{2,10},{10,2},{3,11},{11,3},{4,12},{12,4},... | collective-permute-start | bytes 122888 | tf_op jit(solution)/shard_map/ppermute | solution.py:69
  135.0 3.9 %collective-permute-start.5 = (f32[1,1,1,1,1,8,640]{6,5,4,3,2,1,0:T(8,128)S(1)}, f32[1,1,1,1,1,8,640]{6,5,4,3,2,1,0:T(8,128)S(1)}, u32[]{:S(2)}, u32[]{:S(2)}) collective-permute-start(f32[1,1,1,1,1,8,640]{6,5,4,3,2,1,0:T(8,128)S(1)} %constant_dynamic-slice_fusion.1), channel_id=1, source_target_pairs={{0,128},{128,0},{1,129},{129,1},{2,130},{130,2},{3,131},{131,3},{4... | collective-permute-start | bytes 61448 | tf_op jit(solution)/shard_map/ppermute | solution.py:69
  138.9 10.8 %collective-permute-start.6 = (f32[1,1,1,1,1,8,640]{6,5,4,3,2,1,0:T(8,128)S(1)}, f32[1,1,1,1,1,8,640]{6,5,4,3,2,1,0:T(8,128)S(1)}, u32[]{:S(2)}, u32[]{:S(2)}) collective-permute-start(f32[1,1,1,1,1,8,640]{6,5,4,3,2,1,0:T(8,128)S(1)} %dynamic-slice_add_fusion.2), channel_id=1, source_target_pairs={{0,0},{1,16},{2,32},{3,48},{4,64},{5,80},{6,96},{7,112},{8,2},{9,1... | collective-permute-start | bytes 61448 | tf_op jit(solution)/shard_map/ppermute | solution.py:161
Sparse Core Ops, SparseCore 0:
  68.0 47.1 reduce-scatter.1

commit v6 on v5

--- a/solution.py
+++ b/solution.py
@@ -151,9 +151,11 @@
     cols = lax.broadcasted_iota(jnp.int32, partial.shape, 1)
     slot = (rows % row_count == 1) & (cols == rows - 1)
     partial = jnp.where(slot, local_count, partial)
-    chunk = (8, row_count * width // 8)
-    slab = partial.reshape(tuple(group_sizes) + chunk)
+    pair = group_sizes[-1] * row_count
+    slab = partial.reshape(tuple(group_sizes[:-1]) + (pair, width))
     for stage, group in enumerate(GROUPS):
+        if stage == len(GROUPS) - 1:
+            slab = slab.reshape(tuple(slab.shape[:-2]) + (group_sizes[-1], row_count, width))
         if group[0] in EXCHANGED and len(group) == 1:
             slab = exchange_scatter(slab, group[0], stage)
         else:

time: 161 us -> 152 us (0.944)
  local copies, waits for them, and re-layouts: 15 us -> 7.85 us
  matrix products: 24.6 us -> 22.2 us
    another operation x1, local copies, waits for them, and re-layouts: 6.77 us -> 0.02 us  [exchange_scatter(): halves = slab.reshape(split)]
    dot_general x1, matrix products: 6.03 us -> 3.67 us  [per_device(): lax.dot_general(masked, paired, (((0,), (0,)), ((), ())), preferred_eleme...]
    squeeze x5, local copies, waits for them, and re-layouts: 4.39 us -> 2.76 us  [exchange_scatter(): other = lax.dynamic_index_in_dim(halves, 1 - side, dim, keepdims=False)]
    unnamed x23 -> x25, local copies, waits for them, and re-layouts: 2.68 us -> 3.99 us
where the time goes in v6:
time: 152 us; the launch traced here: 151 us
  waiting for transfers between devices  77.1 us (51%)
  matrix products  22.2 us (15%)
  other arithmetic  17.2 us (11%)
  between operations  15.9 us (10%)
  starting transfers between devices  10.7 us (7%)
  local copies, waits for them, and re-layouts  7.85 us (5%)
    reduce_scatter x1, waiting for transfers between devices, per_device(): slab = lax.psum_scatter(slab, group, scatter_dimension=stage, tiled=True)  47.3 us
    ppermute x5, waiting for transfers between devices, exchange_scatter(): slab = mine + lax.ppermute(other, axis, pairs)  22.2 us
    dot_general x10, matrix products, layer_math(): preact = jnp.dot(paired, conv_one, preferred_element_type=jnp.float32)  8.25 us
    ppermute x1, waiting for transfers between devices, per_device(): slab = lax.ppermute(slab, FINE, owner_pairs(sizes))  7.59 us
    convert_element_type x9, other arithmetic, layer_math(): (jnp.tanh(preact[:, :gate_width]) * jax.nn.sigmoid(preact[:, gate_width:]...  7.06 us
    dot_general x1, matrix products, per_device(): skip_sum = jnp.dot(stacked, skip_weight, preferred_element_type=jnp.float32)  5.88 us
    ppermute x5, starting transfers between devices, exchange_scatter(): slab = mine + lax.ppermute(other, axis, pairs)  5.77 us
    add x5, other arithmetic, exchange_scatter(): slab = mine + lax.ppermute(other, axis, pairs)  4.69 us
  transfers between devices with their start and end apart: 8, of which 7 were waited for; matrix products, arithmetic and copies ran while one was open for 1% of the time, Pallas kernels for 0%

profile of v6, /device:TPU:28, one launch (start us, length us, event | category | flops | bytes accessed | tf_op | source)
XLA Modules:
  0.0 151.0 jit_solution(5254909784156374765)
XLA Ops:
  7.2 1.7 %collective-permute-start = (f32[1,1024]{1,0:T(1,128)}, f32[1,1024]{1,0:T(1,128)S(1)}, u32[]{:S(2)}, u32[]{:S(2)}) collective-permute-start(f32[1,1024]{1,0:T(1,128)} %param.7), channel_id=1, source_target_pairs={{0,64},{64,128},{128,192},{1,65},{65,129},{129,193},{2,66},{66,130... | collective-permute-start | bytes 12296 | tf_op jit(solution)/shard_map/ppermute | solution.py:54
  11.2 1.0 multiply_convert_fusion
  12.2 1.7 %fusion.72 = f32[2048,512]{0,1:T(8,128)S(1)} fusion(bf16[2047,128]{1,0:T(8,128)(2,1)S(1)} %bitcast.103, bf16[2048,128]{1,0:T(8,128)(2,1)S(1)} %multiply_convert_fusion, bf16[10,256,512]{2,1,0:T(8,128)(2,1)} %param.11), kind=kOutput, calls=%fused_computation.106 | convolution fusion | flops 540016640 | bytes 5504768 | tf_op jit(solution)/shard_map/dot_general | solution.py:81
  25.7 1.0 fusion.103
  35.8 5.9 %broadcast_select_fusion = bf16[1024,1024]{0,1:T(8,128)(2,1)S(1)} fusion(pred[1024]{0:T(1024)(128)(4,1)S(1)} %add_compare_fusion, bf16[1024,2560]{0,1:T(8,128)(2,1)S(1)} %fusion.119, bf16[2560,1024]{1,0:T(8,128)(2,1)S(1)} %bitcast.110), kind=kOutput, calls=%fused_computation.83 | convolution fusion | flops 5371854848 | bytes 12583936 | tf_op jit(solution)/shard_map/dot_general | solution.py:123
  41.7 3.7 %fusion.1 = f32[1024,1280]{1,0:T(8,128)S(1)} fusion(bf16[1024,1024]{0,1:T(8,128)(2,1)S(1)} %broadcast_select_fusion, bf16[1024,256]{0,1:T(8,128)(2,1)S(1)} %fusion.94, f32[]{:T(128)} %convert_reduce_fusion, s32[1024]{0:T(1024)S(1)} %get-tuple-element.18, s32[1024]{0:T(1024)S(1)} %get-tuple-element.19, s32[1024]{0:T(1024)S(1)} %fusion.165, ...), kind=kOutput, calls=%fused_computation.3 | convolution fusion | flops 2696151040 | bytes 7877636 | tf_op jit(solution)/shard_map/dot_general | solution.py:134
  45.4 1.8 %dynamic-slice_bitcast_fusion = f32[1,8,4,2,8,1280]{5,4,3,2,1,0:T(8,128)} fusion(f32[2,1,8,4,2,8,1280]{6,5,4,3,2,0,1:T(8,128)S(1)} %bitcast.101, s32[]{:T(128)S(6)} %select_n.95), kind=kLoop, calls=%fused_computation.9 | loop fusion | bytes 5242884 | tf_op jit(solution)/shard_map/jit(dynamic_index_in_dim)/squeeze | solution.py:67
  47.2 1.3 copy-done.2
  48.5 1.5 collective-permute-start.1
  49.9 4.7 %collective-permute-done.1 = f32[1,8,4,2,8,1280]{5,4,3,2,1,0:T(8,128)S(1)} collective-permute-done((f32[1,8,4,2,8,1280]{5,4,3,2,1,0:T(8,128)}, f32[1,8,4,2,8,1280]{5,4,3,2,1,0:T(8,128)S(1)}, u32[]{:S(2)}, u32[]{:S(2)}) %collective-permute-start.1) | collective-permute-done | bytes 2621472 | tf_op jit(solution)/shard_map/ppermute | solution.py:69
  54.7 3.7 %bitcast_add_fusion = f32[1,8,4,2,8,1280]{5,4,3,2,1,0:T(8,128)} fusion(f32[1,8,4,2,8,1280]{5,4,3,2,1,0:T(8,128)S(1)} %collective-permute-done.1, f32[2,1,8,4,2,8,1280]{6,5,4,3,2,0,1:T(8,128)} %bitcast.102, s32[]{:T(128)S(6)} %select_n.94), kind=kLoop, calls=%fused_computation.8 | loop fusion | flops 655360 | bytes 7864324 | tf_op jit(solution)/shard_map/add | solution.py:69
  58.5 47.3 %reduce-scatter.2.cloned.1.call-done = f32[1,1,4,2,8,1280]{5,4,3,2,1,0:T(8,128)} async-done(((f32[1,8,4,2,8,1280]{5,4,3,2,1,0:T(8,128)}), f32[1,1,4,2,8,1280]{5,4,3,2,1,0:T(8,128)}) %reduce-scatter.2.cloned.1.call-update) | async-done | bytes 327696 | tf_op jit(solution)/shard_map/reduce_scatter | solution.py:162
  105.7 0.9 dynamic-slice_bitcast_fusion.1
  106.7 1.5 collective-permute-start.2
  108.2 6.3 %collective-permute-done.2 = f32[1,1,2,2,8,1280]{5,4,3,2,1,0:T(8,128)S(1)} collective-permute-done((f32[1,1,2,2,8,1280]{5,4,3,2,1,0:T(8,128)S(1)}, f32[1,1,2,2,8,1280]{5,4,3,2,1,0:T(8,128)S(1)}, u32[]{:S(2)}, u32[]{:S(2)}) %collective-permute-start.2) | collective-permute-done | bytes 163872 | tf_op jit(solution)/shard_map/ppermute | solution.py:69
  114.4 0.9 bitcast_add_fusion.1
  115.4 0.9 collective-permute-start.3
  116.3 3.6 %collective-permute-done.3 = f32[1,1,1,2,8,1280]{5,4,3,2,1,0:T(8,128)S(1)} collective-permute-done((f32[1,1,1,2,8,1280]{5,4,3,2,1,0:T(8,128)S(1)}, f32[1,1,1,2,8,1280]{5,4,3,2,1,0:T(8,128)S(1)}, u32[]{:S(2)}, u32[]{:S(2)}) %collective-permute-start.3) | collective-permute-done | bytes 81952 | tf_op jit(solution)/shard_map/ppermute | solution.py:69
  120.6 5.0 %collective-permute-done.4 = f32[1,1,1,1,8,1280]{5,4,3,2,1,0:T(8,128)S(1)} collective-permute-done((f32[1,1,1,1,8,1280]{5,4,3,2,1,0:T(8,128)S(1)}, f32[1,1,1,1,8,1280]{5,4,3,2,1,0:T(8,128)S(1)}, u32[]{:S(2)}, u32[]{:S(2)}) %collective-permute-start.4) | collective-permute-done | bytes 40992 | tf_op jit(solution)/shard_map/ppermute | solution.py:69
  125.6 1.2 collective-permute-start.5
  126.8 2.6 %collective-permute-done.5 = f32[1,1,1,1,1,4,1280]{6,5,4,3,2,1,0:T(4,128)S(1)} collective-permute-done((f32[1,1,1,1,1,4,1280]{6,5,4,3,2,1,0:T(4,128)S(1)}, f32[1,1,1,1,1,4,1280]{6,5,4,3,2,1,0:T(4,128)S(1)}, u32[]{:S(2)}, u32[]{:S(2)}) %collective-permute-start.5) | collective-permute-done | bytes 20512 | tf_op jit(solution)/shard_map/ppermute | solution.py:69
  129.5 3.2 %collective-permute-start.6 = (f32[1,1,1,1,1,4,1280]{6,5,4,3,2,1,0:T(4,128)S(1)}, f32[1,1,1,1,1,4,1280]{6,5,4,3,2,1,0:T(4,128)S(1)}, u32[]{:S(2)}, u32[]{:S(2)}) collective-permute-start(f32[1,1,1,1,1,4,1280]{6,5,4,3,2,1,0:T(4,128)S(1)} %bitcast_add_fusion.2), channel_id=1, source_target_pairs={{0,0},{1,16},{2,32},{3,48},{4,64},{5,80},{6,96},{7,112},{8,2},{9,1... | collective-permute-start | bytes 61448 | tf_op jit(solution)/shard_map/ppermute | solution.py:163
  132.7 7.6 %collective-permute-done.6 = f32[1,1,1,1,1,4,1280]{6,5,4,3,2,1,0:T(4,128)S(1)} collective-permute-done((f32[1,1,1,1,1,4,1280]{6,5,4,3,2,1,0:T(4,128)S(1)}, f32[1,1,1,1,1,4,1280]{6,5,4,3,2,1,0:T(4,128)S(1)}, u32[]{:S(2)}, u32[]{:S(2)}) %collective-permute-start.6) | collective-permute-done | bytes 20512 | tf_op jit(solution)/shard_map/ppermute | solution.py:163
  141.6 1.3 slice_divide_fusion
  (83 shorter events, 24.8 us)
Async XLA Ops:
  7.2 2.5 %copy-start = (s32[1,8]{1,0:T(1,128)S(1)}, s32[1,8]{1,0:T(1,128)}, u32[]{:S(2)}) copy-start(s32[1,8]{1,0:T(1,128)} %param.9) | copy-start | bytes 100
  7.2 98.6 %reduce-scatter.2.cloned.1.call-start = ((), (), s32[]{:S(2)}) async-start(), calls=%async_computation.1 | async-start | bytes 2949120 | tf_op jit(solution)/shard_map/reduce_scatter | solution.py:162
  7.2 3.3 %collective-permute-start = (f32[1,1024]{1,0:T(1,128)}, f32[1,1024]{1,0:T(1,128)S(1)}, u32[]{:S(2)}, u32[]{:S(2)}) collective-permute-start(f32[1,1024]{1,0:T(1,128)} %param.7), channel_id=1, source_target_pairs={{0,64},{64,128},{128,192},{1,65},{65,129},{129,193},{2,66},{66,130... | collective-permute-start | bytes 12296 | tf_op jit(solution)/shard_map/ppermute | solution.py:54
  13.9 1.1 copy-start.4
  13.9 1.1 copy-start.5
  14.8 1.8 %copy-start.3 = (bf16[10,256,512]{2,1,0:T(8,128)(2,1)S(1)}, bf16[10,256,512]{2,1,0:T(8,128)(2,1)}, u32[]{:S(2)}) copy-start(bf16[10,256,512]{2,1,0:T(8,128)(2,1)} %param.11) | copy-start | bytes 7864324
  33.1 2.2 %slice-start = ((s8[5242880]{0:T(1024)(128)(4,1)}), s8[4194304]{0:T(1024)(128)(4,1)S(1)}, s32[]{:S(2)}) async-start(s8[5242880]{0:T(1024)(128)(4,1)} %bitcast.109), calls=%async_computation.2 | async-start | bytes 8388608
  34.1 1.7 %slice-start.1 = ((s8[5242880]{0:T(1024)(128)(4,1)}), s8[1048576]{0:T(1024)(128)(4,1)S(1)}, s32[]{:S(2)}) async-start(s8[5242880]{0:T(1024)(128)(4,1)} %bitcast.109), calls=%async_computation.3 | async-start | bytes 2097152
  45.3 3.1 %copy-start.2 = (f32[1024,1280]{1,0:T(8,128)}, f32[1024,1280]{1,0:T(8,128)S(1)}, u32[]{:S(2)}) copy-start(f32[1024,1280]{1,0:T(8,128)S(1)} %fusion.1) | copy-start | bytes 15728644
  48.5 6.2 %collective-permute-start.1 = (f32[1,8,4,2,8,1280]{5,4,3,2,1,0:T(8,128)}, f32[1,8,4,2,8,1280]{5,4,3,2,1,0:T(8,128)S(1)}, u32[]{:S(2)}, u32[]{:S(2)}) collective-permute-start(f32[1,8,4,2,8,1280]{5,4,3,2,1,0:T(8,128)} %dynamic-slice_bitcast_fusion), channel_id=1, source_target_pairs={{0,64},{64,0},{1,65},{65,1},{2,66},{66,2},{3,67},{67,3},{4,68},{68... | collective-permute-start | bytes 7864328 | tf_op jit(solution)/shard_map/ppermute | solution.py:69
  58.4 85.7 %copy-start.1 = (s32[1,8]{1,0:T(1,128)S(1)}, s32[1,8]{1,0:T(1,128)}, u32[]{:S(2)}) copy-start(s32[1,8]{1,0:T(1,128)} %param.9) | copy-start | bytes 100
  106.7 7.8 %collective-permute-start.2 = (f32[1,1,2,2,8,1280]{5,4,3,2,1,0:T(8,128)S(1)}, f32[1,1,2,2,8,1280]{5,4,3,2,1,0:T(8,128)S(1)}, u32[]{:S(2)}, u32[]{:S(2)}) collective-permute-start(f32[1,1,2,2,8,1280]{5,4,3,2,1,0:T(8,128)S(1)} %dynamic-slice_bitcast_fusion.1), channel_id=1, source_target_pairs={{0,32},{16,48},{32,0},{48,16},{1,33},{17,49},{33,1},{49,17},{2,34}... | collective-permute-start | bytes 491528 | tf_op jit(solution)/shard_map/ppermute | solution.py:69
  115.4 4.5 %collective-permute-start.3 = (f32[1,1,1,2,8,1280]{5,4,3,2,1,0:T(8,128)S(1)}, f32[1,1,1,2,8,1280]{5,4,3,2,1,0:T(8,128)S(1)}, u32[]{:S(2)}, u32[]{:S(2)}) collective-permute-start(f32[1,1,1,2,8,1280]{5,4,3,2,1,0:T(8,128)S(1)} %constant_dynamic-slice_fusion.3), channel_id=1, source_target_pairs={{0,16},{16,0},{32,48},{48,32},{1,17},{17,1},{33,49},{49,33},{2,18}... | collective-permute-start | bytes 245768 | tf_op jit(solution)/shard_map/ppermute | solution.py:69
  120.0 5.6 %collective-permute-start.4 = (f32[1,1,1,1,8,1280]{5,4,3,2,1,0:T(8,128)S(1)}, f32[1,1,1,1,8,1280]{5,4,3,2,1,0:T(8,128)S(1)}, u32[]{:S(2)}, u32[]{:S(2)}) collective-permute-start(f32[1,1,1,1,8,1280]{5,4,3,2,1,0:T(8,128)S(1)} %constant_dynamic-slice_fusion.2), channel_id=1, source_target_pairs={{0,8},{8,0},{1,9},{9,1},{2,10},{10,2},{3,11},{11,3},{4,12},{12,4},... | collective-permute-start | bytes 122888 | tf_op jit(solution)/shard_map/ppermute | solution.py:69
  125.6 3.9 %collective-permute-start.5 = (f32[1,1,1,1,1,4,1280]{6,5,4,3,2,1,0:T(4,128)S(1)}, f32[1,1,1,1,1,4,1280]{6,5,4,3,2,1,0:T(4,128)S(1)}, u32[]{:S(2)}, u32[]{:S(2)}) collective-permute-start(f32[1,1,1,1,1,4,1280]{6,5,4,3,2,1,0:T(4,128)S(1)} %dynamic-slice_bitcast_fusion.2), channel_id=1, source_target_pairs={{0,128},{128,0},{1,129},{129,1},{2,130},{130,2},{3,131},{131,3},{4... | collective-permute-start | bytes 61448 | tf_op jit(solution)/shard_map/ppermute | solution.py:69
  129.5 10.8 %collective-permute-start.6 = (f32[1,1,1,1,1,4,1280]{6,5,4,3,2,1,0:T(4,128)S(1)}, f32[1,1,1,1,1,4,1280]{6,5,4,3,2,1,0:T(4,128)S(1)}, u32[]{:S(2)}, u32[]{:S(2)}) collective-permute-start(f32[1,1,1,1,1,4,1280]{6,5,4,3,2,1,0:T(4,128)S(1)} %bitcast_add_fusion.2), channel_id=1, source_target_pairs={{0,0},{1,16},{2,32},{3,48},{4,64},{5,80},{6,96},{7,112},{8,2},{9,1... | collective-permute-start | bytes 61448 | tf_op jit(solution)/shard_map/ppermute | solution.py:163
Sparse Core Ops, SparseCore 0:
  58.6 47.1 reduce-scatter.1

commit v7 on v6

--- a/solution.py
+++ b/solution.py
@@ -1,6 +1,10 @@
+import os
+
 import jax
 import jax.numpy as jnp
 from jax import lax
+from jax.experimental import pallas as pl
+from jax.experimental.pallas import tpu as pltpu
 from jax.sharding import Mesh, PartitionSpec as P
 
 CLASSES = 256
@@ -71,6 +75,74 @@
     return slab
 
 
+CHUNK = 256
+FRONT = 512
+
+
+def layers_kernel(h0_ref, conv_ref, res_ref, out_ref, buf_a, buf_b):
+    window = h0_ref.shape[0]
+    seg_len = out_ref.shape[0]
+    layer_total = conv_ref.shape[0]
+    gate = conv_ref.shape[2] // 2
+    buf_a[0:FRONT, :] = jnp.zeros((FRONT, buf_a.shape[1]), jnp.float32)
+    buf_b[0:FRONT, :] = jnp.zeros((FRONT, buf_b.shape[1]), jnp.float32)
+    buf_a[FRONT:, :] = h0_ref[...].astype(jnp.float32)
+    bufs = (buf_a, buf_b)
+    for layer_num in range(layer_total):
+        dilation = 2**layer_num
+        later_reach = 2**layer_total - 2 ** (layer_num + 1)
+        needed = round_up(seg_len + later_reach, CHUNK)
+        first_chunk = max(0, (window - needed) // CHUNK)
+        src = bufs[layer_num % 2]
+        dst = bufs[(layer_num + 1) % 2]
+        conv_one = conv_ref[layer_num]
+        res_one = res_ref[layer_num] if layer_num < layer_total - 1 else None
+
+        def body(chunk, carry, src=src, dst=dst, dilation=dilation, conv_one=conv_one,
+                 res_one=res_one, layer_num=layer_num):
+            start = pl.multiple_of(FRONT + chunk * CHUNK, CHUNK)
+            current = src[pl.ds(start, CHUNK), :]
+            if dilation % 8 == 0:
+                delayed = src[pl.ds(start - dilation, CHUNK), :]
+            else:
+                wide = src[pl.ds(start - 8, CHUNK + 8), :]
+                delayed = pltpu.roll(wide, dilation, 0)[8:, :]
+            paired = jnp.concatenate(
+                [delayed.astype(jnp.bfloat16), current.astype(jnp.bfloat16)], 1
+            )
+            preact = jnp.dot(paired, conv_one, preferred_element_type=jnp.float32)
+            gated = (jnp.tanh(preact[:, :gate]) * jax.nn.sigmoid(preact[:, gate:])).astype(
+                jnp.bfloat16
+            )
+
+            @pl.when(chunk * CHUNK >= window - seg_len)
+            def _():
+                row = pl.multiple_of(chunk * CHUNK - (window - seg_len), CHUNK)
+                out_ref[pl.ds(row, CHUNK), layer_num * gate : (layer_num + 1) * gate] = gated
+
+            if res_one is not None:
+                residual_term = jnp.dot(gated, res_one, preferred_element_type=jnp.float32)
+                following = ((current + residual_term) * HALF_ROOT).astype(jnp.bfloat16)
+                dst[pl.ds(start, CHUNK), :] = following.astype(jnp.float32)
+            return carry
+
+        lax.fori_loop(first_chunk, window // CHUNK, body, 0)
+
+
+def run_layers(h0, conv_weight, res_weight, seg_len):
+    window, channels = h0.shape
+    layer_total, _, both = conv_weight.shape
+    return pl.pallas_call(
+        layers_kernel,
+        out_shape=jax.ShapeDtypeStruct((seg_len, layer_total * both // 2), jnp.bfloat16),
+        scratch_shapes=[
+            pltpu.VMEM((FRONT + window, channels), jnp.float32),
+            pltpu.VMEM((FRONT + window, channels), jnp.float32),
+        ],
+        interpret=bool(os.environ.get("SOLUTION_INTERPRET")),
+    )(h0, conv_weight, res_weight)
+
+
 def round_up(value, step):
     return -(-value // step) * step
 
@@ -99,27 +171,10 @@
     layer_total = conv_weight.shape[0]
     reach = 2**layer_total - 1
     earlier = shifted(audio_waves, SEG, 1)
-    window = round_up(seg_len + reach, 16)
+    window = round_up(seg_len + reach, CHUNK)
     extended = jnp.concatenate([earlier, audio_waves], 1)[0, 2 * seg_len - window :]
     hidden = (extended[:, None] * input_weight[None, :]).astype(jnp.bfloat16)
-    gated_list = []
-    for layer_num in range(layer_total):
-        dilation = 2**layer_num
-        later_reach = 2**layer_total - 2 ** (layer_num + 1)
-        in_len = hidden.shape[0]
-        out_len = min(in_len, round_up(seg_len + later_reach, 16))
-        if in_len - dilation >= out_len:
-            delayed = hidden[in_len - out_len - dilation : in_len - dilation]
-        else:
-            delayed = jnp.concatenate(
-                [jnp.zeros((dilation, hidden.shape[1]), hidden.dtype), hidden[: in_len - dilation]],
-                0,
-            )
-        current = hidden[in_len - out_len :]
-        res_one = res_weight[layer_num] if layer_num < layer_total - 1 else None
-        gated, hidden = layer_math(delayed, current, conv_weight[layer_num], res_one)
-        gated_list.append(gated[out_len - seg_len :])
-    stacked = jnp.concatenate(gated_list, 1)
+    stacked = run_layers(hidden, conv_weight, res_weight, seg_len)
     skip_sum = jnp.dot(stacked, skip_weight, preferred_element_type=jnp.float32)
     features = jnp.maximum(skip_sum, 0.0).astype(jnp.bfloat16)
     skip_width = features.shape[1]

time: 152 us -> 172 us (1.13)
  Pallas kernels: 0 us -> 39.5 us
  matrix products: 22.2 us -> 12.9 us
  other arithmetic: 17.2 us -> 10.5 us
  local copies, waits for them, and re-layouts: 7.85 us -> 5.6 us
    pallas_call x0 -> x1, Pallas kernels: none -> 39.5 us  [run_layers(): pl.pallas_call(layers_kernel, out_shape=jax.ShapeDtypeStruct((seg_len, la...]
    dot_general x19 -> x0, matrix products: 12.7 us -> none  [the longest x10 8.25 us: layer_math(): preact = jnp.dot(paired, conv_one, preferred_element_type=jnp.float32)]
    convert_element_type x9 -> x0, other arithmetic: 7.06 us -> none  [layer_math(): (jnp.tanh(preact[:, :gate_width]) * jax.nn.sigmoid(preact[:, gate_width:]...]
    dot_general x1, matrix products: 5.88 us -> 9.15 us  [per_device(): skip_sum = jnp.dot(stacked, skip_weight, preferred_element_type=jnp.float32)]
    unnamed x25 -> x4, local copies, waits for them, and re-layouts: 3.99 us -> 2.3 us
  transfers between devices with their start and end apart: 8 -> 8, of which waited for: 7 -> 7; matrix products, arithmetic and copies ran while one was open for 1% -> 0% of each run, Pallas kernels for 0% -> 0%
where the time goes in v7:
time: 172 us
  waiting for transfers between devices  77.5 us (45%)
  Pallas kernels  39.5 us (23%)
  between operations  15.6 us (9%)
  matrix products  12.9 us (8%)
  other arithmetic  10.5 us (6%)
  starting transfers between devices  10.4 us (6%)
  local copies, waits for them, and re-layouts  5.6 us (3%)
    reduce_scatter x1, waiting for transfers between devices, per_device(): slab = lax.psum_scatter(slab, group, scatter_dimension=stage, tiled=True)  47.3 us
    pallas_call x1, Pallas kernels, run_layers(): pl.pallas_call(layers_kernel, out_shape=jax.ShapeDtypeStruct((seg_len, la...  39.5 us
    ppermute x5, waiting for transfers between devices, exchange_scatter(): slab = mine + lax.ppermute(other, axis, pairs)  22.5 us
    dot_general x1, matrix products, per_device(): skip_sum = jnp.dot(stacked, skip_weight, preferred_element_type=jnp.float32)  9.15 us
    ppermute x1, waiting for transfers between devices, per_device(): slab = lax.ppermute(slab, FINE, owner_pairs(sizes))  7.65 us
    ppermute x5, starting transfers between devices, exchange_scatter(): slab = mine + lax.ppermute(other, axis, pairs)  5.48 us
    add x5, other arithmetic, exchange_scatter(): slab = mine + lax.ppermute(other, axis, pairs)  4.69 us
    dot_general x1, matrix products, per_device(): lax.dot_general(masked, paired, (((0,), (0,)), ((), ())), preferred_eleme...  3.7 us
  transfers between devices with their start and end apart: 8, of which 7 were waited for; matrix products, arithmetic and copies ran while one was open for 0% of the time, Pallas kernels for 0%

profile of v7, /device:TPU:28, one launch (start us, length us, event | category | flops | bytes accessed | tf_op | source)
XLA Modules:
  0.0 171.9 jit_solution(13796571460725500499)
XLA Ops:
  7.2 1.7 %collective-permute-start = (f32[1,1024]{1,0:T(1,128)}, f32[1,1024]{1,0:T(1,128)S(1)}, u32[]{:S(2)}, u32[]{:S(2)}) collective-permute-start(f32[1,1024]{1,0:T(1,128)} %param.7), channel_id=1, source_target_pairs={{0,64},{64,128},{128,192},{1,65},{65,129},{129,193},{2,66},{66,130... | collective-permute-start | bytes 12296 | tf_op jit(solution)/shard_map/ppermute | solution.py:58
  11.2 1.8 %multiply_convert_fusion.h0_ref = bf16[2048,128]{1,0:T(8,128)(2,1)} fusion(f32[128]{0:T(128)} %param.10, f32[2048]{0:T(1024)S(1)} %bitcast.35), kind=kLoop, calls=%fused_computation.12 | loop fusion | flops 524288 | bytes 532992 | tf_op jit(solution)/shard_map/convert_element_type | solution.py:176
  13.0 39.5 %shard_map.89 = bf16[1024,2560]{1,0:T(8,128)(2,1)} custom-call(bf16[2048,128]{1,0:T(8,128)(2,1)} %multiply_convert_fusion.h0_ref, bf16[10,256,512]{2,1,0:T(8,128)(2,1)} %conv_ref.1, bf16[9,256,128]{2,1,0:T(8,128)(2,1)} %res_ref.1), custom_call_target="tpu_custom_call" | custom-call | tf_op jit(solution)/shard_map/pallas_call | solution.py:135
  52.5 9.2 %broadcast_select_fusion = bf16[1024,1024]{0,1:T(8,128)(2,1)S(1)} fusion(pred[1024]{0:T(1024)(128)(4,1)S(1)} %add_compare_fusion, bf16[1024,2560]{1,0:T(8,128)(2,1)} %shard_map.89, bf16[2560,1024]{1,0:T(8,128)(2,1)} %param.13), kind=kOutput, calls=%fused_computation.10 | convolution fusion | flops 5371854848 | bytes 12583936 | tf_op jit(solution)/shard_map/dot_general | solution.py:178
  61.7 3.7 %fusion.1 = f32[1024,1280]{1,0:T(8,128)S(1)} fusion(bf16[1024,1024]{0,1:T(8,128)(2,1)S(1)} %broadcast_select_fusion, bf16[1024,256]{0,1:T(8,128)(2,1)S(1)} %fusion.5, f32[]{:T(128)} %convert_reduce_fusion, s32[1024]{0:T(1024)S(1)} %get-tuple-element.4, s32[1024]{0:T(1024)S(1)} %get-tuple-element.5, s32[1024]{0:T(1024)S(1)} %fusion.6, ...), kind=kOutput, calls=%fused_computation.3 | convolution fusion | flops 2696151040 | bytes 7877636 | tf_op jit(solution)/shard_map/dot_general | solution.py:189
  65.4 2.3 %copy-done.1 = f32[1024,1280]{1,0:T(8,128)} copy-done((f32[1024,1280]{1,0:T(8,128)}, f32[1024,1280]{1,0:T(8,128)S(1)}, u32[]{:S(2)}) %copy-start.1) | copy-done | bytes 5242904
  67.7 1.7 dynamic-slice_bitcast_fusion
  69.3 1.5 collective-permute-start.1
  70.8 4.7 %collective-permute-done.1 = f32[1,8,4,2,8,1280]{5,4,3,2,1,0:T(8,128)S(1)} collective-permute-done((f32[1,8,4,2,8,1280]{5,4,3,2,1,0:T(8,128)}, f32[1,8,4,2,8,1280]{5,4,3,2,1,0:T(8,128)S(1)}, u32[]{:S(2)}, u32[]{:S(2)}) %collective-permute-start.1) | collective-permute-done | bytes 2621472 | tf_op jit(solution)/shard_map/ppermute | solution.py:73
  75.6 3.7 %bitcast_add_fusion = f32[1,8,4,2,8,1280]{5,4,3,2,1,0:T(8,128)} fusion(f32[1,8,4,2,8,1280]{5,4,3,2,1,0:T(8,128)S(1)} %collective-permute-done.1, f32[2,1,8,4,2,8,1280]{6,5,4,3,2,0,1:T(8,128)} %bitcast.32, s32[]{:T(128)S(6)} %select_n.94), kind=kLoop, calls=%fused_computation.8 | loop fusion | flops 655360 | bytes 7864324 | tf_op jit(solution)/shard_map/add | solution.py:73
  79.3 47.3 %reduce-scatter.2.cloned.1.call-done = f32[1,1,4,2,8,1280]{5,4,3,2,1,0:T(8,128)} async-done(((f32[1,8,4,2,8,1280]{5,4,3,2,1,0:T(8,128)}), f32[1,1,4,2,8,1280]{5,4,3,2,1,0:T(8,128)}) %reduce-scatter.2.cloned.1.call-update) | async-done | bytes 327696 | tf_op jit(solution)/shard_map/reduce_scatter | solution.py:217
  126.6 0.9 dynamic-slice_bitcast_fusion.1
  127.5 1.5 collective-permute-start.2
  129.0 6.3 %collective-permute-done.2 = f32[1,1,2,2,8,1280]{5,4,3,2,1,0:T(8,128)S(1)} collective-permute-done((f32[1,1,2,2,8,1280]{5,4,3,2,1,0:T(8,128)S(1)}, f32[1,1,2,2,8,1280]{5,4,3,2,1,0:T(8,128)S(1)}, u32[]{:S(2)}, u32[]{:S(2)}) %collective-permute-start.2) | collective-permute-done | bytes 163872 | tf_op jit(solution)/shard_map/ppermute | solution.py:73
  135.3 0.9 bitcast_add_fusion.1
  136.3 1.0 collective-permute-start.3
  137.3 3.6 %collective-permute-done.3 = f32[1,1,1,2,8,1280]{5,4,3,2,1,0:T(8,128)S(1)} collective-permute-done((f32[1,1,1,2,8,1280]{5,4,3,2,1,0:T(8,128)S(1)}, f32[1,1,1,2,8,1280]{5,4,3,2,1,0:T(8,128)S(1)}, u32[]{:S(2)}, u32[]{:S(2)}) %collective-permute-start.3) | collective-permute-done | bytes 81952 | tf_op jit(solution)/shard_map/ppermute | solution.py:73
  141.4 5.0 %collective-permute-done.4 = f32[1,1,1,1,8,1280]{5,4,3,2,1,0:T(8,128)S(1)} collective-permute-done((f32[1,1,1,1,8,1280]{5,4,3,2,1,0:T(8,128)S(1)}, f32[1,1,1,1,8,1280]{5,4,3,2,1,0:T(8,128)S(1)}, u32[]{:S(2)}, u32[]{:S(2)}) %collective-permute-start.4) | collective-permute-done | bytes 40992 | tf_op jit(solution)/shard_map/ppermute | solution.py:73
  146.5 1.0 collective-permute-start.5
  147.5 2.9 %collective-permute-done.5 = f32[1,1,1,1,1,4,1280]{6,5,4,3,2,1,0:T(4,128)S(1)} collective-permute-done((f32[1,1,1,1,1,4,1280]{6,5,4,3,2,1,0:T(4,128)S(1)}, f32[1,1,1,1,1,4,1280]{6,5,4,3,2,1,0:T(4,128)S(1)}, u32[]{:S(2)}, u32[]{:S(2)}) %collective-permute-start.5) | collective-permute-done | bytes 20512 | tf_op jit(solution)/shard_map/ppermute | solution.py:73
  150.4 3.1 %collective-permute-start.6 = (f32[1,1,1,1,1,4,1280]{6,5,4,3,2,1,0:T(4,128)S(1)}, f32[1,1,1,1,1,4,1280]{6,5,4,3,2,1,0:T(4,128)S(1)}, u32[]{:S(2)}, u32[]{:S(2)}) collective-permute-start(f32[1,1,1,1,1,4,1280]{6,5,4,3,2,1,0:T(4,128)S(1)} %bitcast_add_fusion.2), channel_id=1, source_target_pairs={{0,0},{1,16},{2,32},{3,48},{4,64},{5,80},{6,96},{7,112},{8,2},{9,1... | collective-permute-start | bytes 61448 | tf_op jit(solution)/shard_map/ppermute | solution.py:218
  153.5 7.6 %collective-permute-done.6 = f32[1,1,1,1,1,4,1280]{6,5,4,3,2,1,0:T(4,128)S(1)} collective-permute-done((f32[1,1,1,1,1,4,1280]{6,5,4,3,2,1,0:T(4,128)S(1)}, f32[1,1,1,1,1,4,1280]{6,5,4,3,2,1,0:T(4,128)S(1)}, u32[]{:S(2)}, u32[]{:S(2)}) %collective-permute-start.6) | collective-permute-done | bytes 20512 | tf_op jit(solution)/shard_map/ppermute | solution.py:218
  162.4 0.7 bitcast_select_fusion
  163.2 1.3 slice_divide_fusion
  (26 shorter events, 3.4 us)
Async XLA Ops:
  7.2 2.5 %copy-start = (s32[1,8]{1,0:T(1,128)S(1)}, s32[1,8]{1,0:T(1,128)}, u32[]{:S(2)}) copy-start(s32[1,8]{1,0:T(1,128)} %param.9) | copy-start | bytes 100
  7.2 119.4 %reduce-scatter.2.cloned.1.call-start = ((), (), s32[]{:S(2)}) async-start(), calls=%async_computation.1 | async-start | bytes 2949120 | tf_op jit(solution)/shard_map/reduce_scatter | solution.py:217
  7.2 3.3 %collective-permute-start = (f32[1,1024]{1,0:T(1,128)}, f32[1,1024]{1,0:T(1,128)S(1)}, u32[]{:S(2)}, u32[]{:S(2)}) collective-permute-start(f32[1,1024]{1,0:T(1,128)} %param.7), channel_id=1, source_target_pairs={{0,64},{64,128},{128,192},{1,65},{65,129},{129,193},{2,66},{66,130... | collective-permute-start | bytes 12296 | tf_op jit(solution)/shard_map/ppermute | solution.py:58
  65.4 2.3 %copy-start.1 = (f32[1024,1280]{1,0:T(8,128)}, f32[1024,1280]{1,0:T(8,128)S(1)}, u32[]{:S(2)}) copy-start(f32[1024,1280]{1,0:T(8,128)S(1)} %fusion.1) | copy-start | bytes 15728644
  69.3 6.2 %collective-permute-start.1 = (f32[1,8,4,2,8,1280]{5,4,3,2,1,0:T(8,128)}, f32[1,8,4,2,8,1280]{5,4,3,2,1,0:T(8,128)S(1)}, u32[]{:S(2)}, u32[]{:S(2)}) collective-permute-start(f32[1,8,4,2,8,1280]{5,4,3,2,1,0:T(8,128)} %dynamic-slice_bitcast_fusion), channel_id=1, source_target_pairs={{0,64},{64,0},{1,65},{65,1},{2,66},{66,2},{3,67},{67,3},{4,68},{68... | collective-permute-start | bytes 7864328 | tf_op jit(solution)/shard_map/ppermute | solution.py:73
  127.5 7.8 %collective-permute-start.2 = (f32[1,1,2,2,8,1280]{5,4,3,2,1,0:T(8,128)S(1)}, f32[1,1,2,2,8,1280]{5,4,3,2,1,0:T(8,128)S(1)}, u32[]{:S(2)}, u32[]{:S(2)}) collective-permute-start(f32[1,1,2,2,8,1280]{5,4,3,2,1,0:T(8,128)S(1)} %dynamic-slice_bitcast_fusion.1), channel_id=1, source_target_pairs={{0,32},{16,48},{32,0},{48,16},{1,33},{17,49},{33,1},{49,17},{2,34}... | collective-permute-start | bytes 491528 | tf_op jit(solution)/shard_map/ppermute | solution.py:73
  136.3 4.5 %collective-permute-start.3 = (f32[1,1,1,2,8,1280]{5,4,3,2,1,0:T(8,128)S(1)}, f32[1,1,1,2,8,1280]{5,4,3,2,1,0:T(8,128)S(1)}, u32[]{:S(2)}, u32[]{:S(2)}) collective-permute-start(f32[1,1,1,2,8,1280]{5,4,3,2,1,0:T(8,128)S(1)} %constant_dynamic-slice_fusion.3), channel_id=1, source_target_pairs={{0,16},{16,0},{32,48},{48,32},{1,17},{17,1},{33,49},{49,33},{2,18}... | collective-permute-start | bytes 245768 | tf_op jit(solution)/shard_map/ppermute | solution.py:73
  140.9 5.6 %collective-permute-start.4 = (f32[1,1,1,1,8,1280]{5,4,3,2,1,0:T(8,128)S(1)}, f32[1,1,1,1,8,1280]{5,4,3,2,1,0:T(8,128)S(1)}, u32[]{:S(2)}, u32[]{:S(2)}) collective-permute-start(f32[1,1,1,1,8,1280]{5,4,3,2,1,0:T(8,128)S(1)} %constant_dynamic-slice_fusion.2), channel_id=1, source_target_pairs={{0,8},{8,0},{1,9},{9,1},{2,10},{10,2},{3,11},{11,3},{4,12},{12,4},... | collective-permute-start | bytes 122888 | tf_op jit(solution)/shard_map/ppermute | solution.py:73
  146.5 3.9 %collective-permute-start.5 = (f32[1,1,1,1,1,4,1280]{6,5,4,3,2,1,0:T(4,128)S(1)}, f32[1,1,1,1,1,4,1280]{6,5,4,3,2,1,0:T(4,128)S(1)}, u32[]{:S(2)}, u32[]{:S(2)}) collective-permute-start(f32[1,1,1,1,1,4,1280]{6,5,4,3,2,1,0:T(4,128)S(1)} %dynamic-slice_bitcast_fusion.2), channel_id=1, source_target_pairs={{0,128},{128,0},{1,129},{129,1},{2,130},{130,2},{3,131},{131,3},{4... | collective-permute-start | bytes 61448 | tf_op jit(solution)/shard_map/ppermute | solution.py:73
  150.4 10.8 %collective-permute-start.6 = (f32[1,1,1,1,1,4,1280]{6,5,4,3,2,1,0:T(4,128)S(1)}, f32[1,1,1,1,1,4,1280]{6,5,4,3,2,1,0:T(4,128)S(1)}, u32[]{:S(2)}, u32[]{:S(2)}) collective-permute-start(f32[1,1,1,1,1,4,1280]{6,5,4,3,2,1,0:T(4,128)S(1)} %bitcast_add_fusion.2), channel_id=1, source_target_pairs={{0,0},{1,16},{2,32},{3,48},{4,64},{5,80},{6,96},{7,112},{8,2},{9,1... | collective-permute-start | bytes 61448 | tf_op jit(solution)/shard_map/ppermute | solution.py:218
Sparse Core Ops, SparseCore 0:
  79.4 47.1 reduce-scatter.1

commit v8 on v6

--- a/solution.py
+++ b/solution.py
@@ -153,13 +153,16 @@
     partial = jnp.where(slot, local_count, partial)
     pair = group_sizes[-1] * row_count
     slab = partial.reshape(tuple(group_sizes[:-1]) + (pair, width))
-    for stage, group in enumerate(GROUPS):
-        if stage == len(GROUPS) - 1:
-            slab = slab.reshape(tuple(slab.shape[:-2]) + (group_sizes[-1], row_count, width))
-        if group[0] in EXCHANGED and len(group) == 1:
-            slab = exchange_scatter(slab, group[0], stage)
-        else:
-            slab = lax.psum_scatter(slab, group, scatter_dimension=stage, tiled=True)
+    slab = exchange_scatter(slab, "core", 0)
+    half = width // 2
+    left = lax.psum_scatter(slab[..., :half], "z", scatter_dimension=1, tiled=True)
+    right = exchange_scatter(slab[..., half:], "y", 2)
+    left = exchange_scatter(left, "y", 2)
+    right = lax.psum_scatter(right, "z", scatter_dimension=1, tiled=True)
+    slab = jnp.concatenate([left, right], -1)
+    slab = exchange_scatter(slab, "xh", 3)
+    slab = slab.reshape(tuple(slab.shape[:-2]) + (group_sizes[-1], row_count, width))
+    slab = exchange_scatter(slab, "xl", 4)
     slab = lax.ppermute(slab, FINE, owner_pairs(sizes))
     owned_rows = slab.reshape(row_count, width)
     first_col = lax.axis_index(FINE) * row_count

time: 152 us -> 173 us (1.14)
  waiting for transfers between devices: 77.1 us -> 94.5 us
  starting transfers between devices: 10.7 us -> 12.8 us
    ppermute x5 -> x7, waiting for transfers between devices: 22.2 us -> 36.5 us  [exchange_scatter(): slab = mine + lax.ppermute(other, axis, pairs)]
    reduce_scatter x1 -> x2, waiting for transfers between devices: 47.3 us -> 50.5 us  [the longest x1 27.1 us: per_device(): right = lax.psum_scatter(right, 'z', scatter_dimension=1, tiled=True)]
    ppermute x5 -> x7, starting transfers between devices: 5.77 us -> 7.72 us  [exchange_scatter(): slab = mine + lax.ppermute(other, axis, pairs)]
    add x5 -> x7, other arithmetic: 4.69 us -> 4.74 us  [exchange_scatter(): slab = mine + lax.ppermute(other, axis, pairs)]
  transfers between devices with their start and end apart: 8 -> 11, of which waited for: 7 -> 9; matrix products, arithmetic and copies ran while one was open for 1% -> 2% of each run, Pallas kernels for 0% -> 0%
where the time goes in v8:
time: 173 us
  waiting for transfers between devices  94.5 us (55%)
  matrix products  22.3 us (13%)
  other arithmetic  18 us (10%)
  between operations  15.9 us (9%)
  starting transfers between devices  12.8 us (7%)
  local copies, waits for them, and re-layouts  9.26 us (5%)
    ppermute x7, waiting for transfers between devices, exchange_scatter(): slab = mine + lax.ppermute(other, axis, pairs)  36.5 us
    reduce_scatter x1, waiting for transfers between devices, per_device(): right = lax.psum_scatter(right, 'z', scatter_dimension=1, tiled=True)  27.1 us
    reduce_scatter x1, waiting for transfers between devices, per_device(): lax.psum_scatter(slab[..., :half], 'z', scatter_dimension=1, tiled=True)  23.4 us
    dot_general x10, matrix products, layer_math(): preact = jnp.dot(paired, conv_one, preferred_element_type=jnp.float32)  8.26 us
    ppermute x7, starting transfers between devices, exchange_scatter(): slab = mine + lax.ppermute(other, axis, pairs)  7.72 us
    ppermute x1, waiting for transfers between devices, per_device(): slab = lax.ppermute(slab, FINE, owner_pairs(sizes))  7.46 us
    convert_element_type x9, other arithmetic, layer_math(): (jnp.tanh(preact[:, :gate_width]) * jax.nn.sigmoid(preact[:, gate_width:]...  7.07 us
    dot_general x1, matrix products, per_device(): skip_sum = jnp.dot(stacked, skip_weight, preferred_element_type=jnp.float32)  5.88 us
  transfers between devices with their start and end apart: 11, of which 9 were waited for; matrix products, arithmetic and copies ran while one was open for 2% of the time, Pallas kernels for 0%

profile of v8, /device:TPU:28, one launch (start us, length us, event | category | flops | bytes accessed | tf_op | source)
XLA Modules:
  0.0 172.8 jit_solution(16297992108841440149)
XLA Ops:
  7.2 1.7 %collective-permute-start = (f32[1,1024]{1,0:T(1,128)}, f32[1,1024]{1,0:T(1,128)S(1)}, u32[]{:S(2)}, u32[]{:S(2)}) collective-permute-start(f32[1,1024]{1,0:T(1,128)} %param.7), channel_id=1, source_target_pairs={{0,64},{64,128},{128,192},{1,65},{65,129},{129,193},{2,66},{66,130... | collective-permute-start | bytes 12296 | tf_op jit(solution)/shard_map/ppermute | solution.py:54
  11.2 1.0 multiply_convert_fusion
  12.2 1.7 fusion.72
  35.8 5.9 %broadcast_select_fusion = bf16[1024,1024]{0,1:T(8,128)(2,1)S(1)} fusion(pred[1024]{0:T(1024)(128)(4,1)S(1)} %add_compare_fusion, bf16[1024,2560]{0,1:T(8,128)(2,1)S(1)} %fusion.119, bf16[2560,1024]{1,0:T(8,128)(2,1)S(1)} %bitcast.117), kind=kOutput, calls=%fused_computation.83 | convolution fusion | flops 5371854848 | bytes 12583936 | tf_op jit(solution)/shard_map/dot_general | solution.py:123
  41.7 3.7 %fusion.1 = f32[1024,1280]{1,0:T(8,128)S(1)} fusion(bf16[1024,1024]{0,1:T(8,128)(2,1)S(1)} %broadcast_select_fusion, bf16[1024,256]{0,1:T(8,128)(2,1)S(1)} %fusion.94, f32[]{:T(128)} %convert_reduce_fusion, s32[1024]{0:T(1024)S(1)} %get-tuple-element.20, s32[1024]{0:T(1024)S(1)} %get-tuple-element.21, s32[1024]{0:T(1024)S(1)} %fusion.168, ...), kind=kOutput, calls=%fused_computation.3 | convolution fusion | flops 2696151040 | bytes 7877636 | tf_op jit(solution)/shard_map/dot_general | solution.py:134
  45.4 1.8 %dynamic-slice_bitcast_fusion = f32[1,8,4,2,8,1280]{5,4,3,2,1,0:T(8,128)} fusion(f32[2,1,8,4,2,8,1280]{6,5,4,3,2,0,1:T(8,128)S(1)} %bitcast.108, s32[]{:T(128)S(6)} %select_n.107), kind=kLoop, calls=%fused_computation.9 | loop fusion | bytes 5242884 | tf_op jit(solution)/shard_map/jit(dynamic_index_in_dim)/squeeze | solution.py:67
  47.2 1.3 copy-done.2
  48.5 1.5 collective-permute-start.1
  50.0 4.7 %collective-permute-done.1 = f32[1,8,4,2,8,1280]{5,4,3,2,1,0:T(8,128)S(1)} collective-permute-done((f32[1,8,4,2,8,1280]{5,4,3,2,1,0:T(8,128)}, f32[1,8,4,2,8,1280]{5,4,3,2,1,0:T(8,128)S(1)}, u32[]{:S(2)}, u32[]{:S(2)}) %collective-permute-start.1) | collective-permute-done | bytes 2621472 | tf_op jit(solution)/shard_map/ppermute | solution.py:69
  54.8 2.2 %bitcast_add_fusion = f32[1,8,4,2,8,1280]{5,4,3,2,1,0:T(8,128)S(1)} fusion(f32[1,8,4,2,8,1280]{5,4,3,2,1,0:T(8,128)S(1)} %collective-permute-done.1, f32[2,1,8,4,2,8,1280]{6,5,4,3,2,0,1:T(8,128)} %bitcast.109, s32[]{:T(128)S(6)} %select_n.106), kind=kLoop, calls=%fused_computation.8 | loop fusion | flops 655360 | bytes 7864324 | tf_op jit(solution)/shard_map/add | solution.py:69
  57.0 1.4 fusion.189
  58.5 1.3 collective-permute-start.4
  59.8 17.3 %collective-permute-done.4 = f32[1,8,2,2,8,640]{5,4,3,2,1,0:T(8,128)S(1)} collective-permute-done((f32[1,8,2,2,8,640]{5,4,3,2,1,0:T(8,128)S(1)}, f32[1,8,2,2,8,640]{5,4,3,2,1,0:T(8,128)S(1)}, u32[]{:S(2)}, u32[]{:S(2)}) %collective-permute-start.4) | collective-permute-done | bytes 655392 | tf_op jit(solution)/shard_map/ppermute | solution.py:69
  78.1 23.4 %reduce-scatter.3.cloned.1.call-done = f32[1,1,4,2,8,640]{5,4,3,2,1,0:T(8,128)} async-done(((f32[1,8,4,2,8,640]{5,4,3,2,1,0:T(8,128)}), f32[1,1,4,2,8,640]{5,4,3,2,1,0:T(8,128)}) %reduce-scatter.3.cloned.1.call-update) | async-done | bytes 163856 | tf_op jit(solution)/shard_map/reduce_scatter | solution.py:158
  102.3 1.4 collective-permute-start.2
  104.5 3.7 %collective-permute-done.2 = f32[1,1,2,2,8,640]{5,4,3,2,1,0:T(8,128)S(1)} collective-permute-done((f32[1,1,2,2,8,640]{5,4,3,2,1,0:T(8,128)S(1)}, f32[1,1,2,2,8,640]{5,4,3,2,1,0:T(8,128)S(1)}, u32[]{:S(2)}, u32[]{:S(2)}) %collective-permute-start.2) | collective-permute-done | bytes 81952 | tf_op jit(solution)/shard_map/ppermute | solution.py:69
  110.1 3.2 %collective-permute-done.3 = f32[1,1,1,2,8,640]{5,4,3,2,1,0:T(8,128)S(1)} collective-permute-done((f32[1,1,1,2,8,640]{5,4,3,2,1,0:T(8,128)S(1)}, f32[1,1,1,2,8,640]{5,4,3,2,1,0:T(8,128)S(1)}, u32[]{:S(2)}, u32[]{:S(2)}) %collective-permute-start.3) | collective-permute-done | bytes 40992 | tf_op jit(solution)/shard_map/ppermute | solution.py:69
  113.3 27.1 %reduce-scatter.5.cloned.1.call-done = f32[1,1,1,2,8,640]{5,4,3,2,1,0:T(8,128)} async-done(((f32[1,8,1,2,8,640]{5,4,3,2,1,0:T(8,128)}), f32[1,1,1,2,8,640]{5,4,3,2,1,0:T(8,128)}) %reduce-scatter.5.cloned.1.call-update) | async-done | bytes 40976 | tf_op jit(solution)/shard_map/reduce_scatter | solution.py:161
  141.7 5.0 %collective-permute-done.6 = f32[1,1,1,1,8,1280]{5,4,3,2,1,0:T(8,128)S(1)} collective-permute-done((f32[1,1,1,1,8,1280]{5,4,3,2,1,0:T(8,128)S(1)}, f32[1,1,1,1,8,1280]{5,4,3,2,1,0:T(8,128)S(1)}, u32[]{:S(2)}, u32[]{:S(2)}) %collective-permute-start.6) | collective-permute-done | bytes 40992 | tf_op jit(solution)/shard_map/ppermute | solution.py:69
  147.4 1.2 collective-permute-start.7
  148.7 2.6 %collective-permute-done.7 = f32[1,1,1,1,1,4,1280]{6,5,4,3,2,1,0:T(4,128)S(1)} collective-permute-done((f32[1,1,1,1,1,4,1280]{6,5,4,3,2,1,0:T(4,128)S(1)}, f32[1,1,1,1,1,4,1280]{6,5,4,3,2,1,0:T(4,128)S(1)}, u32[]{:S(2)}, u32[]{:S(2)}) %collective-permute-start.7) | collective-permute-done | bytes 20512 | tf_op jit(solution)/shard_map/ppermute | solution.py:69
  151.3 3.3 %collective-permute-start.8 = (f32[1,1,1,1,1,4,1280]{6,5,4,3,2,1,0:T(4,128)S(1)}, f32[1,1,1,1,1,4,1280]{6,5,4,3,2,1,0:T(4,128)S(1)}, u32[]{:S(2)}, u32[]{:S(2)}) collective-permute-start(f32[1,1,1,1,1,4,1280]{6,5,4,3,2,1,0:T(4,128)S(1)} %bitcast_add_fusion.3), channel_id=1, source_target_pairs={{0,0},{1,16},{2,32},{3,48},{4,64},{5,80},{6,96},{7,112},{8,2},{9,1... | collective-permute-start | bytes 61448 | tf_op jit(solution)/shard_map/ppermute | solution.py:166
  154.6 7.5 %collective-permute-done.8 = f32[1,1,1,1,1,4,1280]{6,5,4,3,2,1,0:T(4,128)S(1)} collective-permute-done((f32[1,1,1,1,1,4,1280]{6,5,4,3,2,1,0:T(4,128)S(1)}, f32[1,1,1,1,1,4,1280]{6,5,4,3,2,1,0:T(4,128)S(1)}, u32[]{:S(2)}, u32[]{:S(2)}) %collective-permute-start.8) | collective-permute-done | bytes 20512 | tf_op jit(solution)/shard_map/ppermute | solution.py:166
  163.4 1.3 slice_divide_fusion
  (95 shorter events, 31.7 us)
Async XLA Ops:
  7.2 2.5 %copy-start = (s32[1,8]{1,0:T(1,128)S(1)}, s32[1,8]{1,0:T(1,128)}, u32[]{:S(2)}) copy-start(s32[1,8]{1,0:T(1,128)} %param.9) | copy-start | bytes 100
  7.2 94.3 %reduce-scatter.3.cloned.1.call-start = ((), (), s32[]{:S(2)}) async-start(), calls=%async_computation.2 | async-start | bytes 1474560 | tf_op jit(solution)/shard_map/reduce_scatter | solution.py:158
  7.2 3.3 %collective-permute-start = (f32[1,1024]{1,0:T(1,128)}, f32[1,1024]{1,0:T(1,128)S(1)}, u32[]{:S(2)}, u32[]{:S(2)}) collective-permute-start(f32[1,1024]{1,0:T(1,128)} %param.7), channel_id=1, source_target_pairs={{0,64},{64,128},{128,192},{1,65},{65,129},{129,193},{2,66},{66,130... | collective-permute-start | bytes 12296 | tf_op jit(solution)/shard_map/ppermute | solution.py:54
  13.9 1.1 copy-start.4
  13.9 1.1 copy-start.5
  14.8 1.8 %copy-start.3 = (bf16[10,256,512]{2,1,0:T(8,128)(2,1)S(1)}, bf16[10,256,512]{2,1,0:T(8,128)(2,1)}, u32[]{:S(2)}) copy-start(bf16[10,256,512]{2,1,0:T(8,128)(2,1)} %param.11) | copy-start | bytes 7864324
  33.1 2.2 %slice-start = ((s8[5242880]{0:T(1024)(128)(4,1)}), s8[4194304]{0:T(1024)(128)(4,1)S(1)}, s32[]{:S(2)}) async-start(s8[5242880]{0:T(1024)(128)(4,1)} %bitcast.116), calls=%async_computation.4 | async-start | bytes 8388608
  34.2 1.7 slice-start.1
  45.4 3.1 %copy-start.2 = (f32[1024,1280]{1,0:T(8,128)}, f32[1024,1280]{1,0:T(8,128)S(1)}, u32[]{:S(2)}) copy-start(f32[1024,1280]{1,0:T(8,128)S(1)} %fusion.1) | copy-start | bytes 15728644
  48.5 6.2 %collective-permute-start.1 = (f32[1,8,4,2,8,1280]{5,4,3,2,1,0:T(8,128)}, f32[1,8,4,2,8,1280]{5,4,3,2,1,0:T(8,128)S(1)}, u32[]{:S(2)}, u32[]{:S(2)}) collective-permute-start(f32[1,8,4,2,8,1280]{5,4,3,2,1,0:T(8,128)} %dynamic-slice_bitcast_fusion), channel_id=1, source_target_pairs={{0,64},{64,0},{1,65},{65,1},{2,66},{66,2},{3,67},{67,3},{4,68},{68... | collective-permute-start | bytes 7864328 | tf_op jit(solution)/shard_map/ppermute | solution.py:69
  58.4 82.0 %reduce-scatter.5.cloned.1.call-start = ((), (), s32[]{:S(2)}) async-start(), calls=%async_computation.3 | async-start | bytes 368640 | tf_op jit(solution)/shard_map/reduce_scatter | solution.py:161
  58.5 18.6 %collective-permute-start.4 = (f32[1,8,2,2,8,640]{5,4,3,2,1,0:T(8,128)S(1)}, f32[1,8,2,2,8,640]{5,4,3,2,1,0:T(8,128)S(1)}, u32[]{:S(2)}, u32[]{:S(2)}) collective-permute-start(f32[1,8,2,2,8,640]{5,4,3,2,1,0:T(8,128)S(1)} %dynamic-slice_bitcast_fusion.1), channel_id=1, source_target_pairs={{0,32},{16,48},{32,0},{48,16},{1,33},{17,49},{33,1},{49,17},{2,34}... | collective-permute-start | bytes 1966088 | tf_op jit(solution)/shard_map/ppermute | solution.py:69
  77.1 88.8 %copy-start.1 = (s32[1,8]{1,0:T(1,128)S(1)}, s32[1,8]{1,0:T(1,128)}, u32[]{:S(2)}) copy-start(s32[1,8]{1,0:T(1,128)} %param.9) | copy-start | bytes 100
  77.2 26.5 %collective-permute-start.5 = (f32[1,8,1,2,8,640]{5,4,3,2,1,0:T(8,128)S(1)}, f32[1,8,1,2,8,640]{5,4,3,2,1,0:T(8,128)S(1)}, u32[]{:S(2)}, u32[]{:S(2)}) collective-permute-start(f32[1,8,1,2,8,640]{5,4,3,2,1,0:T(8,128)S(1)} %constant_dynamic-slice_fusion.2), channel_id=1, source_target_pairs={{0,16},{16,0},{32,48},{48,32},{1,17},{17,1},{33,49},{49,33},{2,18}... | collective-permute-start | bytes 983048 | tf_op jit(solution)/shard_map/ppermute | solution.py:69
  102.3 5.9 %collective-permute-start.2 = (f32[1,1,2,2,8,640]{5,4,3,2,1,0:T(8,128)S(1)}, f32[1,1,2,2,8,640]{5,4,3,2,1,0:T(8,128)S(1)}, u32[]{:S(2)}, u32[]{:S(2)}) collective-permute-start(f32[1,1,2,2,8,640]{5,4,3,2,1,0:T(8,128)S(1)} %dynamic-slice_bitcast_fusion.2), channel_id=1, source_target_pairs={{0,32},{16,48},{32,0},{48,16},{1,33},{17,49},{33,1},{49,17},{2,34}... | collective-permute-start | bytes 245768 | tf_op jit(solution)/shard_map/ppermute | solution.py:69
  109.2 4.1 %collective-permute-start.3 = (f32[1,1,1,2,8,640]{5,4,3,2,1,0:T(8,128)S(1)}, f32[1,1,1,2,8,640]{5,4,3,2,1,0:T(8,128)S(1)}, u32[]{:S(2)}, u32[]{:S(2)}) collective-permute-start(f32[1,1,1,2,8,640]{5,4,3,2,1,0:T(8,128)S(1)} %constant_dynamic-slice_fusion.3), channel_id=1, source_target_pairs={{0,16},{16,0},{32,48},{48,32},{1,17},{17,1},{33,49},{49,33},{2,18}... | collective-permute-start | bytes 122888 | tf_op jit(solution)/shard_map/ppermute | solution.py:69
  141.2 5.5 %collective-permute-start.6 = (f32[1,1,1,1,8,1280]{5,4,3,2,1,0:T(8,128)S(1)}, f32[1,1,1,1,8,1280]{5,4,3,2,1,0:T(8,128)S(1)}, u32[]{:S(2)}, u32[]{:S(2)}) collective-permute-start(f32[1,1,1,1,8,1280]{5,4,3,2,1,0:T(8,128)S(1)} %fusion.165), channel_id=1, source_target_pairs={{0,8},{8,0},{1,9},{9,1},{2,10},{10,2},{3,11},{11,3},{4,12},{12,4},... | collective-permute-start | bytes 122888 | tf_op jit(solution)/shard_map/ppermute | solution.py:69
  147.4 3.9 %collective-permute-start.7 = (f32[1,1,1,1,1,4,1280]{6,5,4,3,2,1,0:T(4,128)S(1)}, f32[1,1,1,1,1,4,1280]{6,5,4,3,2,1,0:T(4,128)S(1)}, u32[]{:S(2)}, u32[]{:S(2)}) collective-permute-start(f32[1,1,1,1,1,4,1280]{6,5,4,3,2,1,0:T(4,128)S(1)} %dynamic-slice_bitcast_fusion.3), channel_id=1, source_target_pairs={{0,128},{128,0},{1,129},{129,1},{2,130},{130,2},{3,131},{131,3},{4... | collective-permute-start | bytes 61448 | tf_op jit(solution)/shard_map/ppermute | solution.py:69
  151.3 10.8 %collective-permute-start.8 = (f32[1,1,1,1,1,4,1280]{6,5,4,3,2,1,0:T(4,128)S(1)}, f32[1,1,1,1,1,4,1280]{6,5,4,3,2,1,0:T(4,128)S(1)}, u32[]{:S(2)}, u32[]{:S(2)}) collective-permute-start(f32[1,1,1,1,1,4,1280]{6,5,4,3,2,1,0:T(4,128)S(1)} %bitcast_add_fusion.3), channel_id=1, source_target_pairs={{0,0},{1,16},{2,32},{3,48},{4,64},{5,80},{6,96},{7,112},{8,2},{9,1... | collective-permute-start | bytes 61448 | tf_op jit(solution)/shard_map/ppermute | solution.py:166
Sparse Core Ops, SparseCore 0:
  58.5 42.8 reduce-scatter.2
  104.7 35.7 reduce-scatter.4

commit v9 on v8

--- a/solution.py
+++ b/solution.py
@@ -35,7 +35,7 @@
             size = 1
             for name in group:
                 size *= sizes[name]
-            block = block * size + linear(index, group, sizes)
+            block = block * size + reverse_bits(linear(index, group, sizes), size)
         pairs.append((linear(index, FINE, sizes), block))
     return pairs
 
@@ -54,9 +54,18 @@
     return lax.ppermute(value, axis, pairs)
 
 
+def reverse_bits(value, size):
+    result = 0
+    bit = 1
+    while bit < size:
+        result = result * 2 + (value // bit) % 2
+        bit *= 2
+    return result
+
+
 def exchange_scatter(slab, axis, dim):
     size = slab.shape[dim]
-    index = lax.axis_index(axis)
+    index = reverse_bits(lax.axis_index(axis), size)
     bit = size // 2
     while bit >= 1:
         shape = slab.shape
@@ -65,7 +74,8 @@
         side = (index // bit) % 2
         mine = lax.dynamic_index_in_dim(halves, side, dim, keepdims=False)
         other = lax.dynamic_index_in_dim(halves, 1 - side, dim, keepdims=False)
-        pairs = [(i, i ^ bit) for i in range(size)]
+        flip = reverse_bits(bit, size)
+        pairs = [(i, i ^ flip) for i in range(size)]
         slab = mine + lax.ppermute(other, axis, pairs)
         bit //= 2
     return slab
@@ -155,10 +165,10 @@
     slab = partial.reshape(tuple(group_sizes[:-1]) + (pair, width))
     slab = exchange_scatter(slab, "core", 0)
     half = width // 2
-    left = lax.psum_scatter(slab[..., :half], "z", scatter_dimension=1, tiled=True)
+    left = exchange_scatter(slab[..., :half], "z", 1)
     right = exchange_scatter(slab[..., half:], "y", 2)
     left = exchange_scatter(left, "y", 2)
-    right = lax.psum_scatter(right, "z", scatter_dimension=1, tiled=True)
+    right = exchange_scatter(right, "z", 1)
     slab = jnp.concatenate([left, right], -1)
     slab = exchange_scatter(slab, "xh", 3)
     slab = slab.reshape(tuple(slab.shape[:-2]) + (group_sizes[-1], row_count, width))

time: 173 us -> 144 us (0.83)
  waiting for transfers between devices: 94.5 us -> 63.6 us
  starting transfers between devices: 12.8 us -> 29.9 us
  between operations: 15.9 us -> 2.6 us
  other arithmetic: 18 us -> 16.2 us
    reduce_scatter x2 -> x0, waiting for transfers between devices: 50.5 us -> none  [the longest x1 27.1 us: per_device(): right = lax.psum_scatter(right, 'z', scatter_dimension=1, tiled=True)]
    ppermute x7 -> x13, waiting for transfers between devices: 36.5 us -> 54.6 us  [exchange_scatter(): slab = mine + lax.ppermute(other, axis, pairs)]
    ppermute x7 -> x13, starting transfers between devices: 7.72 us -> 24.5 us  [exchange_scatter(): slab = mine + lax.ppermute(other, axis, pairs)]
    add x7 -> x13, other arithmetic: 4.74 us -> 3.69 us  [exchange_scatter(): slab = mine + lax.ppermute(other, axis, pairs)]
    squeeze x6 -> x12, local copies, waits for them, and re-layouts: 2.81 us -> 3.81 us  [exchange_scatter(): other = lax.dynamic_index_in_dim(halves, 1 - side, dim, keepdims=False)]
  transfers between devices with their start and end apart: 11 -> 15, of which waited for: 9 -> 11; matrix products, arithmetic and copies ran while one was open for 2% -> 2% of each run, Pallas kernels for 0% -> 0%
where the time goes in v9:
time: 144 us
  waiting for transfers between devices  63.6 us (44%)
  starting transfers between devices  29.9 us (21%)
  matrix products  22.2 us (15%)
  other arithmetic  16.2 us (11%)
  local copies, waits for them, and re-layouts  9.17 us (6%)
  between operations  2.6 us (2%)
    ppermute x13, waiting for transfers between devices, exchange_scatter(): slab = mine + lax.ppermute(other, axis, pairs)  54.6 us
    ppermute x13, starting transfers between devices, exchange_scatter(): slab = mine + lax.ppermute(other, axis, pairs)  24.5 us
    ppermute x1, waiting for transfers between devices, per_device(): slab = lax.ppermute(slab, FINE, owner_pairs(sizes))  9.03 us
    dot_general x10, matrix products, layer_math(): preact = jnp.dot(paired, conv_one, preferred_element_type=jnp.float32)  8.25 us
    convert_element_type x9, other arithmetic, layer_math(): (jnp.tanh(preact[:, :gate_width]) * jax.nn.sigmoid(preact[:, gate_width:]...  7.06 us
    dot_general x1, matrix products, per_device(): skip_sum = jnp.dot(stacked, skip_weight, preferred_element_type=jnp.float32)  5.88 us
    dot_general x9, matrix products, layer_math(): residual_term = jnp.dot(gated, res_one, preferred_element_type=jnp.float32)  4.44 us
    unnamed x25, local copies, waits for them, and re-layouts  3.98 us
  transfers between devices with their start and end apart: 15, of which 11 were waited for; matrix products, arithmetic and copies ran while one was open for 2% of the time, Pallas kernels for 0%

profile of v9, /device:TPU:28, one launch (start us, length us, event | category | flops | bytes accessed | tf_op | source)
XLA Modules:
  0.0 143.7 jit_solution(14951335241175484230)
XLA Ops:
  0.6 1.7 %collective-permute-start = (f32[1,1024]{1,0:T(1,128)}, f32[1,1024]{1,0:T(1,128)S(1)}, u32[]{:S(2)}, u32[]{:S(2)}) collective-permute-start(f32[1,1024]{1,0:T(1,128)} %param.7), channel_id=1, source_target_pairs={{0,64},{64,128},{128,192},{1,65},{65,129},{129,193},{2,66},{66,130... | collective-permute-start | bytes 12296 | tf_op jit(solution)/shard_map/ppermute | solution.py:54
  5.6 1.7 %fusion.72 = f32[2048,512]{0,1:T(8,128)S(1)} fusion(bf16[2047,128]{1,0:T(8,128)(2,1)S(1)} %bitcast.132, bf16[2048,128]{1,0:T(8,128)(2,1)S(1)} %multiply_convert_fusion, bf16[10,256,512]{2,1,0:T(8,128)(2,1)} %param.11), kind=kOutput, calls=%fused_computation.106 | convolution fusion | flops 540016640 | bytes 5504768 | tf_op jit(solution)/shard_map/dot_general | solution.py:91
  29.2 5.9 %broadcast_select_fusion = bf16[1024,1024]{0,1:T(8,128)(2,1)S(1)} fusion(pred[1024]{0:T(1024)(128)(4,1)S(1)} %add_compare_fusion, bf16[1024,2560]{0,1:T(8,128)(2,1)S(1)} %fusion.119, bf16[2560,1024]{1,0:T(8,128)(2,1)S(1)} %bitcast.145), kind=kOutput, calls=%fused_computation.83 | convolution fusion | flops 5371854848 | bytes 12583936 | tf_op jit(solution)/shard_map/dot_general | solution.py:133
  35.1 3.7 %fusion.1 = f32[1024,1280]{1,0:T(8,128)S(1)} fusion(bf16[1024,1024]{0,1:T(8,128)(2,1)S(1)} %broadcast_select_fusion, bf16[1024,256]{0,1:T(8,128)(2,1)S(1)} %fusion.94, f32[]{:T(128)} %convert_reduce_fusion, s32[1024]{0:T(1024)S(1)} %get-tuple-element.20, s32[1024]{0:T(1024)S(1)} %get-tuple-element.21, s32[1024]{0:T(1024)S(1)} %fusion.168, ...), kind=kOutput, calls=%fused_computation.3 | convolution fusion | flops 2696151040 | bytes 7877636 | tf_op jit(solution)/shard_map/dot_general | solution.py:144
  38.8 1.8 %dynamic-slice_bitcast_fusion = f32[1,8,4,2,8,1280]{5,4,3,2,1,0:T(8,128)} fusion(f32[2,1,8,4,2,8,1280]{6,5,4,3,2,0,1:T(8,128)S(1)} %bitcast.130, s32[]{:T(128)S(6)} %select_n.227), kind=kLoop, calls=%fused_computation.9 | loop fusion | bytes 5242884 | tf_op jit(solution)/shard_map/jit(dynamic_index_in_dim)/squeeze | solution.py:76
  41.9 1.5 %collective-permute-start.1 = (f32[1,8,4,2,8,1280]{5,4,3,2,1,0:T(8,128)}, f32[1,8,4,2,8,1280]{5,4,3,2,1,0:T(8,128)S(1)}, u32[]{:S(2)}, u32[]{:S(2)}) collective-permute-start(f32[1,8,4,2,8,1280]{5,4,3,2,1,0:T(8,128)} %dynamic-slice_bitcast_fusion), channel_id=1, source_target_pairs={{0,64},{64,0},{1,65},{65,1},{2,66},{66,2},{3,67},{67,3},{4,68},{68... | collective-permute-start | bytes 7864328 | tf_op jit(solution)/shard_map/ppermute | solution.py:79
  43.4 4.7 %collective-permute-done.1 = f32[1,8,4,2,8,1280]{5,4,3,2,1,0:T(8,128)S(1)} collective-permute-done((f32[1,8,4,2,8,1280]{5,4,3,2,1,0:T(8,128)}, f32[1,8,4,2,8,1280]{5,4,3,2,1,0:T(8,128)S(1)}, u32[]{:S(2)}, u32[]{:S(2)}) %collective-permute-start.1) | collective-permute-done | bytes 2621472 | tf_op jit(solution)/shard_map/ppermute | solution.py:79
  48.1 2.2 %bitcast_add_fusion = f32[1,8,4,2,8,1280]{5,4,3,2,1,0:T(8,128)S(1)} fusion(f32[1,8,4,2,8,1280]{5,4,3,2,1,0:T(8,128)S(1)} %collective-permute-done.1, f32[2,1,8,4,2,8,1280]{6,5,4,3,2,0,1:T(8,128)} %bitcast.131, s32[]{:T(128)S(6)} %select_n.226), kind=kLoop, calls=%fused_computation.8 | loop fusion | flops 655360 | bytes 7864324 | tf_op jit(solution)/shard_map/add | solution.py:79
  51.6 1.9 %collective-permute-start.2 = (f32[1,4,4,2,8,640]{5,4,3,2,1,0:T(8,128)}, f32[1,4,4,2,8,640]{5,4,3,2,1,0:T(8,128)S(1)}, u32[]{:S(2)}, u32[]{:S(2)}) collective-permute-start(f32[1,4,4,2,8,640]{5,4,3,2,1,0:T(8,128)} %dynamic-slice_bitcast_fusion.2), channel_id=1, source_target_pairs={{0,1},{1,0},{2,3},{3,2},{4,5},{5,4},{6,7},{7,6},{8,9},{9,8},{10,11... | collective-permute-start | bytes 1966088 | tf_op jit(solution)/shard_map/ppermute | solution.py:79
  55.1 13.8 %collective-permute-done.2 = f32[1,4,4,2,8,640]{5,4,3,2,1,0:T(8,128)S(1)} collective-permute-done((f32[1,4,4,2,8,640]{5,4,3,2,1,0:T(8,128)}, f32[1,4,4,2,8,640]{5,4,3,2,1,0:T(8,128)S(1)}, u32[]{:S(2)}, u32[]{:S(2)}) %collective-permute-start.2) | collective-permute-done | bytes 655392 | tf_op jit(solution)/shard_map/ppermute | solution.py:79
  69.1 3.4 %collective-permute-start.3 = (f32[1,2,4,2,8,640]{5,4,3,2,1,0:T(8,128)S(1)}, f32[1,2,4,2,8,640]{5,4,3,2,1,0:T(8,128)S(1)}, u32[]{:S(2)}, u32[]{:S(2)}) collective-permute-start(f32[1,2,4,2,8,640]{5,4,3,2,1,0:T(8,128)S(1)} %dynamic-slice_bitcast_fusion.3), channel_id=1, source_target_pairs={{0,2},{1,3},{2,0},{3,1},{4,6},{5,7},{6,4},{7,5},{8,10},{9,11},{10,... | collective-permute-start | bytes 983048 | tf_op jit(solution)/shard_map/ppermute | solution.py:79
  75.0 12.1 %collective-permute-done.3 = f32[1,2,4,2,8,640]{5,4,3,2,1,0:T(8,128)S(1)} collective-permute-done((f32[1,2,4,2,8,640]{5,4,3,2,1,0:T(8,128)S(1)}, f32[1,2,4,2,8,640]{5,4,3,2,1,0:T(8,128)S(1)}, u32[]{:S(2)}, u32[]{:S(2)}) %collective-permute-start.3) | collective-permute-done | bytes 327712 | tf_op jit(solution)/shard_map/ppermute | solution.py:79
  87.2 6.3 %collective-permute-start.4 = (f32[1,1,4,2,8,640]{5,4,3,2,1,0:T(8,128)S(1)}, f32[1,1,4,2,8,640]{5,4,3,2,1,0:T(8,128)S(1)}, u32[]{:S(2)}, u32[]{:S(2)}) collective-permute-start(f32[1,1,4,2,8,640]{5,4,3,2,1,0:T(8,128)S(1)} %constant_dynamic-slice_fusion.5), channel_id=1, source_target_pairs={{0,4},{1,5},{2,6},{3,7},{4,0},{5,1},{6,2},{7,3},{8,12},{9,13},{10,... | collective-permute-start | bytes 491528 | tf_op jit(solution)/shard_map/ppermute | solution.py:79
  93.7 7.9 %collective-permute-done.4 = f32[1,1,4,2,8,640]{5,4,3,2,1,0:T(8,128)S(1)} collective-permute-done((f32[1,1,4,2,8,640]{5,4,3,2,1,0:T(8,128)S(1)}, f32[1,1,4,2,8,640]{5,4,3,2,1,0:T(8,128)S(1)}, u32[]{:S(2)}, u32[]{:S(2)}) %collective-permute-start.4) | collective-permute-done | bytes 163872 | tf_op jit(solution)/shard_map/ppermute | solution.py:79
  103.3 1.9 %collective-permute-start.10 = (f32[1,2,1,2,8,640]{5,4,3,2,1,0:T(8,128)S(1)}, f32[1,2,1,2,8,640]{5,4,3,2,1,0:T(8,128)S(1)}, u32[]{:S(2)}, u32[]{:S(2)}) collective-permute-start(f32[1,2,1,2,8,640]{5,4,3,2,1,0:T(8,128)S(1)} %dynamic-slice_bitcast_fusion.5), channel_id=1, source_target_pairs={{0,2},{1,3},{2,0},{3,1},{4,6},{5,7},{6,4},{7,5},{8,10},{9,11},{10,... | collective-permute-start | bytes 245768 | tf_op jit(solution)/shard_map/ppermute | solution.py:79
  106.2 1.3 collective-permute-start.6
  107.5 2.1 %collective-permute-done.10 = f32[1,2,1,2,8,640]{5,4,3,2,1,0:T(8,128)S(1)} collective-permute-done((f32[1,2,1,2,8,640]{5,4,3,2,1,0:T(8,128)S(1)}, f32[1,2,1,2,8,640]{5,4,3,2,1,0:T(8,128)S(1)}, u32[]{:S(2)}, u32[]{:S(2)}) %collective-permute-start.10) | collective-permute-done | bytes 81952 | tf_op jit(solution)/shard_map/ppermute | solution.py:79
  109.6 2.8 %collective-permute-start.11 = (f32[1,1,1,2,8,640]{5,4,3,2,1,0:T(8,128)S(1)}, f32[1,1,1,2,8,640]{5,4,3,2,1,0:T(8,128)S(1)}, u32[]{:S(2)}, u32[]{:S(2)}) collective-permute-start(f32[1,1,1,2,8,640]{5,4,3,2,1,0:T(8,128)S(1)} %constant_dynamic-slice_fusion.2), channel_id=1, source_target_pairs={{0,4},{1,5},{2,6},{3,7},{4,0},{5,1},{6,2},{7,3},{8,12},{9,13},{10,... | collective-permute-start | bytes 122888 | tf_op jit(solution)/shard_map/ppermute | solution.py:79
  112.4 5.2 %collective-permute-done.11 = f32[1,1,1,2,8,640]{5,4,3,2,1,0:T(8,128)S(1)} collective-permute-done((f32[1,1,1,2,8,640]{5,4,3,2,1,0:T(8,128)S(1)}, f32[1,1,1,2,8,640]{5,4,3,2,1,0:T(8,128)S(1)}, u32[]{:S(2)}, u32[]{:S(2)}) %collective-permute-start.11) | collective-permute-done | bytes 40992 | tf_op jit(solution)/shard_map/ppermute | solution.py:79
  118.5 4.7 %collective-permute-done.12 = f32[1,1,1,1,8,1280]{5,4,3,2,1,0:T(8,128)S(1)} collective-permute-done((f32[1,1,1,1,8,1280]{5,4,3,2,1,0:T(8,128)S(1)}, f32[1,1,1,1,8,1280]{5,4,3,2,1,0:T(8,128)S(1)}, u32[]{:S(2)}, u32[]{:S(2)}) %collective-permute-start.12) | collective-permute-done | bytes 40992 | tf_op jit(solution)/shard_map/ppermute | solution.py:79
  123.2 1.6 %collective-permute-start.13 = (f32[1,1,1,1,1,4,1280]{6,5,4,3,2,1,0:T(4,128)S(1)}, f32[1,1,1,1,1,4,1280]{6,5,4,3,2,1,0:T(4,128)S(1)}, u32[]{:S(2)}, u32[]{:S(2)}) collective-permute-start(f32[1,1,1,1,1,4,1280]{6,5,4,3,2,1,0:T(4,128)S(1)} %dynamic-slice_bitcast_fusion.7), channel_id=1, source_target_pairs={{0,128},{128,0},{1,129},{129,1},{2,130},{130,2},{3,131},{131,3},{4... | collective-permute-start | bytes 61448 | tf_op jit(solution)/shard_map/ppermute | solution.py:79
  124.8 2.3 %collective-permute-done.13 = f32[1,1,1,1,1,4,1280]{6,5,4,3,2,1,0:T(4,128)S(1)} collective-permute-done((f32[1,1,1,1,1,4,1280]{6,5,4,3,2,1,0:T(4,128)S(1)}, f32[1,1,1,1,1,4,1280]{6,5,4,3,2,1,0:T(4,128)S(1)}, u32[]{:S(2)}, u32[]{:S(2)}) %collective-permute-start.13) | collective-permute-done | bytes 20512 | tf_op jit(solution)/shard_map/ppermute | solution.py:79
  127.1 3.7 %collective-permute-start.14 = (f32[1,1,1,1,1,4,1280]{6,5,4,3,2,1,0:T(4,128)S(1)}, f32[1,1,1,1,1,4,1280]{6,5,4,3,2,1,0:T(4,128)S(1)}, u32[]{:S(2)}, u32[]{:S(2)}) collective-permute-start(f32[1,1,1,1,1,4,1280]{6,5,4,3,2,1,0:T(4,128)S(1)} %bitcast_add_fusion.7), channel_id=1, source_target_pairs={{0,0},{1,64},{2,32},{3,96},{4,16},{5,80},{6,48},{7,112},{8,2},{9,6... | collective-permute-start | bytes 61448 | tf_op jit(solution)/shard_map/ppermute | solution.py:176
  130.8 9.0 %collective-permute-done.14 = f32[1,1,1,1,1,4,1280]{6,5,4,3,2,1,0:T(4,128)S(1)} collective-permute-done((f32[1,1,1,1,1,4,1280]{6,5,4,3,2,1,0:T(4,128)S(1)}, f32[1,1,1,1,1,4,1280]{6,5,4,3,2,1,0:T(4,128)S(1)}, u32[]{:S(2)}, u32[]{:S(2)}) %collective-permute-start.14) | collective-permute-done | bytes 20512 | tf_op jit(solution)/shard_map/ppermute | solution.py:176
  (113 shorter events, 38.0 us)
Async XLA Ops:
  0.6 2.5 %copy-start = (s32[1,8]{1,0:T(1,128)S(1)}, s32[1,8]{1,0:T(1,128)}, u32[]{:S(2)}) copy-start(s32[1,8]{1,0:T(1,128)} %param.9) | copy-start | bytes 100
  0.6 3.3 %collective-permute-start = (f32[1,1024]{1,0:T(1,128)}, f32[1,1024]{1,0:T(1,128)S(1)}, u32[]{:S(2)}, u32[]{:S(2)}) collective-permute-start(f32[1,1024]{1,0:T(1,128)} %param.7), channel_id=1, source_target_pairs={{0,64},{64,128},{128,192},{1,65},{65,129},{129,193},{2,66},{66,130... | collective-permute-start | bytes 12296 | tf_op jit(solution)/shard_map/ppermute | solution.py:54
  7.3 1.1 copy-start.4
  7.4 1.1 copy-start.5
  8.2 1.8 %copy-start.3 = (bf16[10,256,512]{2,1,0:T(8,128)(2,1)S(1)}, bf16[10,256,512]{2,1,0:T(8,128)(2,1)}, u32[]{:S(2)}) copy-start(bf16[10,256,512]{2,1,0:T(8,128)(2,1)} %param.11) | copy-start | bytes 7864324
  26.5 2.2 %slice-start = ((s8[5242880]{0:T(1024)(128)(4,1)}), s8[4194304]{0:T(1024)(128)(4,1)S(1)}, s32[]{:S(2)}) async-start(s8[5242880]{0:T(1024)(128)(4,1)} %bitcast.144), calls=%async_computation | async-start | bytes 8388608
  27.6 1.7 %slice-start.1 = ((s8[5242880]{0:T(1024)(128)(4,1)}), s8[1048576]{0:T(1024)(128)(4,1)S(1)}, s32[]{:S(2)}) async-start(s8[5242880]{0:T(1024)(128)(4,1)} %bitcast.144), calls=%async_computation.1 | async-start | bytes 2097152
  38.8 3.1 %copy-start.2 = (f32[1024,1280]{1,0:T(8,128)}, f32[1024,1280]{1,0:T(8,128)S(1)}, u32[]{:S(2)}) copy-start(f32[1024,1280]{1,0:T(8,128)S(1)} %fusion.1) | copy-start | bytes 15728644
  41.9 6.2 %collective-permute-start.1 = (f32[1,8,4,2,8,1280]{5,4,3,2,1,0:T(8,128)}, f32[1,8,4,2,8,1280]{5,4,3,2,1,0:T(8,128)S(1)}, u32[]{:S(2)}, u32[]{:S(2)}) collective-permute-start(f32[1,8,4,2,8,1280]{5,4,3,2,1,0:T(8,128)} %dynamic-slice_bitcast_fusion), channel_id=1, source_target_pairs={{0,64},{64,0},{1,65},{65,1},{2,66},{66,2},{3,67},{67,3},{4,68},{68... | collective-permute-start | bytes 7864328 | tf_op jit(solution)/shard_map/ppermute | solution.py:79
  51.6 17.4 %collective-permute-start.2 = (f32[1,4,4,2,8,640]{5,4,3,2,1,0:T(8,128)}, f32[1,4,4,2,8,640]{5,4,3,2,1,0:T(8,128)S(1)}, u32[]{:S(2)}, u32[]{:S(2)}) collective-permute-start(f32[1,4,4,2,8,640]{5,4,3,2,1,0:T(8,128)} %dynamic-slice_bitcast_fusion.2), channel_id=1, source_target_pairs={{0,1},{1,0},{2,3},{3,2},{4,5},{5,4},{6,7},{7,6},{8,9},{9,8},{10,11... | collective-permute-start | bytes 1966088 | tf_op jit(solution)/shard_map/ppermute | solution.py:79
  54.4 18.0 %collective-permute-start.7 = (f32[1,8,2,2,8,640]{5,4,3,2,1,0:T(8,128)}, f32[1,8,2,2,8,640]{5,4,3,2,1,0:T(8,128)}, u32[]{:S(2)}, u32[]{:S(2)}) collective-permute-start(f32[1,8,2,2,8,640]{5,4,3,2,1,0:T(8,128)} %dynamic-slice_bitcast_fusion.1), channel_id=1, source_target_pairs={{0,16},{16,0},{32,48},{48,32},{1,17},{17,1},{33,49},{49,33},{2,18}... | collective-permute-start | bytes 1966088 | tf_op jit(solution)/shard_map/ppermute | solution.py:79
  69.1 18.1 %collective-permute-start.3 = (f32[1,2,4,2,8,640]{5,4,3,2,1,0:T(8,128)S(1)}, f32[1,2,4,2,8,640]{5,4,3,2,1,0:T(8,128)S(1)}, u32[]{:S(2)}, u32[]{:S(2)}) collective-permute-start(f32[1,2,4,2,8,640]{5,4,3,2,1,0:T(8,128)S(1)} %dynamic-slice_bitcast_fusion.3), channel_id=1, source_target_pairs={{0,2},{1,3},{2,0},{3,1},{4,6},{5,7},{6,4},{7,5},{8,10},{9,11},{10,... | collective-permute-start | bytes 983048 | tf_op jit(solution)/shard_map/ppermute | solution.py:79
  73.7 19.8 %collective-permute-start.8 = (f32[1,8,1,2,8,640]{5,4,3,2,1,0:T(8,128)S(1)}, f32[1,8,1,2,8,640]{5,4,3,2,1,0:T(8,128)S(1)}, u32[]{:S(2)}, u32[]{:S(2)}) collective-permute-start(f32[1,8,1,2,8,640]{5,4,3,2,1,0:T(8,128)S(1)} %constant_dynamic-slice_fusion.3), channel_id=1, source_target_pairs={{0,32},{16,48},{32,0},{48,16},{1,33},{17,49},{33,1},{49,17},{2,34}... | collective-permute-start | bytes 983048 | tf_op jit(solution)/shard_map/ppermute | solution.py:79
  87.2 56.5 %copy-start.1 = (s32[1,8]{1,0:T(1,128)S(1)}, s32[1,8]{1,0:T(1,128)}, u32[]{:S(2)}) copy-start(s32[1,8]{1,0:T(1,128)} %param.9) | copy-start | bytes 100
  87.2 14.3 %collective-permute-start.4 = (f32[1,1,4,2,8,640]{5,4,3,2,1,0:T(8,128)S(1)}, f32[1,1,4,2,8,640]{5,4,3,2,1,0:T(8,128)S(1)}, u32[]{:S(2)}, u32[]{:S(2)}) collective-permute-start(f32[1,1,4,2,8,640]{5,4,3,2,1,0:T(8,128)S(1)} %constant_dynamic-slice_fusion.5), channel_id=1, source_target_pairs={{0,4},{1,5},{2,6},{3,7},{4,0},{5,1},{6,2},{7,3},{8,12},{9,13},{10,... | collective-permute-start | bytes 491528 | tf_op jit(solution)/shard_map/ppermute | solution.py:79
  93.6 9.7 %collective-permute-start.9 = (f32[1,4,1,2,8,640]{5,4,3,1,2,0:T(8,128)S(1)}, f32[1,4,1,2,8,640]{5,4,3,1,2,0:T(8,128)S(1)}, u32[]{:S(2)}, u32[]{:S(2)}) collective-permute-start(f32[1,4,1,2,8,640]{5,4,3,1,2,0:T(8,128)S(1)} %dynamic-slice_bitcast_fusion.4), channel_id=1, source_target_pairs={{0,1},{1,0},{2,3},{3,2},{4,5},{5,4},{6,7},{7,6},{8,9},{9,8},{10,11... | collective-permute-start | bytes 491528 | tf_op jit(solution)/shard_map/ppermute | solution.py:79
  101.6 4.5 %collective-permute-start.5 = (f32[1,1,2,2,8,640]{5,4,3,2,1,0:T(8,128)S(1)}, f32[1,1,2,2,8,640]{5,4,3,2,1,0:T(8,128)S(1)}, u32[]{:S(2)}, u32[]{:S(2)}) collective-permute-start(f32[1,1,2,2,8,640]{5,4,3,2,1,0:T(8,128)S(1)} %dynamic-slice_bitcast_fusion.6), channel_id=1, source_target_pairs={{0,16},{16,0},{32,48},{48,32},{1,17},{17,1},{33,49},{49,33},{2,18}... | collective-permute-start | bytes 245768 | tf_op jit(solution)/shard_map/ppermute | solution.py:79
  103.3 6.2 %collective-permute-start.10 = (f32[1,2,1,2,8,640]{5,4,3,2,1,0:T(8,128)S(1)}, f32[1,2,1,2,8,640]{5,4,3,2,1,0:T(8,128)S(1)}, u32[]{:S(2)}, u32[]{:S(2)}) collective-permute-start(f32[1,2,1,2,8,640]{5,4,3,2,1,0:T(8,128)S(1)} %dynamic-slice_bitcast_fusion.5), channel_id=1, source_target_pairs={{0,2},{1,3},{2,0},{3,1},{4,6},{5,7},{6,4},{7,5},{8,10},{9,11},{10,... | collective-permute-start | bytes 245768 | tf_op jit(solution)/shard_map/ppermute | solution.py:79
  106.2 6.2 %collective-permute-start.6 = (f32[1,1,1,2,8,640]{5,4,3,2,1,0:T(8,128)S(1)}, f32[1,1,1,2,8,640]{5,4,3,2,1,0:T(8,128)S(1)}, u32[]{:S(2)}, u32[]{:S(2)}) collective-permute-start(f32[1,1,1,2,8,640]{5,4,3,2,1,0:T(8,128)S(1)} %constant_dynamic-slice_fusion.4), channel_id=1, source_target_pairs={{0,32},{16,48},{32,0},{48,16},{1,33},{17,49},{33,1},{49,17},{2,34}... | collective-permute-start | bytes 122888 | tf_op jit(solution)/shard_map/ppermute | solution.py:79
  109.6 8.0 %collective-permute-start.11 = (f32[1,1,1,2,8,640]{5,4,3,2,1,0:T(8,128)S(1)}, f32[1,1,1,2,8,640]{5,4,3,2,1,0:T(8,128)S(1)}, u32[]{:S(2)}, u32[]{:S(2)}) collective-permute-start(f32[1,1,1,2,8,640]{5,4,3,2,1,0:T(8,128)S(1)} %constant_dynamic-slice_fusion.2), channel_id=1, source_target_pairs={{0,4},{1,5},{2,6},{3,7},{4,0},{5,1},{6,2},{7,3},{8,12},{9,13},{10,... | collective-permute-start | bytes 122888 | tf_op jit(solution)/shard_map/ppermute | solution.py:79
  117.6 5.6 %collective-permute-start.12 = (f32[1,1,1,1,8,1280]{5,4,3,2,1,0:T(8,128)S(1)}, f32[1,1,1,1,8,1280]{5,4,3,2,1,0:T(8,128)S(1)}, u32[]{:S(2)}, u32[]{:S(2)}) collective-permute-start(f32[1,1,1,1,8,1280]{5,4,3,2,1,0:T(8,128)S(1)} %fusion.165), channel_id=1, source_target_pairs={{0,8},{8,0},{1,9},{9,1},{2,10},{10,2},{3,11},{11,3},{4,12},{12,4},... | collective-permute-start | bytes 122888 | tf_op jit(solution)/shard_map/ppermute | solution.py:79
  123.2 3.9 %collective-permute-start.13 = (f32[1,1,1,1,1,4,1280]{6,5,4,3,2,1,0:T(4,128)S(1)}, f32[1,1,1,1,1,4,1280]{6,5,4,3,2,1,0:T(4,128)S(1)}, u32[]{:S(2)}, u32[]{:S(2)}) collective-permute-start(f32[1,1,1,1,1,4,1280]{6,5,4,3,2,1,0:T(4,128)S(1)} %dynamic-slice_bitcast_fusion.7), channel_id=1, source_target_pairs={{0,128},{128,0},{1,129},{129,1},{2,130},{130,2},{3,131},{131,3},{4... | collective-permute-start | bytes 61448 | tf_op jit(solution)/shard_map/ppermute | solution.py:79
  127.1 12.7 %collective-permute-start.14 = (f32[1,1,1,1,1,4,1280]{6,5,4,3,2,1,0:T(4,128)S(1)}, f32[1,1,1,1,1,4,1280]{6,5,4,3,2,1,0:T(4,128)S(1)}, u32[]{:S(2)}, u32[]{:S(2)}) collective-permute-start(f32[1,1,1,1,1,4,1280]{6,5,4,3,2,1,0:T(4,128)S(1)} %bitcast_add_fusion.7), channel_id=1, source_target_pairs={{0,0},{1,64},{2,32},{3,96},{4,16},{5,80},{6,48},{7,112},{8,2},{9,6... | collective-permute-start | bytes 61448 | tf_op jit(solution)/shard_map/ppermute | solution.py:176

commit v10 on v9

--- a/solution.py
+++ b/solution.py
@@ -24,19 +24,22 @@
     return value
 
 
-def owner_pairs(sizes):
+def owner_pairs(sizes, flip=None):
     import itertools
 
     pairs = []
     for digits in itertools.product(*(range(sizes[n]) for n in FINE)):
         index = dict(zip(FINE, digits))
+        source = linear(index, FINE, sizes)
+        if flip is not None:
+            index[flip] = sizes[flip] - 1 - index[flip]
         block = 0
         for group in GROUPS:
             size = 1
             for name in group:
                 size *= sizes[name]
             block = block * size + reverse_bits(linear(index, group, sizes), size)
-        pairs.append((linear(index, FINE, sizes), block))
+        pairs.append((source, block))
     return pairs
 
 
@@ -172,8 +175,12 @@
     slab = jnp.concatenate([left, right], -1)
     slab = exchange_scatter(slab, "xh", 3)
     slab = slab.reshape(tuple(slab.shape[:-2]) + (group_sizes[-1], row_count, width))
-    slab = exchange_scatter(slab, "xl", 4)
-    slab = lax.ppermute(slab, FINE, owner_pairs(sizes))
+    side = lax.axis_index("xl")
+    mine = lax.dynamic_index_in_dim(slab, side, 4, keepdims=True)
+    other = lax.dynamic_index_in_dim(slab, 1 - side, 4, keepdims=True)
+    slab = lax.ppermute(mine, FINE, owner_pairs(sizes)) + lax.ppermute(
+        other, FINE, owner_pairs(sizes, flip="xl")
+    )
     owned_rows = slab.reshape(row_count, width)
     first_col = lax.axis_index(FINE) * row_count
     valid_total = lax.dynamic_slice(owned_rows, (1, first_col), (1, 1))[0, 0]

time: 144 us -> 145 us (level)
  the two profiles are of different devices: /device:TPU:28 before, /device:TPU:24 now
where the time goes in v10:
time: 145 us; the launch traced here: 144 us
  waiting for transfers between devices  59.3 us (41%)
  starting transfers between devices  34.9 us (24%)
  matrix products  22.2 us (15%)
  other arithmetic  16.2 us (11%)
  local copies, waits for them, and re-layouts  9.17 us (6%)
  between operations  2.6 us (2%)
    ppermute x12, waiting for transfers between devices, exchange_scatter(): slab = mine + lax.ppermute(other, axis, pairs)  50.4 us
    ppermute x12, starting transfers between devices, exchange_scatter(): slab = mine + lax.ppermute(other, axis, pairs)  25.1 us
    dot_general x10, matrix products, layer_math(): preact = jnp.dot(paired, conv_one, preferred_element_type=jnp.float32)  8.25 us
    ppermute x1, starting transfers between devices, per_device(): lax.ppermute(mine, FINE, owner_pairs(sizes))  7.93 us
    convert_element_type x9, other arithmetic, layer_math(): (jnp.tanh(preact[:, :gate_width]) * jax.nn.sigmoid(preact[:, gate_width:]...  7.06 us
    ppermute x1, waiting for transfers between devices, per_device(): lax.ppermute(other, FINE, owner_pairs(sizes, flip='xl'))  7.02 us
    dot_general x1, matrix products, per_device(): skip_sum = jnp.dot(stacked, skip_weight, preferred_element_type=jnp.float32)  5.88 us
    dot_general x9, matrix products, layer_math(): residual_term = jnp.dot(gated, res_one, preferred_element_type=jnp.float32)  4.43 us
  transfers between devices with their start and end apart: 15, of which 11 were waited for; matrix products, arithmetic and copies ran while one was open for 2% of the time, Pallas kernels for 0%

profile of v10, /device:TPU:24, one launch (start us, length us, event | category | flops | bytes accessed | tf_op | source)
XLA Modules:
  0.0 144.3 jit_solution(11377465624023886400)
XLA Ops:
  0.6 1.7 %collective-permute-start = (f32[1,1024]{1,0:T(1,128)}, f32[1,1024]{1,0:T(1,128)S(1)}, u32[]{:S(2)}, u32[]{:S(2)}) collective-permute-start(f32[1,1024]{1,0:T(1,128)} %param.7), channel_id=1, source_target_pairs={{0,64},{64,128},{128,192},{1,65},{65,129},{129,193},{2,66},{66,130... | collective-permute-start | bytes 12296 | tf_op jit(solution)/shard_map/ppermute | solution.py:57
  5.6 1.7 %fusion.72 = f32[2048,512]{0,1:T(8,128)S(1)} fusion(bf16[2047,128]{1,0:T(8,128)(2,1)S(1)} %bitcast.128, bf16[2048,128]{1,0:T(8,128)(2,1)S(1)} %multiply_convert_fusion, bf16[10,256,512]{2,1,0:T(8,128)(2,1)} %param.11), kind=kOutput, calls=%fused_computation.106 | convolution fusion | flops 540016640 | bytes 5504768 | tf_op jit(solution)/shard_map/dot_general | solution.py:94
  29.2 5.9 %broadcast_select_fusion = bf16[1024,1024]{0,1:T(8,128)(2,1)S(1)} fusion(pred[1024]{0:T(1024)(128)(4,1)S(1)} %add_compare_fusion, bf16[1024,2560]{0,1:T(8,128)(2,1)S(1)} %fusion.119, bf16[2560,1024]{1,0:T(8,128)(2,1)S(1)} %bitcast.141), kind=kOutput, calls=%fused_computation.83 | convolution fusion | flops 5371854848 | bytes 12583936 | tf_op jit(solution)/shard_map/dot_general | solution.py:136
  35.1 3.7 %fusion.1 = f32[1024,1280]{1,0:T(8,128)S(1)} fusion(bf16[1024,1024]{0,1:T(8,128)(2,1)S(1)} %broadcast_select_fusion, bf16[1024,256]{0,1:T(8,128)(2,1)S(1)} %fusion.94, f32[]{:T(128)} %convert_reduce_fusion, s32[1024]{0:T(1024)S(1)} %get-tuple-element.22, s32[1024]{0:T(1024)S(1)} %get-tuple-element.23, s32[1024]{0:T(1024)S(1)} %fusion.168, ...), kind=kOutput, calls=%fused_computation.3 | convolution fusion | flops 2696151040 | bytes 7877636 | tf_op jit(solution)/shard_map/dot_general | solution.py:147
  38.8 1.8 %dynamic-slice_bitcast_fusion = f32[1,8,4,2,8,1280]{5,4,3,2,1,0:T(8,128)} fusion(f32[2,1,8,4,2,8,1280]{6,5,4,3,2,0,1:T(8,128)S(1)} %bitcast.126, s32[]{:T(128)S(6)} %select_n.217), kind=kLoop, calls=%fused_computation.9 | loop fusion | bytes 5242884 | tf_op jit(solution)/shard_map/jit(dynamic_index_in_dim)/squeeze | solution.py:79
  41.9 1.8 %collective-permute-start.1 = (f32[1,8,4,2,8,1280]{5,4,3,2,1,0:T(8,128)}, f32[1,8,4,2,8,1280]{5,4,3,2,1,0:T(8,128)S(1)}, u32[]{:S(2)}, u32[]{:S(2)}) collective-permute-start(f32[1,8,4,2,8,1280]{5,4,3,2,1,0:T(8,128)} %dynamic-slice_bitcast_fusion), channel_id=1, source_target_pairs={{0,64},{64,0},{1,65},{65,1},{2,66},{66,2},{3,67},{67,3},{4,68},{68... | collective-permute-start | bytes 7864328 | tf_op jit(solution)/shard_map/ppermute | solution.py:82
  43.7 4.7 %collective-permute-done.1 = f32[1,8,4,2,8,1280]{5,4,3,2,1,0:T(8,128)S(1)} collective-permute-done((f32[1,8,4,2,8,1280]{5,4,3,2,1,0:T(8,128)}, f32[1,8,4,2,8,1280]{5,4,3,2,1,0:T(8,128)S(1)}, u32[]{:S(2)}, u32[]{:S(2)}) %collective-permute-start.1) | collective-permute-done | bytes 2621472 | tf_op jit(solution)/shard_map/ppermute | solution.py:82
  48.4 2.2 %bitcast_add_fusion = f32[1,8,4,2,8,1280]{5,4,3,2,1,0:T(8,128)S(1)} fusion(f32[1,8,4,2,8,1280]{5,4,3,2,1,0:T(8,128)S(1)} %collective-permute-done.1, f32[2,1,8,4,2,8,1280]{6,5,4,3,2,0,1:T(8,128)} %bitcast.127, s32[]{:T(128)S(6)} %select_n.216), kind=kLoop, calls=%fused_computation.8 | loop fusion | flops 655360 | bytes 7864324 | tf_op jit(solution)/shard_map/add | solution.py:82
  51.8 1.9 %collective-permute-start.2 = (f32[1,4,4,2,8,640]{5,4,3,2,1,0:T(8,128)}, f32[1,4,4,2,8,640]{5,4,3,2,1,0:T(8,128)S(1)}, u32[]{:S(2)}, u32[]{:S(2)}) collective-permute-start(f32[1,4,4,2,8,640]{5,4,3,2,1,0:T(8,128)} %dynamic-slice_bitcast_fusion.2), channel_id=1, source_target_pairs={{0,1},{1,0},{2,3},{3,2},{4,5},{5,4},{6,7},{7,6},{8,9},{9,8},{10,11... | collective-permute-start | bytes 1966088 | tf_op jit(solution)/shard_map/ppermute | solution.py:82
  55.4 13.8 %collective-permute-done.2 = f32[1,4,4,2,8,640]{5,4,3,2,1,0:T(8,128)S(1)} collective-permute-done((f32[1,4,4,2,8,640]{5,4,3,2,1,0:T(8,128)}, f32[1,4,4,2,8,640]{5,4,3,2,1,0:T(8,128)S(1)}, u32[]{:S(2)}, u32[]{:S(2)}) %collective-permute-start.2) | collective-permute-done | bytes 655392 | tf_op jit(solution)/shard_map/ppermute | solution.py:82
  69.4 3.4 %collective-permute-start.3 = (f32[1,2,4,2,8,640]{5,4,3,2,1,0:T(8,128)S(1)}, f32[1,2,4,2,8,640]{5,4,3,2,1,0:T(8,128)S(1)}, u32[]{:S(2)}, u32[]{:S(2)}) collective-permute-start(f32[1,2,4,2,8,640]{5,4,3,2,1,0:T(8,128)S(1)} %dynamic-slice_bitcast_fusion.3), channel_id=1, source_target_pairs={{0,2},{1,3},{2,0},{3,1},{4,6},{5,7},{6,4},{7,5},{8,10},{9,11},{10,... | collective-permute-start | bytes 983048 | tf_op jit(solution)/shard_map/ppermute | solution.py:82
  74.0 1.3 collective-permute-start.8
  75.3 12.1 %collective-permute-done.3 = f32[1,2,4,2,8,640]{5,4,3,2,1,0:T(8,128)S(1)} collective-permute-done((f32[1,2,4,2,8,640]{5,4,3,2,1,0:T(8,128)S(1)}, f32[1,2,4,2,8,640]{5,4,3,2,1,0:T(8,128)S(1)}, u32[]{:S(2)}, u32[]{:S(2)}) %collective-permute-start.3) | collective-permute-done | bytes 327712 | tf_op jit(solution)/shard_map/ppermute | solution.py:82
  87.5 6.3 %collective-permute-start.4 = (f32[1,1,4,2,8,640]{5,4,3,2,1,0:T(8,128)S(1)}, f32[1,1,4,2,8,640]{5,4,3,2,1,0:T(8,128)S(1)}, u32[]{:S(2)}, u32[]{:S(2)}) collective-permute-start(f32[1,1,4,2,8,640]{5,4,3,2,1,0:T(8,128)S(1)} %constant_dynamic-slice_fusion.7), channel_id=1, source_target_pairs={{0,4},{1,5},{2,6},{3,7},{4,0},{5,1},{6,2},{7,3},{8,12},{9,13},{10,... | collective-permute-start | bytes 491528 | tf_op jit(solution)/shard_map/ppermute | solution.py:82
  94.0 7.9 %collective-permute-done.4 = f32[1,1,4,2,8,640]{5,4,3,2,1,0:T(8,128)S(1)} collective-permute-done((f32[1,1,4,2,8,640]{5,4,3,2,1,0:T(8,128)S(1)}, f32[1,1,4,2,8,640]{5,4,3,2,1,0:T(8,128)S(1)}, u32[]{:S(2)}, u32[]{:S(2)}) %collective-permute-start.4) | collective-permute-done | bytes 163872 | tf_op jit(solution)/shard_map/ppermute | solution.py:82
  103.6 1.9 %collective-permute-start.10 = (f32[1,2,1,2,8,640]{5,4,3,2,1,0:T(8,128)S(1)}, f32[1,2,1,2,8,640]{5,4,3,2,1,0:T(8,128)S(1)}, u32[]{:S(2)}, u32[]{:S(2)}) collective-permute-start(f32[1,2,1,2,8,640]{5,4,3,2,1,0:T(8,128)S(1)} %dynamic-slice_bitcast_fusion.5), channel_id=1, source_target_pairs={{0,2},{1,3},{2,0},{3,1},{4,6},{5,7},{6,4},{7,5},{8,10},{9,11},{10,... | collective-permute-start | bytes 245768 | tf_op jit(solution)/shard_map/ppermute | solution.py:82
  107.7 2.1 %collective-permute-done.10 = f32[1,2,1,2,8,640]{5,4,3,2,1,0:T(8,128)S(1)} collective-permute-done((f32[1,2,1,2,8,640]{5,4,3,2,1,0:T(8,128)S(1)}, f32[1,2,1,2,8,640]{5,4,3,2,1,0:T(8,128)S(1)}, u32[]{:S(2)}, u32[]{:S(2)}) %collective-permute-start.10) | collective-permute-done | bytes 81952 | tf_op jit(solution)/shard_map/ppermute | solution.py:82
  109.9 2.8 %collective-permute-start.11 = (f32[1,1,1,2,8,640]{5,4,3,2,1,0:T(8,128)S(1)}, f32[1,1,1,2,8,640]{5,4,3,2,1,0:T(8,128)S(1)}, u32[]{:S(2)}, u32[]{:S(2)}) collective-permute-start(f32[1,1,1,2,8,640]{5,4,3,2,1,0:T(8,128)S(1)} %constant_dynamic-slice_fusion.4), channel_id=1, source_target_pairs={{0,4},{1,5},{2,6},{3,7},{4,0},{5,1},{6,2},{7,3},{8,12},{9,13},{10,... | collective-permute-start | bytes 122888 | tf_op jit(solution)/shard_map/ppermute | solution.py:82
  112.7 5.2 %collective-permute-done.11 = f32[1,1,1,2,8,640]{5,4,3,2,1,0:T(8,128)S(1)} collective-permute-done((f32[1,1,1,2,8,640]{5,4,3,2,1,0:T(8,128)S(1)}, f32[1,1,1,2,8,640]{5,4,3,2,1,0:T(8,128)S(1)}, u32[]{:S(2)}, u32[]{:S(2)}) %collective-permute-start.11) | collective-permute-done | bytes 40992 | tf_op jit(solution)/shard_map/ppermute | solution.py:82
  117.9 2.8 %collective-permute-start.12 = (f32[1,1,1,1,8,1280]{5,4,3,2,1,0:T(8,128)S(1)}, f32[1,1,1,1,8,1280]{5,4,3,2,1,0:T(8,128)S(1)}, u32[]{:S(2)}, u32[]{:S(2)}) collective-permute-start(f32[1,1,1,1,8,1280]{5,4,3,2,1,0:T(8,128)S(1)} %fusion.165), channel_id=1, source_target_pairs={{0,8},{8,0},{1,9},{9,1},{2,10},{10,2},{3,11},{11,3},{4,12},{12,4},... | collective-permute-start | bytes 122888 | tf_op jit(solution)/shard_map/ppermute | solution.py:82
  120.7 2.8 %collective-permute-done.12 = f32[1,1,1,1,8,1280]{5,4,3,2,1,0:T(8,128)S(1)} collective-permute-done((f32[1,1,1,1,8,1280]{5,4,3,2,1,0:T(8,128)S(1)}, f32[1,1,1,1,8,1280]{5,4,3,2,1,0:T(8,128)S(1)}, u32[]{:S(2)}, u32[]{:S(2)}) %collective-permute-start.12) | collective-permute-done | bytes 40992 | tf_op jit(solution)/shard_map/ppermute | solution.py:82
  123.5 7.9 %collective-permute-start.13 = (f32[1,1,1,1,1,4,1280]{6,5,4,3,2,1,0:T(4,128)S(1)}, f32[1,1,1,1,1,4,1280]{6,5,4,3,2,1,0:T(4,128)S(1)}, u32[]{:S(2)}, u32[]{:S(2)}) collective-permute-start(f32[1,1,1,1,1,4,1280]{6,5,4,3,2,1,0:T(4,128)S(1)} %get-tuple-element.19), channel_id=1, source_target_pairs={{0,0},{1,64},{2,32},{3,96},{4,16},{5,80},{6,48},{7,112},{8,2},{9,6... | collective-permute-start | bytes 61448 | tf_op jit(solution)/shard_map/ppermute | solution.py:181
  131.6 1.9 %collective-permute-done.13 = f32[1,1,1,1,1,4,1280]{6,5,4,3,2,1,0:T(4,128)S(1)} collective-permute-done((f32[1,1,1,1,1,4,1280]{6,5,4,3,2,1,0:T(4,128)S(1)}, f32[1,1,1,1,1,4,1280]{6,5,4,3,2,1,0:T(4,128)S(1)}, u32[]{:S(2)}, u32[]{:S(2)}) %collective-permute-start.13) | collective-permute-done | bytes 20512 | tf_op jit(solution)/shard_map/ppermute | solution.py:181
  133.4 7.0 %collective-permute-done.14 = f32[1,1,1,1,1,4,1280]{6,5,4,3,2,1,0:T(4,128)S(1)} collective-permute-done((f32[1,1,1,1,1,4,1280]{6,5,4,3,2,1,0:T(4,128)S(1)}, f32[1,1,1,1,1,4,1280]{6,5,4,3,2,1,0:T(4,128)S(1)}, u32[]{:S(2)}, u32[]{:S(2)}) %collective-permute-start.14) | collective-permute-done | bytes 20512 | tf_op jit(solution)/shard_map/ppermute | solution.py:181
  (113 shorter events, 37.2 us)
Async XLA Ops:
  0.6 2.5 %copy-start = (s32[1,8]{1,0:T(1,128)S(1)}, s32[1,8]{1,0:T(1,128)}, u32[]{:S(2)}) copy-start(s32[1,8]{1,0:T(1,128)} %param.9) | copy-start | bytes 100
  0.6 3.3 %collective-permute-start = (f32[1,1024]{1,0:T(1,128)}, f32[1,1024]{1,0:T(1,128)S(1)}, u32[]{:S(2)}, u32[]{:S(2)}) collective-permute-start(f32[1,1024]{1,0:T(1,128)} %param.7), channel_id=1, source_target_pairs={{0,64},{64,128},{128,192},{1,65},{65,129},{129,193},{2,66},{66,130... | collective-permute-start | bytes 12296 | tf_op jit(solution)/shard_map/ppermute | solution.py:57
  7.3 1.1 copy-start.4
  7.4 1.1 copy-start.5
  8.2 1.8 %copy-start.3 = (bf16[10,256,512]{2,1,0:T(8,128)(2,1)S(1)}, bf16[10,256,512]{2,1,0:T(8,128)(2,1)}, u32[]{:S(2)}) copy-start(bf16[10,256,512]{2,1,0:T(8,128)(2,1)} %param.11) | copy-start | bytes 7864324
  26.5 2.2 %slice-start = ((s8[5242880]{0:T(1024)(128)(4,1)}), s8[4194304]{0:T(1024)(128)(4,1)S(1)}, s32[]{:S(2)}) async-start(s8[5242880]{0:T(1024)(128)(4,1)} %bitcast.140), calls=%async_computation | async-start | bytes 8388608
  27.6 1.7 %slice-start.1 = ((s8[5242880]{0:T(1024)(128)(4,1)}), s8[1048576]{0:T(1024)(128)(4,1)S(1)}, s32[]{:S(2)}) async-start(s8[5242880]{0:T(1024)(128)(4,1)} %bitcast.140), calls=%async_computation.1 | async-start | bytes 2097152
  38.8 3.1 %copy-start.2 = (f32[1024,1280]{1,0:T(8,128)}, f32[1024,1280]{1,0:T(8,128)S(1)}, u32[]{:S(2)}) copy-start(f32[1024,1280]{1,0:T(8,128)S(1)} %fusion.1) | copy-start | bytes 15728644
  41.9 6.5 %collective-permute-start.1 = (f32[1,8,4,2,8,1280]{5,4,3,2,1,0:T(8,128)}, f32[1,8,4,2,8,1280]{5,4,3,2,1,0:T(8,128)S(1)}, u32[]{:S(2)}, u32[]{:S(2)}) collective-permute-start(f32[1,8,4,2,8,1280]{5,4,3,2,1,0:T(8,128)} %dynamic-slice_bitcast_fusion), channel_id=1, source_target_pairs={{0,64},{64,0},{1,65},{65,1},{2,66},{66,2},{3,67},{67,3},{4,68},{68... | collective-permute-start | bytes 7864328 | tf_op jit(solution)/shard_map/ppermute | solution.py:82
  51.8 17.4 %collective-permute-start.2 = (f32[1,4,4,2,8,640]{5,4,3,2,1,0:T(8,128)}, f32[1,4,4,2,8,640]{5,4,3,2,1,0:T(8,128)S(1)}, u32[]{:S(2)}, u32[]{:S(2)}) collective-permute-start(f32[1,4,4,2,8,640]{5,4,3,2,1,0:T(8,128)} %dynamic-slice_bitcast_fusion.2), channel_id=1, source_target_pairs={{0,1},{1,0},{2,3},{3,2},{4,5},{5,4},{6,7},{7,6},{8,9},{9,8},{10,11... | collective-permute-start | bytes 1966088 | tf_op jit(solution)/shard_map/ppermute | solution.py:82
  54.7 18.0 %collective-permute-start.7 = (f32[1,8,2,2,8,640]{5,4,3,2,1,0:T(8,128)}, f32[1,8,2,2,8,640]{5,4,3,2,1,0:T(8,128)}, u32[]{:S(2)}, u32[]{:S(2)}) collective-permute-start(f32[1,8,2,2,8,640]{5,4,3,2,1,0:T(8,128)} %dynamic-slice_bitcast_fusion.1), channel_id=1, source_target_pairs={{0,16},{16,0},{32,48},{48,32},{1,17},{17,1},{33,49},{49,33},{2,18}... | collective-permute-start | bytes 1966088 | tf_op jit(solution)/shard_map/ppermute | solution.py:82
  69.4 18.0 %collective-permute-start.3 = (f32[1,2,4,2,8,640]{5,4,3,2,1,0:T(8,128)S(1)}, f32[1,2,4,2,8,640]{5,4,3,2,1,0:T(8,128)S(1)}, u32[]{:S(2)}, u32[]{:S(2)}) collective-permute-start(f32[1,2,4,2,8,640]{5,4,3,2,1,0:T(8,128)S(1)} %dynamic-slice_bitcast_fusion.3), channel_id=1, source_target_pairs={{0,2},{1,3},{2,0},{3,1},{4,6},{5,7},{6,4},{7,5},{8,10},{9,11},{10,... | collective-permute-start | bytes 983048 | tf_op jit(solution)/shard_map/ppermute | solution.py:82
  74.0 19.8 %collective-permute-start.8 = (f32[1,8,1,2,8,640]{5,4,3,2,1,0:T(8,128)S(1)}, f32[1,8,1,2,8,640]{5,4,3,2,1,0:T(8,128)S(1)}, u32[]{:S(2)}, u32[]{:S(2)}) collective-permute-start(f32[1,8,1,2,8,640]{5,4,3,2,1,0:T(8,128)S(1)} %constant_dynamic-slice_fusion.5), channel_id=1, source_target_pairs={{0,32},{16,48},{32,0},{48,16},{1,33},{17,49},{33,1},{49,17},{2,34}... | collective-permute-start | bytes 983048 | tf_op jit(solution)/shard_map/ppermute | solution.py:82
  87.4 56.9 %copy-start.1 = (s32[1,8]{1,0:T(1,128)S(1)}, s32[1,8]{1,0:T(1,128)}, u32[]{:S(2)}) copy-start(s32[1,8]{1,0:T(1,128)} %param.9) | copy-start | bytes 100
  87.5 14.3 %collective-permute-start.4 = (f32[1,1,4,2,8,640]{5,4,3,2,1,0:T(8,128)S(1)}, f32[1,1,4,2,8,640]{5,4,3,2,1,0:T(8,128)S(1)}, u32[]{:S(2)}, u32[]{:S(2)}) collective-permute-start(f32[1,1,4,2,8,640]{5,4,3,2,1,0:T(8,128)S(1)} %constant_dynamic-slice_fusion.7), channel_id=1, source_target_pairs={{0,4},{1,5},{2,6},{3,7},{4,0},{5,1},{6,2},{7,3},{8,12},{9,13},{10,... | collective-permute-start | bytes 491528 | tf_op jit(solution)/shard_map/ppermute | solution.py:82
  93.9 9.7 %collective-permute-start.9 = (f32[1,4,1,2,8,640]{5,4,3,1,2,0:T(8,128)S(1)}, f32[1,4,1,2,8,640]{5,4,3,1,2,0:T(8,128)S(1)}, u32[]{:S(2)}, u32[]{:S(2)}) collective-permute-start(f32[1,4,1,2,8,640]{5,4,3,1,2,0:T(8,128)S(1)} %dynamic-slice_bitcast_fusion.4), channel_id=1, source_target_pairs={{0,1},{1,0},{2,3},{3,2},{4,5},{5,4},{6,7},{7,6},{8,9},{9,8},{10,11... | collective-permute-start | bytes 491528 | tf_op jit(solution)/shard_map/ppermute | solution.py:82
  101.9 4.5 %collective-permute-start.5 = (f32[1,1,2,2,8,640]{5,4,3,2,1,0:T(8,128)S(1)}, f32[1,1,2,2,8,640]{5,4,3,2,1,0:T(8,128)S(1)}, u32[]{:S(2)}, u32[]{:S(2)}) collective-permute-start(f32[1,1,2,2,8,640]{5,4,3,2,1,0:T(8,128)S(1)} %dynamic-slice_bitcast_fusion.6), channel_id=1, source_target_pairs={{0,16},{16,0},{32,48},{48,32},{1,17},{17,1},{33,49},{49,33},{2,18}... | collective-permute-start | bytes 245768 | tf_op jit(solution)/shard_map/ppermute | solution.py:82
  103.6 6.2 %collective-permute-start.10 = (f32[1,2,1,2,8,640]{5,4,3,2,1,0:T(8,128)S(1)}, f32[1,2,1,2,8,640]{5,4,3,2,1,0:T(8,128)S(1)}, u32[]{:S(2)}, u32[]{:S(2)}) collective-permute-start(f32[1,2,1,2,8,640]{5,4,3,2,1,0:T(8,128)S(1)} %dynamic-slice_bitcast_fusion.5), channel_id=1, source_target_pairs={{0,2},{1,3},{2,0},{3,1},{4,6},{5,7},{6,4},{7,5},{8,10},{9,11},{10,... | collective-permute-start | bytes 245768 | tf_op jit(solution)/shard_map/ppermute | solution.py:82
  106.4 6.2 %collective-permute-start.6 = (f32[1,1,1,2,8,640]{5,4,3,2,1,0:T(8,128)S(1)}, f32[1,1,1,2,8,640]{5,4,3,2,1,0:T(8,128)S(1)}, u32[]{:S(2)}, u32[]{:S(2)}) collective-permute-start(f32[1,1,1,2,8,640]{5,4,3,2,1,0:T(8,128)S(1)} %constant_dynamic-slice_fusion.6), channel_id=1, source_target_pairs={{0,32},{16,48},{32,0},{48,16},{1,33},{17,49},{33,1},{49,17},{2,34}... | collective-permute-start | bytes 122888 | tf_op jit(solution)/shard_map/ppermute | solution.py:82
  109.9 8.0 %collective-permute-start.11 = (f32[1,1,1,2,8,640]{5,4,3,2,1,0:T(8,128)S(1)}, f32[1,1,1,2,8,640]{5,4,3,2,1,0:T(8,128)S(1)}, u32[]{:S(2)}, u32[]{:S(2)}) collective-permute-start(f32[1,1,1,2,8,640]{5,4,3,2,1,0:T(8,128)S(1)} %constant_dynamic-slice_fusion.4), channel_id=1, source_target_pairs={{0,4},{1,5},{2,6},{3,7},{4,0},{5,1},{6,2},{7,3},{8,12},{9,13},{10,... | collective-permute-start | bytes 122888 | tf_op jit(solution)/shard_map/ppermute | solution.py:82
  117.9 5.6 %collective-permute-start.12 = (f32[1,1,1,1,8,1280]{5,4,3,2,1,0:T(8,128)S(1)}, f32[1,1,1,1,8,1280]{5,4,3,2,1,0:T(8,128)S(1)}, u32[]{:S(2)}, u32[]{:S(2)}) collective-permute-start(f32[1,1,1,1,8,1280]{5,4,3,2,1,0:T(8,128)S(1)} %fusion.165), channel_id=1, source_target_pairs={{0,8},{8,0},{1,9},{9,1},{2,10},{10,2},{3,11},{11,3},{4,12},{12,4},... | collective-permute-start | bytes 122888 | tf_op jit(solution)/shard_map/ppermute | solution.py:82
  123.5 9.9 %collective-permute-start.13 = (f32[1,1,1,1,1,4,1280]{6,5,4,3,2,1,0:T(4,128)S(1)}, f32[1,1,1,1,1,4,1280]{6,5,4,3,2,1,0:T(4,128)S(1)}, u32[]{:S(2)}, u32[]{:S(2)}) collective-permute-start(f32[1,1,1,1,1,4,1280]{6,5,4,3,2,1,0:T(4,128)S(1)} %get-tuple-element.19), channel_id=1, source_target_pairs={{0,0},{1,64},{2,32},{3,96},{4,16},{5,80},{6,48},{7,112},{8,2},{9,6... | collective-permute-start | bytes 61448 | tf_op jit(solution)/shard_map/ppermute | solution.py:181
  131.5 9.0 %collective-permute-start.14 = (f32[1,1,1,1,1,4,1280]{6,5,4,3,2,1,0:T(4,128)S(1)}, f32[1,1,1,1,1,4,1280]{6,5,4,3,2,1,0:T(4,128)S(1)}, u32[]{:S(2)}, u32[]{:S(2)}) collective-permute-start(f32[1,1,1,1,1,4,1280]{6,5,4,3,2,1,0:T(4,128)S(1)} %get-tuple-element.18), channel_id=1, source_target_pairs={{0,1},{1,65},{2,33},{3,97},{4,17},{5,81},{6,49},{7,113},{8,3},{9,6... | collective-permute-start | bytes 61448 | tf_op jit(solution)/shard_map/ppermute | solution.py:181

commit v11 on v10

--- a/solution.py
+++ b/solution.py
@@ -167,12 +167,8 @@
     pair = group_sizes[-1] * row_count
     slab = partial.reshape(tuple(group_sizes[:-1]) + (pair, width))
     slab = exchange_scatter(slab, "core", 0)
-    half = width // 2
-    left = exchange_scatter(slab[..., :half], "z", 1)
-    right = exchange_scatter(slab[..., half:], "y", 2)
-    left = exchange_scatter(left, "y", 2)
-    right = exchange_scatter(right, "z", 1)
-    slab = jnp.concatenate([left, right], -1)
+    slab = exchange_scatter(slab, "z", 1)
+    slab = exchange_scatter(slab, "y", 2)
     slab = exchange_scatter(slab, "xh", 3)
     slab = slab.reshape(tuple(slab.shape[:-2]) + (group_sizes[-1], row_count, width))
     side = lax.axis_index("xl")

time: 145 us -> 178 us (1.23)
  the two profiles are of different devices: /device:TPU:24 before, /device:TPU:88 now
where the time goes in v11:
time: 178 us; the launch traced here: 177 us
  waiting for transfers between devices  100 us (56%)
  starting transfers between devices  25.9 us (15%)
  matrix products  22.2 us (12%)
  other arithmetic  18.3 us (10%)
  local copies, waits for them, and re-layouts  8.5 us (5%)
  between operations  2.57 us (1%)
    ppermute x7, waiting for transfers between devices, exchange_scatter(): slab = mine + lax.ppermute(other, axis, pairs)  88.1 us
    ppermute x7, starting transfers between devices, exchange_scatter(): slab = mine + lax.ppermute(other, axis, pairs)  14.4 us
    ppermute x1, starting transfers between devices, per_device(): lax.ppermute(mine, FINE, owner_pairs(sizes))  9.71 us
    dot_general x10, matrix products, layer_math(): preact = jnp.dot(paired, conv_one, preferred_element_type=jnp.float32)  8.25 us
    ppermute x1, waiting for transfers between devices, per_device(): lax.ppermute(other, FINE, owner_pairs(sizes, flip='xl'))  7.61 us
    convert_element_type x9, other arithmetic, layer_math(): (jnp.tanh(preact[:, :gate_width]) * jax.nn.sigmoid(preact[:, gate_width:]...  7.06 us
    unnamed x27, local copies, waits for them, and re-layouts  5.9 us
    dot_general x1, matrix products, per_device(): skip_sum = jnp.dot(stacked, skip_weight, preferred_element_type=jnp.float32)  5.88 us
  transfers between devices with their start and end apart: 10, of which 9 were waited for; matrix products, arithmetic and copies ran while one was open for 0% of the time, Pallas kernels for 0%

profile of v11, /device:TPU:88, one launch (start us, length us, event | category | flops | bytes accessed | tf_op | source)
XLA Modules:
  0.0 177.5 jit_solution(2541816613937632249)
XLA Ops:
  0.6 1.7 collective-permute-start
  5.6 1.7 fusion.72
  29.2 5.9 %broadcast_select_fusion = bf16[1024,1024]{0,1:T(8,128)(2,1)S(1)} fusion(pred[1024]{0:T(1024)(128)(4,1)S(1)} %add_compare_fusion, bf16[1024,2560]{0,1:T(8,128)(2,1)S(1)} %fusion.119, bf16[2560,1024]{1,0:T(8,128)(2,1)S(1)} %bitcast.120), kind=kOutput, calls=%fused_computation.83 | convolution fusion | flops 5371854848 | bytes 12583936 | tf_op jit(solution)/shard_map/dot_general | solution.py:136
  35.1 3.7 %fusion.1 = f32[1024,1280]{1,0:T(8,128)S(1)} fusion(bf16[1024,1024]{0,1:T(8,128)(2,1)S(1)} %broadcast_select_fusion, bf16[1024,256]{0,1:T(8,128)(2,1)S(1)} %fusion.94, f32[]{:T(128)} %convert_reduce_fusion, s32[1024]{0:T(1024)S(1)} %get-tuple-element.20, s32[1024]{0:T(1024)S(1)} %get-tuple-element.21, s32[1024]{0:T(1024)S(1)} %fusion.165, ...), kind=kOutput, calls=%fused_computation.3 | convolution fusion | flops 2696151040 | bytes 7877636 | tf_op jit(solution)/shard_map/dot_general | solution.py:147
  39.0 2.1 %copy-done.2 = f32[1024,1280]{1,0:T(8,128)} copy-done((f32[1024,1280]{1,0:T(8,128)}, f32[1024,1280]{1,0:T(8,128)S(1)}, u32[]{:S(2)}) %copy-start.2) | copy-done | bytes 5242904
  41.1 1.8 collective-permute-start.1
  42.9 4.7 %collective-permute-done.1 = f32[1,8,4,2,8,1280]{5,4,3,2,1,0:T(8,128)} collective-permute-done((f32[1,8,4,2,8,1280]{5,4,3,2,1,0:T(8,128)S(1)}, f32[1,8,4,2,8,1280]{5,4,3,2,1,0:T(8,128)}, u32[]{:S(2)}, u32[]{:S(2)}) %collective-permute-start.1) | collective-permute-done | bytes 2621472 | tf_op jit(solution)/shard_map/ppermute | solution.py:82
  47.6 2.9 %bitcast_add_fusion = f32[1,8,4,2,8,1280]{5,4,3,2,1,0:T(8,128)S(1)} fusion(f32[1,8,4,2,8,1280]{5,4,3,2,1,0:T(8,128)} %collective-permute-done.1, f32[2,1,8,4,2,8,1280]{6,5,4,3,2,0,1:T(8,128)} %bitcast.110, s32[]{:T(128)S(6)} %select_n.171), kind=kLoop, calls=%fused_computation.8 | loop fusion | flops 655360 | bytes 7864324 | tf_op jit(solution)/shard_map/add | solution.py:82
  50.5 1.2 dynamic-slice_bitcast_fusion.1
  51.7 1.9 %collective-permute-start.2 = (f32[1,4,4,2,8,1280]{5,4,3,2,1,0:T(8,128)}, f32[1,4,4,2,8,1280]{5,4,3,2,1,0:T(8,128)}, u32[]{:S(2)}, u32[]{:S(2)}) collective-permute-start(f32[1,4,4,2,8,1280]{5,4,3,2,1,0:T(8,128)} %dynamic-slice_bitcast_fusion.1), channel_id=1, source_target_pairs={{0,1},{1,0},{2,3},{3,2},{4,5},{5,4},{6,7},{7,6},{8,9},{9,8},{10,11... | collective-permute-start | bytes 3932168 | tf_op jit(solution)/shard_map/ppermute | solution.py:82
  53.6 29.6 %collective-permute-done.2 = f32[1,4,4,2,8,1280]{5,4,3,2,1,0:T(8,128)} collective-permute-done((f32[1,4,4,2,8,1280]{5,4,3,2,1,0:T(8,128)}, f32[1,4,4,2,8,1280]{5,4,3,2,1,0:T(8,128)}, u32[]{:S(2)}, u32[]{:S(2)}) %collective-permute-start.2) | collective-permute-done | bytes 1310752 | tf_op jit(solution)/shard_map/ppermute | solution.py:82
  83.2 1.6 bitcast_add_fusion.1
  86.0 28.1 %collective-permute-done.3 = f32[1,2,4,2,8,1280]{5,4,3,2,1,0:T(8,128)S(1)} collective-permute-done((f32[1,2,4,2,8,1280]{5,4,3,2,1,0:T(8,128)S(1)}, f32[1,2,4,2,8,1280]{5,4,3,2,1,0:T(8,128)S(1)}, u32[]{:S(2)}, u32[]{:S(2)}) %collective-permute-start.3) | collective-permute-done | bytes 655392 | tf_op jit(solution)/shard_map/ppermute | solution.py:82
  114.1 1.2 bitcast_add_fusion.2
  115.4 6.3 %collective-permute-start.4 = (f32[1,1,4,2,8,1280]{5,4,3,2,1,0:T(8,128)S(1)}, f32[1,1,4,2,8,1280]{5,4,3,2,1,0:T(8,128)S(1)}, u32[]{:S(2)}, u32[]{:S(2)}) collective-permute-start(f32[1,1,4,2,8,1280]{5,4,3,2,1,0:T(8,128)S(1)} %constant_dynamic-slice_fusion.6), channel_id=1, source_target_pairs={{0,4},{1,5},{2,6},{3,7},{4,0},{5,1},{6,2},{7,3},{8,12},{9,13},{10,... | collective-permute-start | bytes 983048 | tf_op jit(solution)/shard_map/ppermute | solution.py:82
  121.7 12.3 %collective-permute-done.4 = f32[1,1,4,2,8,1280]{5,4,3,2,1,0:T(8,128)S(1)} collective-permute-done((f32[1,1,4,2,8,1280]{5,4,3,2,1,0:T(8,128)S(1)}, f32[1,1,4,2,8,1280]{5,4,3,2,1,0:T(8,128)S(1)}, u32[]{:S(2)}, u32[]{:S(2)}) %collective-permute-start.4) | collective-permute-done | bytes 327712 | tf_op jit(solution)/shard_map/ppermute | solution.py:82
  134.9 5.2 %collective-permute-done.5 = f32[1,1,2,2,8,1280]{5,4,3,2,1,0:T(8,128)S(1)} collective-permute-done((f32[1,1,2,2,8,1280]{5,4,3,2,1,0:T(8,128)S(1)}, f32[1,1,2,2,8,1280]{5,4,3,2,1,0:T(8,128)S(1)}, u32[]{:S(2)}, u32[]{:S(2)}) %collective-permute-start.5) | collective-permute-done | bytes 163872 | tf_op jit(solution)/shard_map/ppermute | solution.py:82
  140.9 5.3 %collective-permute-done.6 = f32[1,1,1,2,8,1280]{5,4,3,2,1,0:T(8,128)S(1)} collective-permute-done((f32[1,1,1,2,8,1280]{5,4,3,2,1,0:T(8,128)S(1)}, f32[1,1,1,2,8,1280]{5,4,3,2,1,0:T(8,128)S(1)}, u32[]{:S(2)}, u32[]{:S(2)}) %collective-permute-start.6) | collective-permute-done | bytes 81952 | tf_op jit(solution)/shard_map/ppermute | solution.py:82
  146.2 2.7 %collective-permute-start.7 = (f32[1,1,1,1,8,1280]{5,4,3,2,1,0:T(8,128)S(1)}, f32[1,1,1,1,8,1280]{5,4,3,2,1,0:T(8,128)S(1)}, u32[]{:S(2)}, u32[]{:S(2)}) collective-permute-start(f32[1,1,1,1,8,1280]{5,4,3,2,1,0:T(8,128)S(1)} %constant_dynamic-slice_fusion.4), channel_id=1, source_target_pairs={{0,8},{8,0},{1,9},{9,1},{2,10},{10,2},{3,11},{11,3},{4,12},{12,4},... | collective-permute-start | bytes 122888 | tf_op jit(solution)/shard_map/ppermute | solution.py:82
  149.0 2.8 %collective-permute-done.7 = f32[1,1,1,1,8,1280]{5,4,3,2,1,0:T(8,128)S(1)} collective-permute-done((f32[1,1,1,1,8,1280]{5,4,3,2,1,0:T(8,128)S(1)}, f32[1,1,1,1,8,1280]{5,4,3,2,1,0:T(8,128)S(1)}, u32[]{:S(2)}, u32[]{:S(2)}) %collective-permute-start.7) | collective-permute-done | bytes 40992 | tf_op jit(solution)/shard_map/ppermute | solution.py:82
  151.9 9.7 %collective-permute-start.8 = (f32[1,1,1,1,1,4,1280]{6,5,4,3,2,1,0:T(4,128)S(1)}, f32[1,1,1,1,1,4,1280]{6,5,4,3,2,1,0:T(4,128)S(1)}, u32[]{:S(2)}, u32[]{:S(2)}) collective-permute-start(f32[1,1,1,1,1,4,1280]{6,5,4,3,2,1,0:T(4,128)S(1)} %get-tuple-element.17), channel_id=1, source_target_pairs={{0,0},{1,64},{2,32},{3,96},{4,16},{5,80},{6,48},{7,112},{8,2},{9,6... | collective-permute-start | bytes 61448 | tf_op jit(solution)/shard_map/ppermute | solution.py:177
  161.7 4.3 %collective-permute-done.8 = f32[1,1,1,1,1,4,1280]{6,5,4,3,2,1,0:T(4,128)S(1)} collective-permute-done((f32[1,1,1,1,1,4,1280]{6,5,4,3,2,1,0:T(4,128)S(1)}, f32[1,1,1,1,1,4,1280]{6,5,4,3,2,1,0:T(4,128)S(1)}, u32[]{:S(2)}, u32[]{:S(2)}) %collective-permute-start.8) | collective-permute-done | bytes 20512 | tf_op jit(solution)/shard_map/ppermute | solution.py:177
  166.0 7.6 %collective-permute-done.9 = f32[1,1,1,1,1,4,1280]{6,5,4,3,2,1,0:T(4,128)S(1)} collective-permute-done((f32[1,1,1,1,1,4,1280]{6,5,4,3,2,1,0:T(4,128)S(1)}, f32[1,1,1,1,1,4,1280]{6,5,4,3,2,1,0:T(4,128)S(1)}, u32[]{:S(2)}, u32[]{:S(2)}) %collective-permute-start.9) | collective-permute-done | bytes 20512 | tf_op jit(solution)/shard_map/ppermute | solution.py:177
  174.9 1.3 slice_divide_fusion
  (94 shorter events, 29.2 us)
Async XLA Ops:
  0.6 2.5 %copy-start = (s32[1,8]{1,0:T(1,128)S(1)}, s32[1,8]{1,0:T(1,128)}, u32[]{:S(2)}) copy-start(s32[1,8]{1,0:T(1,128)} %param.9) | copy-start | bytes 100
  0.6 3.3 %collective-permute-start = (f32[1,1024]{1,0:T(1,128)}, f32[1,1024]{1,0:T(1,128)S(1)}, u32[]{:S(2)}, u32[]{:S(2)}) collective-permute-start(f32[1,1024]{1,0:T(1,128)} %param.7), channel_id=1, source_target_pairs={{0,64},{64,128},{128,192},{1,65},{65,129},{129,193},{2,66},{66,130... | collective-permute-start | bytes 12296 | tf_op jit(solution)/shard_map/ppermute | solution.py:57
  7.3 1.1 copy-start.5
  7.4 1.1 copy-start.6
  8.2 1.8 %copy-start.4 = (bf16[10,256,512]{2,1,0:T(8,128)(2,1)S(1)}, bf16[10,256,512]{2,1,0:T(8,128)(2,1)}, u32[]{:S(2)}) copy-start(bf16[10,256,512]{2,1,0:T(8,128)(2,1)} %param.11) | copy-start | bytes 7864324
  26.5 2.2 %slice-start = ((s8[5242880]{0:T(1024)(128)(4,1)}), s8[4194304]{0:T(1024)(128)(4,1)S(1)}, s32[]{:S(2)}) async-start(s8[5242880]{0:T(1024)(128)(4,1)} %bitcast.119), calls=%async_computation | async-start | bytes 8388608
  27.6 1.7 slice-start.1
  38.8 2.3 %copy-start.2 = (f32[1024,1280]{1,0:T(8,128)}, f32[1024,1280]{1,0:T(8,128)S(1)}, u32[]{:S(2)}) copy-start(f32[1024,1280]{1,0:T(8,128)S(1)} %fusion.1) | copy-start | bytes 15728644
  41.1 6.4 %collective-permute-start.1 = (f32[1,8,4,2,8,1280]{5,4,3,2,1,0:T(8,128)S(1)}, f32[1,8,4,2,8,1280]{5,4,3,2,1,0:T(8,128)}, u32[]{:S(2)}, u32[]{:S(2)}) collective-permute-start(f32[1,8,4,2,8,1280]{5,4,3,2,1,0:T(8,128)S(1)} %dynamic-slice_bitcast_fusion), channel_id=1, source_target_pairs={{0,64},{64,0},{1,65},{65,1},{2,66},{66,2},{3,67},{67,3},{4,68},{68... | collective-permute-start | bytes 7864328 | tf_op jit(solution)/shard_map/ppermute | solution.py:82
  51.7 31.5 %collective-permute-start.2 = (f32[1,4,4,2,8,1280]{5,4,3,2,1,0:T(8,128)}, f32[1,4,4,2,8,1280]{5,4,3,2,1,0:T(8,128)}, u32[]{:S(2)}, u32[]{:S(2)}) collective-permute-start(f32[1,4,4,2,8,1280]{5,4,3,2,1,0:T(8,128)} %dynamic-slice_bitcast_fusion.1), channel_id=1, source_target_pairs={{0,1},{1,0},{2,3},{3,2},{4,5},{5,4},{6,7},{7,6},{8,9},{9,8},{10,11... | collective-permute-start | bytes 3932168 | tf_op jit(solution)/shard_map/ppermute | solution.py:82
  84.8 1.1 copy-start.3
  85.9 28.3 %collective-permute-start.3 = (f32[1,2,4,2,8,1280]{5,4,3,2,1,0:T(8,128)S(1)}, f32[1,2,4,2,8,1280]{5,4,3,2,1,0:T(8,128)S(1)}, u32[]{:S(2)}, u32[]{:S(2)}) collective-permute-start(f32[1,2,4,2,8,1280]{5,4,3,2,1,0:T(8,128)S(1)} %dynamic-slice_bitcast_fusion.2), channel_id=1, source_target_pairs={{0,2},{1,3},{2,0},{3,1},{4,6},{5,7},{6,4},{7,5},{8,10},{9,11},{10,... | collective-permute-start | bytes 1966088 | tf_op jit(solution)/shard_map/ppermute | solution.py:82
  114.1 63.3 %copy-start.1 = (s32[1,8]{1,0:T(1,128)S(1)}, s32[1,8]{1,0:T(1,128)}, u32[]{:S(2)}) copy-start(s32[1,8]{1,0:T(1,128)} %param.9) | copy-start | bytes 100
  115.4 18.6 %collective-permute-start.4 = (f32[1,1,4,2,8,1280]{5,4,3,2,1,0:T(8,128)S(1)}, f32[1,1,4,2,8,1280]{5,4,3,2,1,0:T(8,128)S(1)}, u32[]{:S(2)}, u32[]{:S(2)}) collective-permute-start(f32[1,1,4,2,8,1280]{5,4,3,2,1,0:T(8,128)S(1)} %constant_dynamic-slice_fusion.6), channel_id=1, source_target_pairs={{0,4},{1,5},{2,6},{3,7},{4,0},{5,1},{6,2},{7,3},{8,12},{9,13},{10,... | collective-permute-start | bytes 983048 | tf_op jit(solution)/shard_map/ppermute | solution.py:82
  134.1 6.0 %collective-permute-start.5 = (f32[1,1,2,2,8,1280]{5,4,3,2,1,0:T(8,128)S(1)}, f32[1,1,2,2,8,1280]{5,4,3,2,1,0:T(8,128)S(1)}, u32[]{:S(2)}, u32[]{:S(2)}) collective-permute-start(f32[1,1,2,2,8,1280]{5,4,3,2,1,0:T(8,128)S(1)} %dynamic-slice_bitcast_fusion.3), channel_id=1, source_target_pairs={{0,16},{16,0},{32,48},{48,32},{1,17},{17,1},{33,49},{49,33},{2,18}... | collective-permute-start | bytes 491528 | tf_op jit(solution)/shard_map/ppermute | solution.py:82
  140.2 6.0 %collective-permute-start.6 = (f32[1,1,1,2,8,1280]{5,4,3,2,1,0:T(8,128)S(1)}, f32[1,1,1,2,8,1280]{5,4,3,2,1,0:T(8,128)S(1)}, u32[]{:S(2)}, u32[]{:S(2)}) collective-permute-start(f32[1,1,1,2,8,1280]{5,4,3,2,1,0:T(8,128)S(1)} %constant_dynamic-slice_fusion.5), channel_id=1, source_target_pairs={{0,32},{16,48},{32,0},{48,16},{1,33},{17,49},{33,1},{49,17},{2,34}... | collective-permute-start | bytes 245768 | tf_op jit(solution)/shard_map/ppermute | solution.py:82
  146.2 5.6 %collective-permute-start.7 = (f32[1,1,1,1,8,1280]{5,4,3,2,1,0:T(8,128)S(1)}, f32[1,1,1,1,8,1280]{5,4,3,2,1,0:T(8,128)S(1)}, u32[]{:S(2)}, u32[]{:S(2)}) collective-permute-start(f32[1,1,1,1,8,1280]{5,4,3,2,1,0:T(8,128)S(1)} %constant_dynamic-slice_fusion.4), channel_id=1, source_target_pairs={{0,8},{8,0},{1,9},{9,1},{2,10},{10,2},{3,11},{11,3},{4,12},{12,4},... | collective-permute-start | bytes 122888 | tf_op jit(solution)/shard_map/ppermute | solution.py:82
  151.9 14.1 %collective-permute-start.8 = (f32[1,1,1,1,1,4,1280]{6,5,4,3,2,1,0:T(4,128)S(1)}, f32[1,1,1,1,1,4,1280]{6,5,4,3,2,1,0:T(4,128)S(1)}, u32[]{:S(2)}, u32[]{:S(2)}) collective-permute-start(f32[1,1,1,1,1,4,1280]{6,5,4,3,2,1,0:T(4,128)S(1)} %get-tuple-element.17), channel_id=1, source_target_pairs={{0,0},{1,64},{2,32},{3,96},{4,16},{5,80},{6,48},{7,112},{8,2},{9,6... | collective-permute-start | bytes 61448 | tf_op jit(solution)/shard_map/ppermute | solution.py:177
  161.6 12.0 %collective-permute-start.9 = (f32[1,1,1,1,1,4,1280]{6,5,4,3,2,1,0:T(4,128)S(1)}, f32[1,1,1,1,1,4,1280]{6,5,4,3,2,1,0:T(4,128)S(1)}, u32[]{:S(2)}, u32[]{:S(2)}) collective-permute-start(f32[1,1,1,1,1,4,1280]{6,5,4,3,2,1,0:T(4,128)S(1)} %get-tuple-element.16), channel_id=1, source_target_pairs={{0,1},{1,65},{2,33},{3,97},{4,17},{5,81},{6,49},{7,113},{8,3},{9,6... | collective-permute-start | bytes 61448 | tf_op jit(solution)/shard_map/ppermute | solution.py:177

commit v12 on v9

--- a/solution.py
+++ b/solution.py
@@ -141,29 +141,37 @@
         jnp.bfloat16
     )
     paired = jnp.concatenate([masked, onehot], 1)
-    partial = lax.dot_general(
-        masked, paired, (((0,), (0,)), ((), ())), preferred_element_type=jnp.float32
-    )
     sizes = {name: lax.axis_size(name) for name in FINE}
     owners = 1
     for name in FINE:
         owners *= sizes[name]
-    row_count = partial.shape[0] // owners
-    width = partial.shape[1]
+    row_count = skip_width // owners
+    width = paired.shape[1]
     group_sizes = []
     for group in GROUPS:
         size = 1
         for name in group:
             size *= sizes[name]
         group_sizes.append(size)
+    pair = group_sizes[-1] * row_count
     local_count = jnp.sum(valid.astype(jnp.float32))
-    rows = lax.broadcasted_iota(jnp.int32, partial.shape, 0)
-    cols = lax.broadcasted_iota(jnp.int32, partial.shape, 1)
-    slot = (rows % row_count == 1) & (cols == rows - 1)
-    partial = jnp.where(slot, local_count, partial)
-    pair = group_sizes[-1] * row_count
-    slab = partial.reshape(tuple(group_sizes[:-1]) + (pair, width))
-    slab = exchange_scatter(slab, "core", 0)
+    cores = group_sizes[0]
+    core_rows = skip_width // cores
+    core = lax.axis_index("core")
+
+    def core_half(part):
+        lhs = lax.dynamic_slice_in_dim(masked, part * core_rows, core_rows, 1)
+        rows_part = lax.dot_general(
+            lhs, paired, (((0,), (0,)), ((), ())), preferred_element_type=jnp.float32
+        )
+        rows = lax.broadcasted_iota(jnp.int32, rows_part.shape, 0) + part * core_rows
+        cols = lax.broadcasted_iota(jnp.int32, rows_part.shape, 1)
+        slot = (rows % row_count == 1) & (cols == rows - 1)
+        rows_part = jnp.where(slot, local_count, rows_part)
+        return rows_part.reshape((1,) + tuple(group_sizes[1:-1]) + (pair, width))
+
+    sent = lax.ppermute(core_half(1 - core), "core", [(i, i ^ 1) for i in range(cores)])
+    slab = core_half(core) + sent
     half = width // 2
     left = exchange_scatter(slab[..., :half], "z", 1)
     right = exchange_scatter(slab[..., half:], "y", 2)

time: 144 us -> 139 us (0.965)
  matrix products: 22.2 us -> 26.5 us
  waiting for transfers between devices: 63.6 us -> 59.4 us
  local copies, waits for them, and re-layouts: 9.17 us -> 6.06 us
  other arithmetic: 16.2 us -> 14.4 us
    ppermute x13 -> x12, waiting for transfers between devices: 54.6 us -> 49.8 us  [exchange_scatter(): slab = mine + lax.ppermute(other, axis, pairs)]
    dot_general x1 -> x2, matrix products: 3.67 us -> 7.95 us  [core_half(): lax.dot_general(lhs, paired, (((0,), (0,)), ((), ())), preferred_element_...]
    add x13 -> x12, other arithmetic: 3.69 us -> 1.45 us  [exchange_scatter(): slab = mine + lax.ppermute(other, axis, pairs)]
    squeeze x12 -> x11, local copies, waits for them, and re-layouts: 3.81 us -> 1.98 us  [exchange_scatter(): other = lax.dynamic_index_in_dim(halves, 1 - side, dim, keepdims=False)]
    ppermute x13 -> x12, starting transfers between devices: 24.5 us -> 23 us  [exchange_scatter(): slab = mine + lax.ppermute(other, axis, pairs)]
    ppermute x0 -> x1, starting transfers between devices: none -> 1.48 us  [per_device(): lax.ppermute(core_half(1 - core), 'core', [(i, i ^ 1) for i in range(core...]
  transfers between devices with their start and end apart: 15 -> 15, of which waited for: 11 -> 11; matrix products, arithmetic and copies ran while one was open for 2% -> 5% of each run, Pallas kernels for 0% -> 0%
where the time goes in v12:
time: 139 us
  waiting for transfers between devices  59.4 us (43%)
  starting transfers between devices  29.9 us (22%)
  matrix products  26.5 us (19%)
  other arithmetic  14.4 us (10%)
  local copies, waits for them, and re-layouts  6.06 us (4%)
  between operations  2.59 us (2%)
    ppermute x12, waiting for transfers between devices, exchange_scatter(): slab = mine + lax.ppermute(other, axis, pairs)  49.8 us
    ppermute x12, starting transfers between devices, exchange_scatter(): slab = mine + lax.ppermute(other, axis, pairs)  23 us
    ppermute x1, waiting for transfers between devices, per_device(): slab = lax.ppermute(slab, FINE, owner_pairs(sizes))  9.03 us
    dot_general x10, matrix products, layer_math(): preact = jnp.dot(paired, conv_one, preferred_element_type=jnp.float32)  8.26 us
    dot_general x2, matrix products, core_half(): lax.dot_general(lhs, paired, (((0,), (0,)), ((), ())), preferred_element_...  7.95 us
    convert_element_type x9, other arithmetic, layer_math(): (jnp.tanh(preact[:, :gate_width]) * jax.nn.sigmoid(preact[:, gate_width:]...  7.07 us
    dot_general x1, matrix products, per_device(): skip_sum = jnp.dot(stacked, skip_weight, preferred_element_type=jnp.float32)  5.88 us
    dot_general x9, matrix products, layer_math(): residual_term = jnp.dot(gated, res_one, preferred_element_type=jnp.float32)  4.46 us
  transfers between devices with their start and end apart: 15, of which 11 were waited for; matrix products, arithmetic and copies ran while one was open for 5% of the time, Pallas kernels for 0%

profile of v12, /device:TPU:28, one launch (start us, length us, event | category | flops | bytes accessed | tf_op | source)
XLA Modules:
  0.0 138.9 jit_solution(15304285649533098710)
XLA Ops:
  0.6 1.7 %collective-permute-start = (f32[1,1024]{1,0:T(1,128)}, f32[1,1024]{1,0:T(1,128)S(1)}, u32[]{:S(2)}, u32[]{:S(2)}) collective-permute-start(f32[1,1024]{1,0:T(1,128)} %param.7), channel_id=1, source_target_pairs={{0,64},{64,128},{128,192},{1,65},{65,129},{129,193},{2,66},{66,130... | collective-permute-start | bytes 12296 | tf_op jit(solution)/shard_map/ppermute | solution.py:54
  5.6 1.7 %fusion.69 = f32[2048,512]{0,1:T(8,128)S(1)} fusion(bf16[2047,128]{1,0:T(8,128)(2,1)S(1)} %bitcast.126, bf16[2048,128]{1,0:T(8,128)(2,1)S(1)} %multiply_convert_fusion, bf16[10,256,512]{2,1,0:T(8,128)(2,1)} %param.11), kind=kOutput, calls=%fused_computation.106 | convolution fusion | flops 540016640 | bytes 5504768 | tf_op jit(solution)/shard_map/dot_general | solution.py:91
  29.3 5.9 %broadcast_select_fusion = bf16[1024,1024]{0,1:T(8,128)(2,1)S(1)} fusion(pred[1024]{0:T(1024)(128)(4,1)S(1)} %add_compare_fusion, bf16[1024,2560]{0,1:T(8,128)(2,1)S(1)} %fusion.118, bf16[2560,1024]{1,0:T(8,128)(2,1)S(1)} %bitcast.140), kind=kOutput, calls=%fused_computation.83 | convolution fusion | flops 5371854848 | bytes 12583936 | tf_op jit(solution)/shard_map/dot_general | solution.py:133
  35.2 3.8 %convolution_select_fusion = f32[512,1280]{1,0:T(8,128)} fusion(bf16[1024,256]{0,1:T(8,128)(2,1)S(1)} %fusion.93, bf16[1024,1024]{0,1:T(8,128)(2,1)S(1)} %broadcast_select_fusion, s32[512]{0:T(512)S(1)} %fusion.171, s32[512]{0:T(512)S(1)} %get-tuple-element.20, s32[512]{0:T(512)S(1)} %get-tuple-element.24, f32[]{:T(128)} %convert_reduce_fusion, ...), kind=kOutput, calls=%fused_computation.1 | convolution fusion | flops 1350696960 | bytes 6298120 | tf_op jit(solution)/shard_map/dot_general | solution.py:164
  38.9 1.5 %collective-permute-start.1 = (f32[1,8,4,2,8,1280]{5,4,3,2,1,0:T(8,128)}, f32[1,8,4,2,8,1280]{5,4,3,2,1,0:T(8,128)S(1)}, u32[]{:S(2)}, u32[]{:S(2)}) collective-permute-start(f32[1,8,4,2,8,1280]{5,4,3,2,1,0:T(8,128)} %bitcast.24), channel_id=1, source_target_pairs={{0,64},{64,0},{1,65},{65,1},{2,66},{66,2},{3,67},{67,3},{4,68},{68... | collective-permute-start | bytes 7864328 | tf_op jit(solution)/shard_map/ppermute | solution.py:173
  40.4 4.2 %convolution_select_fusion.1 = f32[512,1280]{1,0:T(8,128)S(1)} fusion(bf16[1024,256]{0,1:T(8,128)(2,1)S(1)} %fusion.93, bf16[1024,1024]{0,1:T(8,128)(2,1)} %copy-done.5, f32[]{:T(128)} %convert_reduce_fusion, s32[512]{0:T(512)S(1)} %fusion.172, s32[512]{0:T(512)S(1)} %get-tuple-element.21, s32[512]{0:T(512)S(1)} %get-tuple-element.25, ...), kind=kOutput, calls=%fused_computation.2 | convolution fusion | flops 1350696960 | bytes 6298628 | tf_op jit(solution)/shard_map/dot_general | solution.py:164
  46.8 1.9 %collective-permute-start.2 = (f32[1,4,4,2,8,640]{5,4,3,2,1,0:T(8,128)}, f32[1,4,4,2,8,640]{5,4,3,2,1,0:T(8,128)S(1)}, u32[]{:S(2)}, u32[]{:S(2)}) collective-permute-start(f32[1,4,4,2,8,640]{5,4,3,2,1,0:T(8,128)} %dynamic-slice_bitcast_fusion.1), channel_id=1, source_target_pairs={{0,1},{1,0},{2,3},{3,2},{4,5},{5,4},{6,7},{7,6},{8,9},{9,8},{10,11... | collective-permute-start | bytes 1966088 | tf_op jit(solution)/shard_map/ppermute | solution.py:79
  50.3 13.8 %collective-permute-done.2 = f32[1,4,4,2,8,640]{5,4,3,2,1,0:T(8,128)S(1)} collective-permute-done((f32[1,4,4,2,8,640]{5,4,3,2,1,0:T(8,128)}, f32[1,4,4,2,8,640]{5,4,3,2,1,0:T(8,128)S(1)}, u32[]{:S(2)}, u32[]{:S(2)}) %collective-permute-start.2) | collective-permute-done | bytes 655392 | tf_op jit(solution)/shard_map/ppermute | solution.py:79
  64.3 3.4 %collective-permute-start.3 = (f32[1,2,4,2,8,640]{5,4,3,2,1,0:T(8,128)S(1)}, f32[1,2,4,2,8,640]{5,4,3,2,1,0:T(8,128)S(1)}, u32[]{:S(2)}, u32[]{:S(2)}) collective-permute-start(f32[1,2,4,2,8,640]{5,4,3,2,1,0:T(8,128)S(1)} %dynamic-slice_bitcast_fusion.2), channel_id=1, source_target_pairs={{0,2},{1,3},{2,0},{3,1},{4,6},{5,7},{6,4},{7,5},{8,10},{9,11},{10,... | collective-permute-start | bytes 983048 | tf_op jit(solution)/shard_map/ppermute | solution.py:79
  68.9 1.3 collective-permute-start.8
  70.2 12.1 %collective-permute-done.3 = f32[1,2,4,2,8,640]{5,4,3,2,1,0:T(8,128)S(1)} collective-permute-done((f32[1,2,4,2,8,640]{5,4,3,2,1,0:T(8,128)S(1)}, f32[1,2,4,2,8,640]{5,4,3,2,1,0:T(8,128)S(1)}, u32[]{:S(2)}, u32[]{:S(2)}) %collective-permute-start.3) | collective-permute-done | bytes 327712 | tf_op jit(solution)/shard_map/ppermute | solution.py:79
  82.4 6.3 %collective-permute-start.4 = (f32[1,1,4,2,8,640]{5,4,3,2,1,0:T(8,128)S(1)}, f32[1,1,4,2,8,640]{5,4,3,2,1,0:T(8,128)S(1)}, u32[]{:S(2)}, u32[]{:S(2)}) collective-permute-start(f32[1,1,4,2,8,640]{5,4,3,2,1,0:T(8,128)S(1)} %constant_dynamic-slice_fusion.5), channel_id=1, source_target_pairs={{0,4},{1,5},{2,6},{3,7},{4,0},{5,1},{6,2},{7,3},{8,12},{9,13},{10,... | collective-permute-start | bytes 491528 | tf_op jit(solution)/shard_map/ppermute | solution.py:79
  88.9 7.9 %collective-permute-done.4 = f32[1,1,4,2,8,640]{5,4,3,2,1,0:T(8,128)S(1)} collective-permute-done((f32[1,1,4,2,8,640]{5,4,3,2,1,0:T(8,128)S(1)}, f32[1,1,4,2,8,640]{5,4,3,2,1,0:T(8,128)S(1)}, u32[]{:S(2)}, u32[]{:S(2)}) %collective-permute-start.4) | collective-permute-done | bytes 163872 | tf_op jit(solution)/shard_map/ppermute | solution.py:79
  98.5 1.9 %collective-permute-start.10 = (f32[1,2,1,2,8,640]{5,4,3,2,1,0:T(8,128)S(1)}, f32[1,2,1,2,8,640]{5,4,3,2,1,0:T(8,128)S(1)}, u32[]{:S(2)}, u32[]{:S(2)}) collective-permute-start(f32[1,2,1,2,8,640]{5,4,3,2,1,0:T(8,128)S(1)} %dynamic-slice_bitcast_fusion.4), channel_id=1, source_target_pairs={{0,2},{1,3},{2,0},{3,1},{4,6},{5,7},{6,4},{7,5},{8,10},{9,11},{10,... | collective-permute-start | bytes 245768 | tf_op jit(solution)/shard_map/ppermute | solution.py:79
  101.4 1.3 collective-permute-start.6
  102.7 2.1 %collective-permute-done.10 = f32[1,2,1,2,8,640]{5,4,3,2,1,0:T(8,128)S(1)} collective-permute-done((f32[1,2,1,2,8,640]{5,4,3,2,1,0:T(8,128)S(1)}, f32[1,2,1,2,8,640]{5,4,3,2,1,0:T(8,128)S(1)}, u32[]{:S(2)}, u32[]{:S(2)}) %collective-permute-start.10) | collective-permute-done | bytes 81952 | tf_op jit(solution)/shard_map/ppermute | solution.py:79
  104.8 2.8 %collective-permute-start.11 = (f32[1,1,1,2,8,640]{5,4,3,2,1,0:T(8,128)S(1)}, f32[1,1,1,2,8,640]{5,4,3,2,1,0:T(8,128)S(1)}, u32[]{:S(2)}, u32[]{:S(2)}) collective-permute-start(f32[1,1,1,2,8,640]{5,4,3,2,1,0:T(8,128)S(1)} %constant_dynamic-slice_fusion.2), channel_id=1, source_target_pairs={{0,4},{1,5},{2,6},{3,7},{4,0},{5,1},{6,2},{7,3},{8,12},{9,13},{10,... | collective-permute-start | bytes 122888 | tf_op jit(solution)/shard_map/ppermute | solution.py:79
  107.6 5.2 %collective-permute-done.11 = f32[1,1,1,2,8,640]{5,4,3,2,1,0:T(8,128)S(1)} collective-permute-done((f32[1,1,1,2,8,640]{5,4,3,2,1,0:T(8,128)S(1)}, f32[1,1,1,2,8,640]{5,4,3,2,1,0:T(8,128)S(1)}, u32[]{:S(2)}, u32[]{:S(2)}) %collective-permute-start.11) | collective-permute-done | bytes 40992 | tf_op jit(solution)/shard_map/ppermute | solution.py:79
  113.7 4.7 %collective-permute-done.12 = f32[1,1,1,1,8,1280]{5,4,3,2,1,0:T(8,128)S(1)} collective-permute-done((f32[1,1,1,1,8,1280]{5,4,3,2,1,0:T(8,128)S(1)}, f32[1,1,1,1,8,1280]{5,4,3,2,1,0:T(8,128)S(1)}, u32[]{:S(2)}, u32[]{:S(2)}) %collective-permute-start.12) | collective-permute-done | bytes 40992 | tf_op jit(solution)/shard_map/ppermute | solution.py:79
  118.4 1.6 %collective-permute-start.13 = (f32[1,1,1,1,1,4,1280]{6,5,4,3,2,1,0:T(4,128)S(1)}, f32[1,1,1,1,1,4,1280]{6,5,4,3,2,1,0:T(4,128)S(1)}, u32[]{:S(2)}, u32[]{:S(2)}) collective-permute-start(f32[1,1,1,1,1,4,1280]{6,5,4,3,2,1,0:T(4,128)S(1)} %dynamic-slice_bitcast_fusion.6), channel_id=1, source_target_pairs={{0,128},{128,0},{1,129},{129,1},{2,130},{130,2},{3,131},{131,3},{4... | collective-permute-start | bytes 61448 | tf_op jit(solution)/shard_map/ppermute | solution.py:79
  120.0 2.3 %collective-permute-done.13 = f32[1,1,1,1,1,4,1280]{6,5,4,3,2,1,0:T(4,128)S(1)} collective-permute-done((f32[1,1,1,1,1,4,1280]{6,5,4,3,2,1,0:T(4,128)S(1)}, f32[1,1,1,1,1,4,1280]{6,5,4,3,2,1,0:T(4,128)S(1)}, u32[]{:S(2)}, u32[]{:S(2)}) %collective-permute-start.13) | collective-permute-done | bytes 20512 | tf_op jit(solution)/shard_map/ppermute | solution.py:79
  122.3 3.7 %collective-permute-start.14 = (f32[1,1,1,1,1,4,1280]{6,5,4,3,2,1,0:T(4,128)S(1)}, f32[1,1,1,1,1,4,1280]{6,5,4,3,2,1,0:T(4,128)S(1)}, u32[]{:S(2)}, u32[]{:S(2)}) collective-permute-start(f32[1,1,1,1,1,4,1280]{6,5,4,3,2,1,0:T(4,128)S(1)} %bitcast_add_fusion.6), channel_id=1, source_target_pairs={{0,0},{1,64},{2,32},{3,96},{4,16},{5,80},{6,48},{7,112},{8,2},{9,6... | collective-permute-start | bytes 61448 | tf_op jit(solution)/shard_map/ppermute | solution.py:184
  126.0 9.0 %collective-permute-done.14 = f32[1,1,1,1,1,4,1280]{6,5,4,3,2,1,0:T(4,128)S(1)} collective-permute-done((f32[1,1,1,1,1,4,1280]{6,5,4,3,2,1,0:T(4,128)S(1)}, f32[1,1,1,1,1,4,1280]{6,5,4,3,2,1,0:T(4,128)S(1)}, u32[]{:S(2)}, u32[]{:S(2)}) %collective-permute-start.14) | collective-permute-done | bytes 20512 | tf_op jit(solution)/shard_map/ppermute | solution.py:184
  136.4 1.3 slice_divide_fusion
  (115 shorter events, 35.1 us)
Async XLA Ops:
  0.6 1.8 %copy-start = (s32[1,8]{1,0:T(1,128)S(1)}, s32[1,8]{1,0:T(1,128)}, u32[]{:S(2)}) copy-start(s32[1,8]{1,0:T(1,128)} %param.9) | copy-start | bytes 100
  0.6 3.3 %collective-permute-start = (f32[1,1024]{1,0:T(1,128)}, f32[1,1024]{1,0:T(1,128)S(1)}, u32[]{:S(2)}, u32[]{:S(2)}) collective-permute-start(f32[1,1024]{1,0:T(1,128)} %param.7), channel_id=1, source_target_pairs={{0,64},{64,128},{128,192},{1,65},{65,129},{129,193},{2,66},{66,130... | collective-permute-start | bytes 12296 | tf_op jit(solution)/shard_map/ppermute | solution.py:54
  7.3 1.1 copy-start.3
  7.4 1.1 copy-start.4
  8.2 1.8 %copy-start.2 = (bf16[10,256,512]{2,1,0:T(8,128)(2,1)S(1)}, bf16[10,256,512]{2,1,0:T(8,128)(2,1)}, u32[]{:S(2)}) copy-start(bf16[10,256,512]{2,1,0:T(8,128)(2,1)} %param.11) | copy-start | bytes 7864324
  26.5 2.2 %slice-start = ((s8[5242880]{0:T(1024)(128)(4,1)}), s8[4194304]{0:T(1024)(128)(4,1)S(1)}, s32[]{:S(2)}) async-start(s8[5242880]{0:T(1024)(128)(4,1)} %bitcast.139), calls=%async_computation | async-start | bytes 8388608
  27.6 1.7 %slice-start.1 = ((s8[5242880]{0:T(1024)(128)(4,1)}), s8[1048576]{0:T(1024)(128)(4,1)S(1)}, s32[]{:S(2)}) async-start(s8[5242880]{0:T(1024)(128)(4,1)} %bitcast.139), calls=%async_computation.1 | async-start | bytes 2097152
  35.1 3.8 %copy-start.5 = (bf16[1024,1024]{0,1:T(8,128)(2,1)}, bf16[1024,1024]{0,1:T(8,128)(2,1)S(1)}, u32[]{:S(2)}) copy-start(bf16[1024,1024]{0,1:T(8,128)(2,1)S(1)} %broadcast_select_fusion) | copy-start | bytes 6291460
  38.9 6.2 %collective-permute-start.1 = (f32[1,8,4,2,8,1280]{5,4,3,2,1,0:T(8,128)}, f32[1,8,4,2,8,1280]{5,4,3,2,1,0:T(8,128)S(1)}, u32[]{:S(2)}, u32[]{:S(2)}) collective-permute-start(f32[1,8,4,2,8,1280]{5,4,3,2,1,0:T(8,128)} %bitcast.24), channel_id=1, source_target_pairs={{0,64},{64,0},{1,65},{65,1},{2,66},{66,2},{3,67},{67,3},{4,68},{68... | collective-permute-start | bytes 7864328 | tf_op jit(solution)/shard_map/ppermute | solution.py:173
  46.8 17.4 %collective-permute-start.2 = (f32[1,4,4,2,8,640]{5,4,3,2,1,0:T(8,128)}, f32[1,4,4,2,8,640]{5,4,3,2,1,0:T(8,128)S(1)}, u32[]{:S(2)}, u32[]{:S(2)}) collective-permute-start(f32[1,4,4,2,8,640]{5,4,3,2,1,0:T(8,128)} %dynamic-slice_bitcast_fusion.1), channel_id=1, source_target_pairs={{0,1},{1,0},{2,3},{3,2},{4,5},{5,4},{6,7},{7,6},{8,9},{9,8},{10,11... | collective-permute-start | bytes 1966088 | tf_op jit(solution)/shard_map/ppermute | solution.py:79
  49.6 18.0 %collective-permute-start.7 = (f32[1,8,2,2,8,640]{5,4,3,2,1,0:T(8,128)}, f32[1,8,2,2,8,640]{5,4,3,2,1,0:T(8,128)}, u32[]{:S(2)}, u32[]{:S(2)}) collective-permute-start(f32[1,8,2,2,8,640]{5,4,3,2,1,0:T(8,128)} %dynamic-slice_bitcast_fusion), channel_id=1, source_target_pairs={{0,16},{16,0},{32,48},{48,32},{1,17},{17,1},{33,49},{49,33},{2,18}... | collective-permute-start | bytes 1966088 | tf_op jit(solution)/shard_map/ppermute | solution.py:79
  64.3 18.1 %collective-permute-start.3 = (f32[1,2,4,2,8,640]{5,4,3,2,1,0:T(8,128)S(1)}, f32[1,2,4,2,8,640]{5,4,3,2,1,0:T(8,128)S(1)}, u32[]{:S(2)}, u32[]{:S(2)}) collective-permute-start(f32[1,2,4,2,8,640]{5,4,3,2,1,0:T(8,128)S(1)} %dynamic-slice_bitcast_fusion.2), channel_id=1, source_target_pairs={{0,2},{1,3},{2,0},{3,1},{4,6},{5,7},{6,4},{7,5},{8,10},{9,11},{10,... | collective-permute-start | bytes 983048 | tf_op jit(solution)/shard_map/ppermute | solution.py:79
  68.9 19.8 %collective-permute-start.8 = (f32[1,8,1,2,8,640]{5,4,3,2,1,0:T(8,128)S(1)}, f32[1,8,1,2,8,640]{5,4,3,2,1,0:T(8,128)S(1)}, u32[]{:S(2)}, u32[]{:S(2)}) collective-permute-start(f32[1,8,1,2,8,640]{5,4,3,2,1,0:T(8,128)S(1)} %constant_dynamic-slice_fusion.3), channel_id=1, source_target_pairs={{0,32},{16,48},{32,0},{48,16},{1,33},{17,49},{33,1},{49,17},{2,34}... | collective-permute-start | bytes 983048 | tf_op jit(solution)/shard_map/ppermute | solution.py:79
  82.4 56.5 %copy-start.1 = (s32[1,8]{1,0:T(1,128)S(1)}, s32[1,8]{1,0:T(1,128)}, u32[]{:S(2)}) copy-start(s32[1,8]{1,0:T(1,128)} %param.9) | copy-start | bytes 100
  82.4 14.3 %collective-permute-start.4 = (f32[1,1,4,2,8,640]{5,4,3,2,1,0:T(8,128)S(1)}, f32[1,1,4,2,8,640]{5,4,3,2,1,0:T(8,128)S(1)}, u32[]{:S(2)}, u32[]{:S(2)}) collective-permute-start(f32[1,1,4,2,8,640]{5,4,3,2,1,0:T(8,128)S(1)} %constant_dynamic-slice_fusion.5), channel_id=1, source_target_pairs={{0,4},{1,5},{2,6},{3,7},{4,0},{5,1},{6,2},{7,3},{8,12},{9,13},{10,... | collective-permute-start | bytes 491528 | tf_op jit(solution)/shard_map/ppermute | solution.py:79
  88.8 9.7 %collective-permute-start.9 = (f32[1,4,1,2,8,640]{5,4,3,1,2,0:T(8,128)S(1)}, f32[1,4,1,2,8,640]{5,4,3,1,2,0:T(8,128)S(1)}, u32[]{:S(2)}, u32[]{:S(2)}) collective-permute-start(f32[1,4,1,2,8,640]{5,4,3,1,2,0:T(8,128)S(1)} %dynamic-slice_bitcast_fusion.3), channel_id=1, source_target_pairs={{0,1},{1,0},{2,3},{3,2},{4,5},{5,4},{6,7},{7,6},{8,9},{9,8},{10,11... | collective-permute-start | bytes 491528 | tf_op jit(solution)/shard_map/ppermute | solution.py:79
  96.8 4.5 %collective-permute-start.5 = (f32[1,1,2,2,8,640]{5,4,3,2,1,0:T(8,128)S(1)}, f32[1,1,2,2,8,640]{5,4,3,2,1,0:T(8,128)S(1)}, u32[]{:S(2)}, u32[]{:S(2)}) collective-permute-start(f32[1,1,2,2,8,640]{5,4,3,2,1,0:T(8,128)S(1)} %dynamic-slice_bitcast_fusion.5), channel_id=1, source_target_pairs={{0,16},{16,0},{32,48},{48,32},{1,17},{17,1},{33,49},{49,33},{2,18}... | collective-permute-start | bytes 245768 | tf_op jit(solution)/shard_map/ppermute | solution.py:79
  98.5 6.2 %collective-permute-start.10 = (f32[1,2,1,2,8,640]{5,4,3,2,1,0:T(8,128)S(1)}, f32[1,2,1,2,8,640]{5,4,3,2,1,0:T(8,128)S(1)}, u32[]{:S(2)}, u32[]{:S(2)}) collective-permute-start(f32[1,2,1,2,8,640]{5,4,3,2,1,0:T(8,128)S(1)} %dynamic-slice_bitcast_fusion.4), channel_id=1, source_target_pairs={{0,2},{1,3},{2,0},{3,1},{4,6},{5,7},{6,4},{7,5},{8,10},{9,11},{10,... | collective-permute-start | bytes 245768 | tf_op jit(solution)/shard_map/ppermute | solution.py:79
  101.4 6.2 %collective-permute-start.6 = (f32[1,1,1,2,8,640]{5,4,3,2,1,0:T(8,128)S(1)}, f32[1,1,1,2,8,640]{5,4,3,2,1,0:T(8,128)S(1)}, u32[]{:S(2)}, u32[]{:S(2)}) collective-permute-start(f32[1,1,1,2,8,640]{5,4,3,2,1,0:T(8,128)S(1)} %constant_dynamic-slice_fusion.4), channel_id=1, source_target_pairs={{0,32},{16,48},{32,0},{48,16},{1,33},{17,49},{33,1},{49,17},{2,34}... | collective-permute-start | bytes 122888 | tf_op jit(solution)/shard_map/ppermute | solution.py:79
  104.8 8.0 %collective-permute-start.11 = (f32[1,1,1,2,8,640]{5,4,3,2,1,0:T(8,128)S(1)}, f32[1,1,1,2,8,640]{5,4,3,2,1,0:T(8,128)S(1)}, u32[]{:S(2)}, u32[]{:S(2)}) collective-permute-start(f32[1,1,1,2,8,640]{5,4,3,2,1,0:T(8,128)S(1)} %constant_dynamic-slice_fusion.2), channel_id=1, source_target_pairs={{0,4},{1,5},{2,6},{3,7},{4,0},{5,1},{6,2},{7,3},{8,12},{9,13},{10,... | collective-permute-start | bytes 122888 | tf_op jit(solution)/shard_map/ppermute | solution.py:79
  112.8 5.6 %collective-permute-start.12 = (f32[1,1,1,1,8,1280]{5,4,3,2,1,0:T(8,128)S(1)}, f32[1,1,1,1,8,1280]{5,4,3,2,1,0:T(8,128)S(1)}, u32[]{:S(2)}, u32[]{:S(2)}) collective-permute-start(f32[1,1,1,1,8,1280]{5,4,3,2,1,0:T(8,128)S(1)} %fusion.164), channel_id=1, source_target_pairs={{0,8},{8,0},{1,9},{9,1},{2,10},{10,2},{3,11},{11,3},{4,12},{12,4},... | collective-permute-start | bytes 122888 | tf_op jit(solution)/shard_map/ppermute | solution.py:79
  118.4 3.9 %collective-permute-start.13 = (f32[1,1,1,1,1,4,1280]{6,5,4,3,2,1,0:T(4,128)S(1)}, f32[1,1,1,1,1,4,1280]{6,5,4,3,2,1,0:T(4,128)S(1)}, u32[]{:S(2)}, u32[]{:S(2)}) collective-permute-start(f32[1,1,1,1,1,4,1280]{6,5,4,3,2,1,0:T(4,128)S(1)} %dynamic-slice_bitcast_fusion.6), channel_id=1, source_target_pairs={{0,128},{128,0},{1,129},{129,1},{2,130},{130,2},{3,131},{131,3},{4... | collective-permute-start | bytes 61448 | tf_op jit(solution)/shard_map/ppermute | solution.py:79
  122.3 12.7 %collective-permute-start.14 = (f32[1,1,1,1,1,4,1280]{6,5,4,3,2,1,0:T(4,128)S(1)}, f32[1,1,1,1,1,4,1280]{6,5,4,3,2,1,0:T(4,128)S(1)}, u32[]{:S(2)}, u32[]{:S(2)}) collective-permute-start(f32[1,1,1,1,1,4,1280]{6,5,4,3,2,1,0:T(4,128)S(1)} %bitcast_add_fusion.6), channel_id=1, source_target_pairs={{0,0},{1,64},{2,32},{3,96},{4,16},{5,80},{6,48},{7,112},{8,2},{9,6... | collective-permute-start | bytes 61448 | tf_op jit(solution)/shard_map/ppermute | solution.py:184

commit v13 on v12

--- a/solution.py
+++ b/solution.py
@@ -159,22 +159,27 @@
     core_rows = skip_width // cores
     core = lax.axis_index("core")
 
-    def core_half(part):
+    half = width // 2
+
+    def core_half(part, first_col):
         lhs = lax.dynamic_slice_in_dim(masked, part * core_rows, core_rows, 1)
+        rhs = paired[:, first_col : first_col + half]
         rows_part = lax.dot_general(
-            lhs, paired, (((0,), (0,)), ((), ())), preferred_element_type=jnp.float32
+            lhs, rhs, (((0,), (0,)), ((), ())), preferred_element_type=jnp.float32
         )
         rows = lax.broadcasted_iota(jnp.int32, rows_part.shape, 0) + part * core_rows
-        cols = lax.broadcasted_iota(jnp.int32, rows_part.shape, 1)
+        cols = lax.broadcasted_iota(jnp.int32, rows_part.shape, 1) + first_col
         slot = (rows % row_count == 1) & (cols == rows - 1)
         rows_part = jnp.where(slot, local_count, rows_part)
-        return rows_part.reshape((1,) + tuple(group_sizes[1:-1]) + (pair, width))
-
-    sent = lax.ppermute(core_half(1 - core), "core", [(i, i ^ 1) for i in range(cores)])
-    slab = core_half(core) + sent
-    half = width // 2
-    left = exchange_scatter(slab[..., :half], "z", 1)
-    right = exchange_scatter(slab[..., half:], "y", 2)
+        return rows_part.reshape((1,) + tuple(group_sizes[1:-1]) + (pair, half))
+
+    partner = [(i, i ^ 1) for i in range(cores)]
+    sent_left = lax.ppermute(core_half(1 - core, 0), "core", partner)
+    sent_right = lax.ppermute(core_half(1 - core, half), "core", partner)
+    left_slab = core_half(core, 0) + sent_left
+    right_slab = core_half(core, half) + sent_right
+    left = exchange_scatter(left_slab, "z", 1)
+    right = exchange_scatter(right_slab, "y", 2)
     left = exchange_scatter(left, "y", 2)
     right = exchange_scatter(right, "z", 1)
     slab = jnp.concatenate([left, right], -1)

time: 139 us -> 142 us (1.022)
  waiting for transfers between devices: 59.4 us -> 55.3 us
  other arithmetic: 14.4 us -> 17.1 us
  matrix products: 26.5 us -> 29.2 us
  local copies, waits for them, and re-layouts: 6.06 us -> 7.9 us
    ppermute x12, waiting for transfers between devices: 49.8 us -> 46.3 us  [exchange_scatter(): slab = mine + lax.ppermute(other, axis, pairs)]
    add x1 -> x3, other arithmetic: 0.42 us -> 3.13 us  [the longest x1 1.64 us: per_device(): left_slab = core_half(core, 0) + sent_left]
    dot_general x2 -> x4, matrix products: 7.95 us -> 10.5 us  [core_half(): lax.dot_general(lhs, rhs, (((0,), (0,)), ((), ())), preferred_element_typ...]
    unnamed x25 -> x35, local copies, waits for them, and re-layouts: 2.7 us -> 4.82 us
  transfers between devices with their start and end apart: 15 -> 16, of which waited for: 11 -> 11; matrix products, arithmetic and copies ran while one was open for 5% -> 11% of each run, Pallas kernels for 0% -> 0%
where the time goes in v13:
time: 142 us
  waiting for transfers between devices  55.3 us (39%)
  starting transfers between devices  29.5 us (21%)
  matrix products  29.2 us (21%)
  other arithmetic  17.1 us (12%)
  local copies, waits for them, and re-layouts  7.9 us (6%)
  between operations  2.64 us (2%)
    ppermute x12, waiting for transfers between devices, exchange_scatter(): slab = mine + lax.ppermute(other, axis, pairs)  46.3 us
    ppermute x12, starting transfers between devices, exchange_scatter(): slab = mine + lax.ppermute(other, axis, pairs)  22.6 us
    dot_general x4, matrix products, core_half(): lax.dot_general(lhs, rhs, (((0,), (0,)), ((), ())), preferred_element_typ...  10.5 us
    ppermute x1, waiting for transfers between devices, per_device(): slab = lax.ppermute(slab, FINE, owner_pairs(sizes))  9.03 us
    dot_general x10, matrix products, layer_math(): preact = jnp.dot(paired, conv_one, preferred_element_type=jnp.float32)  8.26 us
    convert_element_type x9, other arithmetic, layer_math(): (jnp.tanh(preact[:, :gate_width]) * jax.nn.sigmoid(preact[:, gate_width:]...  7.07 us
    dot_general x1, matrix products, per_device(): skip_sum = jnp.dot(stacked, skip_weight, preferred_element_type=jnp.float32)  5.97 us
    unnamed x35, local copies, waits for them, and re-layouts  4.82 us
  transfers between devices with their start and end apart: 16, of which 11 were waited for; matrix products, arithmetic and copies ran while one was open for 11% of the time, Pallas kernels for 0%

profile of v13, /device:TPU:28, one launch (start us, length us, event | category | flops | bytes accessed | tf_op | source)
XLA Modules:
  0.0 141.6 jit_solution(8649400610397425069)
XLA Ops:
  0.6 1.7 %collective-permute-start = (f32[1,1024]{1,0:T(1,128)}, f32[1,1024]{1,0:T(1,128)S(1)}, u32[]{:S(2)}, u32[]{:S(2)}) collective-permute-start(f32[1,1024]{1,0:T(1,128)} %param.7), channel_id=1, source_target_pairs={{0,64},{64,128},{128,192},{1,65},{65,129},{129,193},{2,66},{66,130... | collective-permute-start | bytes 12296 | tf_op jit(solution)/shard_map/ppermute | solution.py:54
  5.5 1.7 %fusion.73 = f32[2048,512]{0,1:T(8,128)S(1)} fusion(bf16[2047,128]{1,0:T(8,128)(2,1)S(1)} %bitcast.128, bf16[2048,128]{1,0:T(8,128)(2,1)S(1)} %multiply_convert_fusion, bf16[10,256,512]{2,1,0:T(8,128)(2,1)} %param.11), kind=kOutput, calls=%fused_computation.112 | convolution fusion | flops 540016640 | bytes 5504768 | tf_op jit(solution)/shard_map/dot_general | solution.py:91
  29.1 6.0 %broadcast_select_fusion = bf16[1024,1024]{0,1:T(8,128)(2,1)S(1)} fusion(pred[1024]{0:T(1024)(128)(4,1)S(1)} %add_compare_fusion, bf16[1024,2560]{0,1:T(8,128)(2,1)S(1)} %fusion.124, bf16[2560,1024]{1,0:T(8,128)(2,1)S(1)} %bitcast.143), kind=kOutput, calls=%fused_computation.74 | convolution fusion | flops 5371854848 | bytes 12583936 | tf_op jit(solution)/shard_map/dot_general | solution.py:133
  35.1 2.8 %convolution_select_fusion.2 = f32[512,640]{1,0:T(8,128)} fusion(bf16[1024,1024]{0,1:T(8,128)(2,1)S(1)} %broadcast_select_fusion, s32[]{:T(128)S(6)} %select_n.234, s32[512]{0:T(512)S(1)} %get-tuple-element.18, s32[512]{0:T(512)S(1)} %get-tuple-element.22, f32[]{:T(128)} %convert_reduce_fusion, s32[512]{0:T(512)S(1)} %fusion.179, ...), kind=kOutput, calls=%fused_computation.98 | convolution fusion | flops 672727040 | bytes 3676680 | tf_op jit(solution)/shard_map/dot_general | solution.py:167
  37.9 1.5 %collective-permute-start.1 = (f32[1,8,4,2,8,640]{5,4,3,2,1,0:T(8,128)}, f32[1,8,4,2,8,640]{5,4,3,2,1,0:T(8,128)S(1)}, u32[]{:S(2)}, u32[]{:S(2)}) collective-permute-start(f32[1,8,4,2,8,640]{5,4,3,2,1,0:T(8,128)} %bitcast.22), channel_id=1, source_target_pairs={{0,64},{64,0},{1,65},{65,1},{2,66},{66,2},{3,67},{67,3},{4,68},{68... | collective-permute-start | bytes 3932168 | tf_op jit(solution)/shard_map/ppermute | solution.py:177
  39.5 2.8 %convolution_select_fusion = f32[512,640]{1,0:T(8,128)} fusion(bf16[1024,1024]{0,1:T(8,128)(2,1)S(1)} %broadcast_select_fusion, s32[]{:T(128)S(6)} %select_n.234, s32[640]{0:T(1024)S(1)} %iota_add_fusion, s32[512]{0:T(512)S(1)} %get-tuple-element.18, s32[512]{0:T(512)S(1)} %get-tuple-element.22, f32[]{:T(128)} %convert_reduce_fusion, s32[512]{0:T(512)S(1)} %fusion.179, ...), kind=kOutput, calls=%fused_computation.96 | convolution fusion | flops 675348480 | bytes 4991496 | tf_op jit(solution)/shard_map/dot_general | solution.py:167
  42.3 3.3 %convolution_select_fusion.3 = f32[512,640]{1,0:T(8,128)S(1)} fusion(bf16[1024,1024]{0,1:T(8,128)(2,1)} %copy-done.9, s32[]{:T(128)S(6)} %select_n.231, f32[]{:T(128)} %convert_reduce_fusion, s32[512]{0:T(512)S(1)} %get-tuple-element.19, s32[512]{0:T(512)S(1)} %get-tuple-element.23, s32[512]{0:T(512)S(1)} %fusion.180, pred[512]{0:T(512)(128)(4,1)S(1)} %get-tuple-element.21), kind=kOutput, calls=%fused_computation.99 | convolution fusion | flops 672727040 | bytes 3677188 | tf_op jit(solution)/shard_map/dot_general | solution.py:167
  46.7 1.6 %add.379 = f32[1,8,4,2,8,640]{5,4,3,2,1,0:T(8,128)S(1)} add(f32[1,8,4,2,8,640]{5,4,3,2,1,0:T(8,128)S(1)} %bitcast.135, f32[1,8,4,2,8,640]{5,4,3,2,1,0:T(8,128)} %copy-done.4) | non-fusion elementwise | flops 327680 | bytes 3932160 | tf_op jit(solution)/shard_map/add | solution.py:179
  49.2 1.9 %collective-permute-start.2 = (f32[1,4,4,2,8,640]{5,4,3,2,1,0:T(8,128)}, f32[1,4,4,2,8,640]{5,4,3,2,1,0:T(8,128)S(1)}, u32[]{:S(2)}, u32[]{:S(2)}) collective-permute-start(f32[1,4,4,2,8,640]{5,4,3,2,1,0:T(8,128)} %dynamic-slice_bitcast_fusion.1), channel_id=1, source_target_pairs={{0,1},{1,0},{2,3},{3,2},{4,5},{5,4},{6,7},{7,6},{8,9},{9,8},{10,11... | collective-permute-start | bytes 1966088 | tf_op jit(solution)/shard_map/ppermute | solution.py:79
  51.2 1.7 %convolution_select_fusion.1 = f32[512,640]{1,0:T(8,128)S(1)} fusion(bf16[1024,1024]{0,1:T(8,128)(2,1)S(1)} %copy-done.10, s32[]{:T(128)S(6)} %select_n.231, s32[640]{0:T(1024)S(1)} %iota_add_fusion, f32[]{:T(128)} %convert_reduce_fusion, s32[512]{0:T(512)S(1)} %get-tuple-element.19, s32[512]{0:T(512)S(1)} %get-tuple-element.23, s32[512]{0:T(512)S(1)} %fusion.180, ...), kind=kOutput, calls=%fused_computation.97 | convolution fusion | flops 675348480 | bytes 4991496 | tf_op jit(solution)/shard_map/dot_general | solution.py:167
  57.1 9.7 %collective-permute-done.2 = f32[1,4,4,2,8,640]{5,4,3,2,1,0:T(8,128)S(1)} collective-permute-done((f32[1,4,4,2,8,640]{5,4,3,2,1,0:T(8,128)}, f32[1,4,4,2,8,640]{5,4,3,2,1,0:T(8,128)S(1)}, u32[]{:S(2)}, u32[]{:S(2)}) %collective-permute-start.2) | collective-permute-done | bytes 655392 | tf_op jit(solution)/shard_map/ppermute | solution.py:79
  66.9 3.4 %collective-permute-start.3 = (f32[1,2,4,2,8,640]{5,4,3,2,1,0:T(8,128)S(1)}, f32[1,2,4,2,8,640]{5,4,3,2,1,0:T(8,128)S(1)}, u32[]{:S(2)}, u32[]{:S(2)}) collective-permute-start(f32[1,2,4,2,8,640]{5,4,3,2,1,0:T(8,128)S(1)} %dynamic-slice_bitcast_fusion.2), channel_id=1, source_target_pairs={{0,2},{1,3},{2,0},{3,1},{4,6},{5,7},{6,4},{7,5},{8,10},{9,11},{10,... | collective-permute-start | bytes 983048 | tf_op jit(solution)/shard_map/ppermute | solution.py:79
  70.2 3.3 %collective-permute-done.8 = f32[1,8,2,2,8,640]{5,4,3,2,1,0:T(8,128)} collective-permute-done((f32[1,8,2,2,8,640]{5,4,3,2,1,0:T(8,128)}, f32[1,8,2,2,8,640]{5,4,3,2,1,0:T(8,128)}, u32[]{:S(2)}, u32[]{:S(2)}) %collective-permute-start.8) | collective-permute-done | bytes 655392 | tf_op jit(solution)/shard_map/ppermute | solution.py:79
  76.0 9.0 %collective-permute-done.3 = f32[1,2,4,2,8,640]{5,4,3,2,1,0:T(8,128)S(1)} collective-permute-done((f32[1,2,4,2,8,640]{5,4,3,2,1,0:T(8,128)S(1)}, f32[1,2,4,2,8,640]{5,4,3,2,1,0:T(8,128)S(1)}, u32[]{:S(2)}, u32[]{:S(2)}) %collective-permute-start.3) | collective-permute-done | bytes 327712 | tf_op jit(solution)/shard_map/ppermute | solution.py:79
  85.1 6.3 %collective-permute-start.4 = (f32[1,1,4,2,8,640]{5,4,3,2,1,0:T(8,128)S(1)}, f32[1,1,4,2,8,640]{5,4,3,2,1,0:T(8,128)S(1)}, u32[]{:S(2)}, u32[]{:S(2)}) collective-permute-start(f32[1,1,4,2,8,640]{5,4,3,2,1,0:T(8,128)S(1)} %constant_dynamic-slice_fusion.5), channel_id=1, source_target_pairs={{0,4},{1,5},{2,6},{3,7},{4,0},{5,1},{6,2},{7,3},{8,12},{9,13},{10,... | collective-permute-start | bytes 491528 | tf_op jit(solution)/shard_map/ppermute | solution.py:79
  91.6 7.9 %collective-permute-done.4 = f32[1,1,4,2,8,640]{5,4,3,2,1,0:T(8,128)S(1)} collective-permute-done((f32[1,1,4,2,8,640]{5,4,3,2,1,0:T(8,128)S(1)}, f32[1,1,4,2,8,640]{5,4,3,2,1,0:T(8,128)S(1)}, u32[]{:S(2)}, u32[]{:S(2)}) %collective-permute-start.4) | collective-permute-done | bytes 163872 | tf_op jit(solution)/shard_map/ppermute | solution.py:79
  101.2 1.8 %collective-permute-start.11 = (f32[1,2,1,2,8,640]{5,4,3,2,1,0:T(8,128)S(1)}, f32[1,2,1,2,8,640]{5,4,3,2,1,0:T(8,128)S(1)}, u32[]{:S(2)}, u32[]{:S(2)}) collective-permute-start(f32[1,2,1,2,8,640]{5,4,3,2,1,0:T(8,128)S(1)} %dynamic-slice_bitcast_fusion.4), channel_id=1, source_target_pairs={{0,2},{1,3},{2,0},{3,1},{4,6},{5,7},{6,4},{7,5},{8,10},{9,11},{10,... | collective-permute-start | bytes 245768 | tf_op jit(solution)/shard_map/ppermute | solution.py:79
  105.4 2.1 %collective-permute-done.11 = f32[1,2,1,2,8,640]{5,4,3,2,1,0:T(8,128)S(1)} collective-permute-done((f32[1,2,1,2,8,640]{5,4,3,2,1,0:T(8,128)S(1)}, f32[1,2,1,2,8,640]{5,4,3,2,1,0:T(8,128)S(1)}, u32[]{:S(2)}, u32[]{:S(2)}) %collective-permute-start.11) | collective-permute-done | bytes 81952 | tf_op jit(solution)/shard_map/ppermute | solution.py:79
  107.5 2.8 %collective-permute-start.12 = (f32[1,1,1,2,8,640]{5,4,3,2,1,0:T(8,128)S(1)}, f32[1,1,1,2,8,640]{5,4,3,2,1,0:T(8,128)S(1)}, u32[]{:S(2)}, u32[]{:S(2)}) collective-permute-start(f32[1,1,1,2,8,640]{5,4,3,2,1,0:T(8,128)S(1)} %constant_dynamic-slice_fusion.2), channel_id=1, source_target_pairs={{0,4},{1,5},{2,6},{3,7},{4,0},{5,1},{6,2},{7,3},{8,12},{9,13},{10,... | collective-permute-start | bytes 122888 | tf_op jit(solution)/shard_map/ppermute | solution.py:79
  110.3 5.2 %collective-permute-done.12 = f32[1,1,1,2,8,640]{5,4,3,2,1,0:T(8,128)S(1)} collective-permute-done((f32[1,1,1,2,8,640]{5,4,3,2,1,0:T(8,128)S(1)}, f32[1,1,1,2,8,640]{5,4,3,2,1,0:T(8,128)S(1)}, u32[]{:S(2)}, u32[]{:S(2)}) %collective-permute-start.12) | collective-permute-done | bytes 40992 | tf_op jit(solution)/shard_map/ppermute | solution.py:79
  116.4 4.7 %collective-permute-done.13 = f32[1,1,1,1,8,1280]{5,4,3,2,1,0:T(8,128)S(1)} collective-permute-done((f32[1,1,1,1,8,1280]{5,4,3,2,1,0:T(8,128)S(1)}, f32[1,1,1,1,8,1280]{5,4,3,2,1,0:T(8,128)S(1)}, u32[]{:S(2)}, u32[]{:S(2)}) %collective-permute-start.13) | collective-permute-done | bytes 40992 | tf_op jit(solution)/shard_map/ppermute | solution.py:79
  122.4 2.6 %collective-permute-done.14 = f32[1,1,1,1,1,4,1280]{6,5,4,3,2,1,0:T(4,128)S(1)} collective-permute-done((f32[1,1,1,1,1,4,1280]{6,5,4,3,2,1,0:T(4,128)S(1)}, f32[1,1,1,1,1,4,1280]{6,5,4,3,2,1,0:T(4,128)S(1)}, u32[]{:S(2)}, u32[]{:S(2)}) %collective-permute-start.14) | collective-permute-done | bytes 20512 | tf_op jit(solution)/shard_map/ppermute | solution.py:79
  125.0 3.7 %collective-permute-start.15 = (f32[1,1,1,1,1,4,1280]{6,5,4,3,2,1,0:T(4,128)S(1)}, f32[1,1,1,1,1,4,1280]{6,5,4,3,2,1,0:T(4,128)S(1)}, u32[]{:S(2)}, u32[]{:S(2)}) collective-permute-start(f32[1,1,1,1,1,4,1280]{6,5,4,3,2,1,0:T(4,128)S(1)} %bitcast_add_fusion.6), channel_id=1, source_target_pairs={{0,0},{1,64},{2,32},{3,96},{4,16},{5,80},{6,48},{7,112},{8,2},{9,6... | collective-permute-start | bytes 61448 | tf_op jit(solution)/shard_map/ppermute | solution.py:189
  128.7 9.0 %collective-permute-done.15 = f32[1,1,1,1,1,4,1280]{6,5,4,3,2,1,0:T(4,128)S(1)} collective-permute-done((f32[1,1,1,1,1,4,1280]{6,5,4,3,2,1,0:T(4,128)S(1)}, f32[1,1,1,1,1,4,1280]{6,5,4,3,2,1,0:T(4,128)S(1)}, u32[]{:S(2)}, u32[]{:S(2)}) %collective-permute-start.15) | collective-permute-done | bytes 20512 | tf_op jit(solution)/shard_map/ppermute | solution.py:189
  (130 shorter events, 42.5 us)
Async XLA Ops:
  0.6 2.5 %copy-start = (s32[1,8]{1,0:T(1,128)S(1)}, s32[1,8]{1,0:T(1,128)}, u32[]{:S(2)}) copy-start(s32[1,8]{1,0:T(1,128)} %param.9) | copy-start | bytes 100
  0.6 3.2 %collective-permute-start = (f32[1,1024]{1,0:T(1,128)}, f32[1,1024]{1,0:T(1,128)S(1)}, u32[]{:S(2)}, u32[]{:S(2)}) collective-permute-start(f32[1,1024]{1,0:T(1,128)} %param.7), channel_id=1, source_target_pairs={{0,64},{64,128},{128,192},{1,65},{65,129},{129,193},{2,66},{66,130... | collective-permute-start | bytes 12296 | tf_op jit(solution)/shard_map/ppermute | solution.py:54
  8.1 1.8 %copy-start.2 = (bf16[10,256,512]{2,1,0:T(8,128)(2,1)S(1)}, bf16[10,256,512]{2,1,0:T(8,128)(2,1)}, u32[]{:S(2)}) copy-start(bf16[10,256,512]{2,1,0:T(8,128)(2,1)} %param.11) | copy-start | bytes 7864324
  26.4 2.2 %slice-start = ((s8[5242880]{0:T(1024)(128)(4,1)}), s8[4194304]{0:T(1024)(128)(4,1)S(1)}, s32[]{:S(2)}) async-start(s8[5242880]{0:T(1024)(128)(4,1)} %bitcast.142), calls=%async_computation | async-start | bytes 8388608
  35.1 4.4 %copy-start.9 = (bf16[1024,1024]{0,1:T(8,128)(2,1)}, bf16[1024,1024]{0,1:T(8,128)(2,1)S(1)}, u32[]{:S(2)}) copy-start(bf16[1024,1024]{0,1:T(8,128)(2,1)S(1)} %broadcast_select_fusion) | copy-start | bytes 6291460
  37.9 7.8 %collective-permute-start.1 = (f32[1,8,4,2,8,640]{5,4,3,2,1,0:T(8,128)}, f32[1,8,4,2,8,640]{5,4,3,2,1,0:T(8,128)S(1)}, u32[]{:S(2)}, u32[]{:S(2)}) collective-permute-start(f32[1,8,4,2,8,640]{5,4,3,2,1,0:T(8,128)} %bitcast.22), channel_id=1, source_target_pairs={{0,64},{64,0},{1,65},{65,1},{2,66},{66,2},{3,67},{67,3},{4,68},{68... | collective-permute-start | bytes 3932168 | tf_op jit(solution)/shard_map/ppermute | solution.py:177
  39.5 2.8 %copy-start.5 = (bf16[1024,256]{0,1:T(8,128)(2,1)}, bf16[1024,256]{0,1:T(8,128)(2,1)S(1)}, u32[]{:S(2)}) copy-start(bf16[1024,256]{0,1:T(8,128)(2,1)S(1)} %fusion.95) | copy-start | bytes 1572868
  42.3 10.6 %collective-permute-start.7 = (f32[1,8,4,2,8,640]{5,4,3,2,1,0:T(8,128)}, f32[1,8,4,2,8,640]{5,4,3,2,1,0:T(8,128)S(1)}, u32[]{:S(2)}, u32[]{:S(2)}) collective-permute-start(f32[1,8,4,2,8,640]{5,4,3,2,1,0:T(8,128)} %bitcast.35), channel_id=1, source_target_pairs={{0,64},{64,0},{1,65},{65,1},{2,66},{66,2},{3,67},{67,3},{4,68},{68... | collective-permute-start | bytes 3932168 | tf_op jit(solution)/shard_map/ppermute | solution.py:178
  46.7 4.5 %copy-start.6 = (bf16[1024,256]{0,1:T(8,128)(2,1)S(1)}, bf16[1024,256]{0,1:T(8,128)(2,1)}, u32[]{:S(2)}) copy-start(bf16[1024,256]{0,1:T(8,128)(2,1)} %copy-done.5) | copy-start | bytes 1572868
  46.7 4.5 %copy-start.10 = (bf16[1024,1024]{0,1:T(8,128)(2,1)S(1)}, bf16[1024,1024]{0,1:T(8,128)(2,1)}, u32[]{:S(2)}) copy-start(bf16[1024,1024]{0,1:T(8,128)(2,1)} %copy-done.9) | copy-start | bytes 6291460
  49.2 17.5 %collective-permute-start.2 = (f32[1,4,4,2,8,640]{5,4,3,2,1,0:T(8,128)}, f32[1,4,4,2,8,640]{5,4,3,2,1,0:T(8,128)S(1)}, u32[]{:S(2)}, u32[]{:S(2)}) collective-permute-start(f32[1,4,4,2,8,640]{5,4,3,2,1,0:T(8,128)} %dynamic-slice_bitcast_fusion.1), channel_id=1, source_target_pairs={{0,1},{1,0},{2,3},{3,2},{4,5},{5,4},{6,7},{7,6},{8,9},{9,8},{10,11... | collective-permute-start | bytes 1966088 | tf_op jit(solution)/shard_map/ppermute | solution.py:79
  56.4 17.2 %collective-permute-start.8 = (f32[1,8,2,2,8,640]{5,4,3,2,1,0:T(8,128)}, f32[1,8,2,2,8,640]{5,4,3,2,1,0:T(8,128)}, u32[]{:S(2)}, u32[]{:S(2)}) collective-permute-start(f32[1,8,2,2,8,640]{5,4,3,2,1,0:T(8,128)} %dynamic-slice_bitcast_fusion), channel_id=1, source_target_pairs={{0,16},{16,0},{32,48},{48,32},{1,17},{17,1},{33,49},{49,33},{2,18}... | collective-permute-start | bytes 1966088 | tf_op jit(solution)/shard_map/ppermute | solution.py:79
  66.9 18.2 %collective-permute-start.3 = (f32[1,2,4,2,8,640]{5,4,3,2,1,0:T(8,128)S(1)}, f32[1,2,4,2,8,640]{5,4,3,2,1,0:T(8,128)S(1)}, u32[]{:S(2)}, u32[]{:S(2)}) collective-permute-start(f32[1,2,4,2,8,640]{5,4,3,2,1,0:T(8,128)S(1)} %dynamic-slice_bitcast_fusion.2), channel_id=1, source_target_pairs={{0,2},{1,3},{2,0},{3,1},{4,6},{5,7},{6,4},{7,5},{8,10},{9,11},{10,... | collective-permute-start | bytes 983048 | tf_op jit(solution)/shard_map/ppermute | solution.py:79
  74.7 16.7 %collective-permute-start.9 = (f32[1,8,1,2,8,640]{5,4,3,2,1,0:T(8,128)S(1)}, f32[1,8,1,2,8,640]{5,4,3,2,1,0:T(8,128)S(1)}, u32[]{:S(2)}, u32[]{:S(2)}) collective-permute-start(f32[1,8,1,2,8,640]{5,4,3,2,1,0:T(8,128)S(1)} %constant_dynamic-slice_fusion.3), channel_id=1, source_target_pairs={{0,32},{16,48},{32,0},{48,16},{1,33},{17,49},{33,1},{49,17},{2,34}... | collective-permute-start | bytes 983048 | tf_op jit(solution)/shard_map/ppermute | solution.py:79
  85.1 56.5 %copy-start.1 = (s32[1,8]{1,0:T(1,128)S(1)}, s32[1,8]{1,0:T(1,128)}, u32[]{:S(2)}) copy-start(s32[1,8]{1,0:T(1,128)} %param.9) | copy-start | bytes 100
  85.1 14.4 %collective-permute-start.4 = (f32[1,1,4,2,8,640]{5,4,3,2,1,0:T(8,128)S(1)}, f32[1,1,4,2,8,640]{5,4,3,2,1,0:T(8,128)S(1)}, u32[]{:S(2)}, u32[]{:S(2)}) collective-permute-start(f32[1,1,4,2,8,640]{5,4,3,2,1,0:T(8,128)S(1)} %constant_dynamic-slice_fusion.5), channel_id=1, source_target_pairs={{0,4},{1,5},{2,6},{3,7},{4,0},{5,1},{6,2},{7,3},{8,12},{9,13},{10,... | collective-permute-start | bytes 491528 | tf_op jit(solution)/shard_map/ppermute | solution.py:79
  91.5 9.7 %collective-permute-start.10 = (f32[1,4,1,2,8,640]{5,4,3,1,2,0:T(8,128)S(1)}, f32[1,4,1,2,8,640]{5,4,3,1,2,0:T(8,128)S(1)}, u32[]{:S(2)}, u32[]{:S(2)}) collective-permute-start(f32[1,4,1,2,8,640]{5,4,3,1,2,0:T(8,128)S(1)} %dynamic-slice_bitcast_fusion.3), channel_id=1, source_target_pairs={{0,1},{1,0},{2,3},{3,2},{4,5},{5,4},{6,7},{7,6},{8,9},{9,8},{10,11... | collective-permute-start | bytes 491528 | tf_op jit(solution)/shard_map/ppermute | solution.py:79
  99.5 4.5 %collective-permute-start.5 = (f32[1,1,2,2,8,640]{5,4,3,2,1,0:T(8,128)S(1)}, f32[1,1,2,2,8,640]{5,4,3,2,1,0:T(8,128)S(1)}, u32[]{:S(2)}, u32[]{:S(2)}) collective-permute-start(f32[1,1,2,2,8,640]{5,4,3,2,1,0:T(8,128)S(1)} %dynamic-slice_bitcast_fusion.5), channel_id=1, source_target_pairs={{0,16},{16,0},{32,48},{48,32},{1,17},{17,1},{33,49},{49,33},{2,18}... | collective-permute-start | bytes 245768 | tf_op jit(solution)/shard_map/ppermute | solution.py:79
  101.2 6.2 %collective-permute-start.11 = (f32[1,2,1,2,8,640]{5,4,3,2,1,0:T(8,128)S(1)}, f32[1,2,1,2,8,640]{5,4,3,2,1,0:T(8,128)S(1)}, u32[]{:S(2)}, u32[]{:S(2)}) collective-permute-start(f32[1,2,1,2,8,640]{5,4,3,2,1,0:T(8,128)S(1)} %dynamic-slice_bitcast_fusion.4), channel_id=1, source_target_pairs={{0,2},{1,3},{2,0},{3,1},{4,6},{5,7},{6,4},{7,5},{8,10},{9,11},{10,... | collective-permute-start | bytes 245768 | tf_op jit(solution)/shard_map/ppermute | solution.py:79
  104.1 6.2 %collective-permute-start.6 = (f32[1,1,1,2,8,640]{5,4,3,2,1,0:T(8,128)S(1)}, f32[1,1,1,2,8,640]{5,4,3,2,1,0:T(8,128)S(1)}, u32[]{:S(2)}, u32[]{:S(2)}) collective-permute-start(f32[1,1,1,2,8,640]{5,4,3,2,1,0:T(8,128)S(1)} %constant_dynamic-slice_fusion.4), channel_id=1, source_target_pairs={{0,32},{16,48},{32,0},{48,16},{1,33},{17,49},{33,1},{49,17},{2,34}... | collective-permute-start | bytes 122888 | tf_op jit(solution)/shard_map/ppermute | solution.py:79
  107.5 8.0 %collective-permute-start.12 = (f32[1,1,1,2,8,640]{5,4,3,2,1,0:T(8,128)S(1)}, f32[1,1,1,2,8,640]{5,4,3,2,1,0:T(8,128)S(1)}, u32[]{:S(2)}, u32[]{:S(2)}) collective-permute-start(f32[1,1,1,2,8,640]{5,4,3,2,1,0:T(8,128)S(1)} %constant_dynamic-slice_fusion.2), channel_id=1, source_target_pairs={{0,4},{1,5},{2,6},{3,7},{4,0},{5,1},{6,2},{7,3},{8,12},{9,13},{10,... | collective-permute-start | bytes 122888 | tf_op jit(solution)/shard_map/ppermute | solution.py:79
  115.5 5.6 %collective-permute-start.13 = (f32[1,1,1,1,8,1280]{5,4,3,2,1,0:T(8,128)S(1)}, f32[1,1,1,1,8,1280]{5,4,3,2,1,0:T(8,128)S(1)}, u32[]{:S(2)}, u32[]{:S(2)}) collective-permute-start(f32[1,1,1,1,8,1280]{5,4,3,2,1,0:T(8,128)S(1)} %fusion.170), channel_id=1, source_target_pairs={{0,8},{8,0},{1,9},{9,1},{2,10},{10,2},{3,11},{11,3},{4,12},{12,4},... | collective-permute-start | bytes 122888 | tf_op jit(solution)/shard_map/ppermute | solution.py:79
  121.2 3.9 %collective-permute-start.14 = (f32[1,1,1,1,1,4,1280]{6,5,4,3,2,1,0:T(4,128)S(1)}, f32[1,1,1,1,1,4,1280]{6,5,4,3,2,1,0:T(4,128)S(1)}, u32[]{:S(2)}, u32[]{:S(2)}) collective-permute-start(f32[1,1,1,1,1,4,1280]{6,5,4,3,2,1,0:T(4,128)S(1)} %dynamic-slice_bitcast_fusion.6), channel_id=1, source_target_pairs={{0,128},{128,0},{1,129},{129,1},{2,130},{130,2},{3,131},{131,3},{4... | collective-permute-start | bytes 61448 | tf_op jit(solution)/shard_map/ppermute | solution.py:79
  125.0 12.7 %collective-permute-start.15 = (f32[1,1,1,1,1,4,1280]{6,5,4,3,2,1,0:T(4,128)S(1)}, f32[1,1,1,1,1,4,1280]{6,5,4,3,2,1,0:T(4,128)S(1)}, u32[]{:S(2)}, u32[]{:S(2)}) collective-permute-start(f32[1,1,1,1,1,4,1280]{6,5,4,3,2,1,0:T(4,128)S(1)} %bitcast_add_fusion.6), channel_id=1, source_target_pairs={{0,0},{1,64},{2,32},{3,96},{4,16},{5,80},{6,48},{7,112},{8,2},{9,6... | collective-permute-start | bytes 61448 | tf_op jit(solution)/shard_map/ppermute | solution.py:189
  (5 other events, 5.9 us)

commit v14 on v12

--- a/solution.py
+++ b/solution.py
@@ -172,7 +172,7 @@
 
     sent = lax.ppermute(core_half(1 - core), "core", [(i, i ^ 1) for i in range(cores)])
     slab = core_half(core) + sent
-    half = width // 2
+    half = (width // 128 * 2 // 5) * 128
     left = exchange_scatter(slab[..., :half], "z", 1)
     right = exchange_scatter(slab[..., half:], "y", 2)
     left = exchange_scatter(left, "y", 2)

time: 139 us -> 149 us (1.072)
  waiting for transfers between devices: 59.4 us -> 67.5 us
  starting transfers between devices: 29.9 us -> 24.8 us
  local copies, waits for them, and re-layouts: 6.06 us -> 10.4 us
  other arithmetic: 14.4 us -> 17.1 us
    ppermute x12, waiting for transfers between devices: 49.8 us -> 56 us  [exchange_scatter(): slab = mine + lax.ppermute(other, axis, pairs)]
    unnamed x25 -> x35, local copies, waits for them, and re-layouts: 2.7 us -> 6.39 us
    ppermute x12, starting transfers between devices: 23 us -> 19.7 us  [exchange_scatter(): slab = mine + lax.ppermute(other, axis, pairs)]
    ppermute x1, waiting for transfers between devices: 9.03 us -> 10.9 us  [per_device(): slab = lax.ppermute(slab, FINE, owner_pairs(sizes))]
    ppermute x1, starting transfers between devices: 3.68 us -> 1.92 us  [per_device(): slab = lax.ppermute(slab, FINE, owner_pairs(sizes))]
    add x1, other arithmetic: 0.42 us -> 2.15 us  [per_device(): slab = core_half(core) + sent]
  transfers between devices with their start and end apart: 15 -> 15, of which waited for: 11 -> 11; matrix products, arithmetic and copies ran while one was open for 5% -> 6% of each run, Pallas kernels for 0% -> 0%
where the time goes in v14:
time: 149 us
  waiting for transfers between devices  67.5 us (45%)
  matrix products  26.5 us (18%)
  starting transfers between devices  24.8 us (17%)
  other arithmetic  17.1 us (11%)
  local copies, waits for them, and re-layouts  10.4 us (7%)
  between operations  2.61 us (2%)
    ppermute x12, waiting for transfers between devices, exchange_scatter(): slab = mine + lax.ppermute(other, axis, pairs)  56 us
    ppermute x12, starting transfers between devices, exchange_scatter(): slab = mine + lax.ppermute(other, axis, pairs)  19.7 us
    ppermute x1, waiting for transfers between devices, per_device(): slab = lax.ppermute(slab, FINE, owner_pairs(sizes))  10.9 us
    dot_general x10, matrix products, layer_math(): preact = jnp.dot(paired, conv_one, preferred_element_type=jnp.float32)  8.26 us
    dot_general x2, matrix products, core_half(): lax.dot_general(lhs, paired, (((0,), (0,)), ((), ())), preferred_element_...  7.95 us
    convert_element_type x9, other arithmetic, layer_math(): (jnp.tanh(preact[:, :gate_width]) * jax.nn.sigmoid(preact[:, gate_width:]...  7.07 us
    unnamed x35, local copies, waits for them, and re-layouts  6.39 us
    dot_general x1, matrix products, per_device(): skip_sum = jnp.dot(stacked, skip_weight, preferred_element_type=jnp.float32)  5.88 us
  transfers between devices with their start and end apart: 15, of which 11 were waited for; matrix products, arithmetic and copies ran while one was open for 6% of the time, Pallas kernels for 0%

profile of v14, /device:TPU:28, one launch (start us, length us, event | category | flops | bytes accessed | tf_op | source)
XLA Modules:
  0.0 148.9 jit_solution(10708688890445884724)
XLA Ops:
  0.6 1.7 %collective-permute-start = (f32[1,1024]{1,0:T(1,128)}, f32[1,1024]{1,0:T(1,128)S(1)}, u32[]{:S(2)}, u32[]{:S(2)}) collective-permute-start(f32[1,1024]{1,0:T(1,128)} %param.7), channel_id=1, source_target_pairs={{0,64},{64,128},{128,192},{1,65},{65,129},{129,193},{2,66},{66,130... | collective-permute-start | bytes 12296 | tf_op jit(solution)/shard_map/ppermute | solution.py:54
  5.6 1.7 %fusion.69 = f32[2048,512]{0,1:T(8,128)S(1)} fusion(bf16[2047,128]{1,0:T(8,128)(2,1)S(1)} %bitcast.124, bf16[2048,128]{1,0:T(8,128)(2,1)S(1)} %multiply_convert_fusion, bf16[10,256,512]{2,1,0:T(8,128)(2,1)} %param.11), kind=kOutput, calls=%fused_computation.106 | convolution fusion | flops 540016640 | bytes 5504768 | tf_op jit(solution)/shard_map/dot_general | solution.py:91
  29.3 5.9 %broadcast_select_fusion = bf16[1024,1024]{0,1:T(8,128)(2,1)S(1)} fusion(pred[1024]{0:T(1024)(128)(4,1)S(1)} %add_compare_fusion, bf16[1024,2560]{0,1:T(8,128)(2,1)S(1)} %fusion.118, bf16[2560,1024]{1,0:T(8,128)(2,1)S(1)} %bitcast.140), kind=kOutput, calls=%fused_computation.83 | convolution fusion | flops 5371854848 | bytes 12583936 | tf_op jit(solution)/shard_map/dot_general | solution.py:133
  35.2 3.8 %convolution_select_fusion = f32[512,1280]{1,0:T(8,128)} fusion(bf16[1024,256]{0,1:T(8,128)(2,1)S(1)} %fusion.93, bf16[1024,1024]{0,1:T(8,128)(2,1)S(1)} %broadcast_select_fusion, s32[512]{0:T(512)S(1)} %fusion.171, s32[512]{0:T(512)S(1)} %get-tuple-element.18, s32[512]{0:T(512)S(1)} %get-tuple-element.22, f32[]{:T(128)} %convert_reduce_fusion, ...), kind=kOutput, calls=%fused_computation.1 | convolution fusion | flops 1350696960 | bytes 6298120 | tf_op jit(solution)/shard_map/dot_general | solution.py:164
  38.9 1.5 collective-permute-start.1
  40.4 4.2 %convolution_select_fusion.1 = f32[512,1280]{1,0:T(8,128)S(1)} fusion(bf16[1024,256]{0,1:T(8,128)(2,1)S(1)} %fusion.93, bf16[1024,1024]{0,1:T(8,128)(2,1)} %copy-done.10, f32[]{:T(128)} %convert_reduce_fusion, s32[512]{0:T(512)S(1)} %fusion.172, s32[512]{0:T(512)S(1)} %get-tuple-element.19, s32[512]{0:T(512)S(1)} %get-tuple-element.23, ...), kind=kOutput, calls=%fused_computation.2 | convolution fusion | flops 1350696960 | bytes 6298628 | tf_op jit(solution)/shard_map/dot_general | solution.py:164
  45.2 1.5 %copy-done.6 = f32[1,8,4,2,8,1280]{5,4,3,2,1,0:T(8,128)} copy-done((f32[1,8,4,2,8,1280]{5,4,3,2,1,0:T(8,128)}, f32[1,8,4,2,8,1280]{5,4,3,2,1,0:T(8,128)S(1)}, u32[]{:S(2)}) %copy-start.6) | copy-done | bytes 2621464
  46.6 2.2 %add.359 = f32[1,8,4,2,8,1280]{5,4,3,2,1,0:T(8,128)S(1)} add(f32[1,8,4,2,8,1280]{5,4,3,2,1,0:T(8,128)S(1)} %bitcast.128, f32[1,8,4,2,8,1280]{5,4,3,2,1,0:T(8,128)} %copy-done.6) | non-fusion elementwise | flops 655360 | bytes 7864320 | tf_op jit(solution)/shard_map/add | solution.py:174
  50.8 1.9 %collective-permute-start.2 = (f32[1,4,4,2,8,512]{5,4,3,2,1,0:T(8,128)}, f32[1,4,4,2,8,512]{5,4,3,2,1,0:T(8,128)}, u32[]{:S(2)}, u32[]{:S(2)}) collective-permute-start(f32[1,4,4,2,8,512]{5,4,3,2,1,0:T(8,128)} %dynamic-slice_bitcast_fusion.1), channel_id=1, source_target_pairs={{0,1},{1,0},{2,3},{3,2},{4,5},{5,4},{6,7},{7,6},{8,9},{9,8},{10,11... | collective-permute-start | bytes 1572872 | tf_op jit(solution)/shard_map/ppermute | solution.py:79
  55.8 9.7 %collective-permute-done.2 = f32[1,4,4,2,8,512]{5,4,3,2,1,0:T(8,128)} collective-permute-done((f32[1,4,4,2,8,512]{5,4,3,2,1,0:T(8,128)}, f32[1,4,4,2,8,512]{5,4,3,2,1,0:T(8,128)}, u32[]{:S(2)}, u32[]{:S(2)}) %collective-permute-start.2) | collective-permute-done | bytes 524320 | tf_op jit(solution)/shard_map/ppermute | solution.py:79
  66.7 3.4 %collective-permute-start.3 = (f32[1,2,4,2,8,512]{5,4,3,2,1,0:T(8,128)S(1)}, f32[1,2,4,2,8,512]{5,4,3,2,1,0:T(8,128)}, u32[]{:S(2)}, u32[]{:S(2)}) collective-permute-start(f32[1,2,4,2,8,512]{5,4,3,2,1,0:T(8,128)S(1)} %dynamic-slice_bitcast_fusion.2), channel_id=1, source_target_pairs={{0,2},{1,3},{2,0},{3,1},{4,6},{5,7},{6,4},{7,5},{8,10},{9,11},{10,... | collective-permute-start | bytes 786440 | tf_op jit(solution)/shard_map/ppermute | solution.py:79
  70.1 11.9 %collective-permute-done.3 = f32[1,2,4,2,8,512]{5,4,3,2,1,0:T(8,128)} collective-permute-done((f32[1,2,4,2,8,512]{5,4,3,2,1,0:T(8,128)S(1)}, f32[1,2,4,2,8,512]{5,4,3,2,1,0:T(8,128)}, u32[]{:S(2)}, u32[]{:S(2)}) %collective-permute-start.3) | collective-permute-done | bytes 262176 | tf_op jit(solution)/shard_map/ppermute | solution.py:79
  83.6 6.2 %collective-permute-start.4 = (f32[1,1,4,2,8,512]{5,4,3,2,1,0:T(8,128)}, f32[1,1,4,2,8,512]{5,4,3,2,1,0:T(8,128)S(1)}, u32[]{:S(2)}, u32[]{:S(2)}) collective-permute-start(f32[1,1,4,2,8,512]{5,4,3,2,1,0:T(8,128)} %constant_dynamic-slice_fusion.5), channel_id=1, source_target_pairs={{0,4},{1,5},{2,6},{3,7},{4,0},{5,1},{6,2},{7,3},{8,12},{9,13},{10,... | collective-permute-start | bytes 393224 | tf_op jit(solution)/shard_map/ppermute | solution.py:79
  90.0 1.3 collective-permute-start.8
  91.3 4.8 %collective-permute-done.4 = f32[1,1,4,2,8,512]{5,4,3,2,1,0:T(8,128)S(1)} collective-permute-done((f32[1,1,4,2,8,512]{5,4,3,2,1,0:T(8,128)}, f32[1,1,4,2,8,512]{5,4,3,2,1,0:T(8,128)S(1)}, u32[]{:S(2)}, u32[]{:S(2)}) %collective-permute-start.4) | collective-permute-done | bytes 131104 | tf_op jit(solution)/shard_map/ppermute | solution.py:79
  96.9 5.6 %collective-permute-done.8 = f32[1,8,1,2,8,768]{5,4,3,2,1,0:T(8,128)S(1)} collective-permute-done((f32[1,8,1,2,8,768]{5,4,3,2,1,0:T(8,128)S(1)}, f32[1,8,1,2,8,768]{5,4,3,2,1,0:T(8,128)S(1)}, u32[]{:S(2)}, u32[]{:S(2)}) %collective-permute-start.8) | collective-permute-done | bytes 393248 | tf_op jit(solution)/shard_map/ppermute | solution.py:79
  102.8 5.6 %collective-permute-done.9 = f32[1,4,1,2,8,768]{5,4,3,1,2,0:T(8,128)S(1)} collective-permute-done((f32[1,4,1,2,8,768]{5,4,3,1,2,0:T(8,128)S(1)}, f32[1,4,1,2,8,768]{5,4,3,1,2,0:T(8,128)S(1)}, u32[]{:S(2)}, u32[]{:S(2)}) %collective-permute-start.9) | collective-permute-done | bytes 196640 | tf_op jit(solution)/shard_map/ppermute | solution.py:79
  110.2 4.3 %collective-permute-done.10 = f32[1,2,1,2,8,768]{5,4,3,2,1,0:T(8,128)S(1)} collective-permute-done((f32[1,2,1,2,8,768]{5,4,3,2,1,0:T(8,128)S(1)}, f32[1,2,1,2,8,768]{5,4,3,2,1,0:T(8,128)S(1)}, u32[]{:S(2)}, u32[]{:S(2)}) %collective-permute-start.10) | collective-permute-done | bytes 98336 | tf_op jit(solution)/shard_map/ppermute | solution.py:79
  115.5 7.1 %collective-permute-done.11 = f32[1,1,1,2,8,768]{5,4,3,2,1,0:T(8,128)S(1)} collective-permute-done((f32[1,1,1,2,8,768]{5,4,3,2,1,0:T(8,128)S(1)}, f32[1,1,1,2,8,768]{5,4,3,2,1,0:T(8,128)S(1)}, u32[]{:S(2)}, u32[]{:S(2)}) %collective-permute-start.11) | collective-permute-done | bytes 49184 | tf_op jit(solution)/shard_map/ppermute | solution.py:79
  123.6 4.7 %collective-permute-done.12 = f32[1,1,1,1,8,1280]{5,4,3,2,1,0:T(8,128)S(1)} collective-permute-done((f32[1,1,1,1,8,1280]{5,4,3,2,1,0:T(8,128)S(1)}, f32[1,1,1,1,8,1280]{5,4,3,2,1,0:T(8,128)S(1)}, u32[]{:S(2)}, u32[]{:S(2)}) %collective-permute-start.12) | collective-permute-done | bytes 40992 | tf_op jit(solution)/shard_map/ppermute | solution.py:79
  128.3 1.6 %collective-permute-start.13 = (f32[1,1,1,1,1,4,1280]{6,5,4,3,2,1,0:T(4,128)S(1)}, f32[1,1,1,1,1,4,1280]{6,5,4,3,2,1,0:T(4,128)S(1)}, u32[]{:S(2)}, u32[]{:S(2)}) collective-permute-start(f32[1,1,1,1,1,4,1280]{6,5,4,3,2,1,0:T(4,128)S(1)} %dynamic-slice_bitcast_fusion.6), channel_id=1, source_target_pairs={{0,128},{128,0},{1,129},{129,1},{2,130},{130,2},{3,131},{131,3},{4... | collective-permute-start | bytes 61448 | tf_op jit(solution)/shard_map/ppermute | solution.py:79
  129.9 2.3 %collective-permute-done.13 = f32[1,1,1,1,1,4,1280]{6,5,4,3,2,1,0:T(4,128)S(1)} collective-permute-done((f32[1,1,1,1,1,4,1280]{6,5,4,3,2,1,0:T(4,128)S(1)}, f32[1,1,1,1,1,4,1280]{6,5,4,3,2,1,0:T(4,128)S(1)}, u32[]{:S(2)}, u32[]{:S(2)}) %collective-permute-start.13) | collective-permute-done | bytes 20512 | tf_op jit(solution)/shard_map/ppermute | solution.py:79
  132.2 1.9 %collective-permute-start.14 = (f32[1,1,1,1,1,4,1280]{6,5,4,3,2,1,0:T(4,128)S(1)}, f32[1,1,1,1,1,4,1280]{6,5,4,3,2,1,0:T(4,128)S(1)}, u32[]{:S(2)}, u32[]{:S(2)}) collective-permute-start(f32[1,1,1,1,1,4,1280]{6,5,4,3,2,1,0:T(4,128)S(1)} %bitcast_add_fusion.6), channel_id=1, source_target_pairs={{0,0},{1,64},{2,32},{3,96},{4,16},{5,80},{6,48},{7,112},{8,2},{9,6... | collective-permute-start | bytes 61448 | tf_op jit(solution)/shard_map/ppermute | solution.py:184
  134.2 10.9 %collective-permute-done.14 = f32[1,1,1,1,1,4,1280]{6,5,4,3,2,1,0:T(4,128)S(1)} collective-permute-done((f32[1,1,1,1,1,4,1280]{6,5,4,3,2,1,0:T(4,128)S(1)}, f32[1,1,1,1,1,4,1280]{6,5,4,3,2,1,0:T(4,128)S(1)}, u32[]{:S(2)}, u32[]{:S(2)}) %collective-permute-start.14) | collective-permute-done | bytes 20512 | tf_op jit(solution)/shard_map/ppermute | solution.py:184
  (126 shorter events, 40.7 us)
Async XLA Ops:
  0.6 1.8 %copy-start = (s32[1,8]{1,0:T(1,128)S(1)}, s32[1,8]{1,0:T(1,128)}, u32[]{:S(2)}) copy-start(s32[1,8]{1,0:T(1,128)} %param.9) | copy-start | bytes 100
  0.6 3.3 %collective-permute-start = (f32[1,1024]{1,0:T(1,128)}, f32[1,1024]{1,0:T(1,128)S(1)}, u32[]{:S(2)}, u32[]{:S(2)}) collective-permute-start(f32[1,1024]{1,0:T(1,128)} %param.7), channel_id=1, source_target_pairs={{0,64},{64,128},{128,192},{1,65},{65,129},{129,193},{2,66},{66,130... | collective-permute-start | bytes 12296 | tf_op jit(solution)/shard_map/ppermute | solution.py:54
  8.2 1.8 %copy-start.7 = (bf16[10,256,512]{2,1,0:T(8,128)(2,1)S(1)}, bf16[10,256,512]{2,1,0:T(8,128)(2,1)}, u32[]{:S(2)}) copy-start(bf16[10,256,512]{2,1,0:T(8,128)(2,1)} %param.11) | copy-start | bytes 7864324
  26.5 2.2 %slice-start = ((s8[5242880]{0:T(1024)(128)(4,1)}), s8[4194304]{0:T(1024)(128)(4,1)S(1)}, s32[]{:S(2)}) async-start(s8[5242880]{0:T(1024)(128)(4,1)} %bitcast.139), calls=%async_computation | async-start | bytes 8388608
  27.6 1.7 %slice-start.1 = ((s8[5242880]{0:T(1024)(128)(4,1)}), s8[1048576]{0:T(1024)(128)(4,1)S(1)}, s32[]{:S(2)}) async-start(s8[5242880]{0:T(1024)(128)(4,1)} %bitcast.139), calls=%async_computation.1 | async-start | bytes 2097152
  35.1 3.8 %copy-start.10 = (bf16[1024,1024]{0,1:T(8,128)(2,1)}, bf16[1024,1024]{0,1:T(8,128)(2,1)S(1)}, u32[]{:S(2)}) copy-start(bf16[1024,1024]{0,1:T(8,128)(2,1)S(1)} %broadcast_select_fusion) | copy-start | bytes 6291460
  38.9 6.2 %collective-permute-start.1 = (f32[1,8,4,2,8,1280]{5,4,3,2,1,0:T(8,128)}, f32[1,8,4,2,8,1280]{5,4,3,2,1,0:T(8,128)S(1)}, u32[]{:S(2)}, u32[]{:S(2)}) collective-permute-start(f32[1,8,4,2,8,1280]{5,4,3,2,1,0:T(8,128)} %bitcast.24), channel_id=1, source_target_pairs={{0,64},{64,0},{1,65},{65,1},{2,66},{66,2},{3,67},{67,3},{4,68},{68... | collective-permute-start | bytes 7864328 | tf_op jit(solution)/shard_map/ppermute | solution.py:173
  45.2 1.5 %copy-start.6 = (f32[1,8,4,2,8,1280]{5,4,3,2,1,0:T(8,128)}, f32[1,8,4,2,8,1280]{5,4,3,2,1,0:T(8,128)S(1)}, u32[]{:S(2)}) copy-start(f32[1,8,4,2,8,1280]{5,4,3,2,1,0:T(8,128)S(1)} %collective-permute-done.1) | copy-start | bytes 7864324
  50.8 14.7 %collective-permute-start.2 = (f32[1,4,4,2,8,512]{5,4,3,2,1,0:T(8,128)}, f32[1,4,4,2,8,512]{5,4,3,2,1,0:T(8,128)}, u32[]{:S(2)}, u32[]{:S(2)}) collective-permute-start(f32[1,4,4,2,8,512]{5,4,3,2,1,0:T(8,128)} %dynamic-slice_bitcast_fusion.1), channel_id=1, source_target_pairs={{0,1},{1,0},{2,3},{3,2},{4,5},{5,4},{6,7},{7,6},{8,9},{9,8},{10,11... | collective-permute-start | bytes 1572872 | tf_op jit(solution)/shard_map/ppermute | solution.py:79
  52.7 12.8 %copy-start.5 = (f32[1,8,4,2,8,512]{5,4,3,2,1,0:T(8,128)S(1)}, f32[1,8,4,2,8,512]{5,4,3,2,1,0:T(8,128)}, u32[]{:S(2)}) copy-start(f32[1,8,4,2,8,512]{5,4,3,2,1,0:T(8,128)} %copy-done.4) | copy-start | bytes 3145732
  55.0 34.8 %copy-start.3 = (f32[1,8,4,2,8,768]{5,4,3,2,1,0:T(8,128)S(1)}, f32[1,8,4,2,8,768]{5,4,3,2,1,0:T(8,128)}, u32[]{:S(2)}) copy-start(f32[1,8,4,2,8,768]{5,4,3,2,1,0:T(8,128)} %copy-done.2) | copy-start | bytes 4718596
  55.0 34.8 %collective-permute-start.7 = (f32[1,8,2,2,8,768]{5,4,3,2,1,0:T(8,128)}, f32[1,8,2,2,8,768]{5,4,3,2,1,0:T(8,128)S(1)}, u32[]{:S(2)}, u32[]{:S(2)}) collective-permute-start(f32[1,8,2,2,8,768]{5,4,3,2,1,0:T(8,128)} %dynamic-slice_bitcast_fusion), channel_id=1, source_target_pairs={{0,16},{16,0},{32,48},{48,32},{1,17},{17,1},{33,49},{49,33},{2,18}... | collective-permute-start | bytes 2359304 | tf_op jit(solution)/shard_map/ppermute | solution.py:79
  66.7 15.2 %collective-permute-start.3 = (f32[1,2,4,2,8,512]{5,4,3,2,1,0:T(8,128)S(1)}, f32[1,2,4,2,8,512]{5,4,3,2,1,0:T(8,128)}, u32[]{:S(2)}, u32[]{:S(2)}) collective-permute-start(f32[1,2,4,2,8,512]{5,4,3,2,1,0:T(8,128)S(1)} %dynamic-slice_bitcast_fusion.2), channel_id=1, source_target_pairs={{0,2},{1,3},{2,0},{3,1},{4,6},{5,7},{6,4},{7,5},{8,10},{9,11},{10,... | collective-permute-start | bytes 786440 | tf_op jit(solution)/shard_map/ppermute | solution.py:79
  83.6 12.4 %collective-permute-start.4 = (f32[1,1,4,2,8,512]{5,4,3,2,1,0:T(8,128)}, f32[1,1,4,2,8,512]{5,4,3,2,1,0:T(8,128)S(1)}, u32[]{:S(2)}, u32[]{:S(2)}) collective-permute-start(f32[1,1,4,2,8,512]{5,4,3,2,1,0:T(8,128)} %constant_dynamic-slice_fusion.5), channel_id=1, source_target_pairs={{0,4},{1,5},{2,6},{3,7},{4,0},{5,1},{6,2},{7,3},{8,12},{9,13},{10,... | collective-permute-start | bytes 393224 | tf_op jit(solution)/shard_map/ppermute | solution.py:79
  90.0 12.6 %collective-permute-start.8 = (f32[1,8,1,2,8,768]{5,4,3,2,1,0:T(8,128)S(1)}, f32[1,8,1,2,8,768]{5,4,3,2,1,0:T(8,128)S(1)}, u32[]{:S(2)}, u32[]{:S(2)}) collective-permute-start(f32[1,8,1,2,8,768]{5,4,3,2,1,0:T(8,128)S(1)} %constant_dynamic-slice_fusion.3), channel_id=1, source_target_pairs={{0,32},{16,48},{32,0},{48,16},{1,33},{17,49},{33,1},{49,17},{2,34}... | collective-permute-start | bytes 1179656 | tf_op jit(solution)/shard_map/ppermute | solution.py:79
  96.0 52.8 %copy-start.1 = (s32[1,8]{1,0:T(1,128)S(1)}, s32[1,8]{1,0:T(1,128)}, u32[]{:S(2)}) copy-start(s32[1,8]{1,0:T(1,128)} %param.9) | copy-start | bytes 100
  96.1 6.6 %collective-permute-start.5 = (f32[1,1,2,2,8,512]{5,4,3,2,1,0:T(8,128)S(1)}, f32[1,1,2,2,8,512]{5,4,3,2,1,0:T(8,128)S(1)}, u32[]{:S(2)}, u32[]{:S(2)}) collective-permute-start(f32[1,1,2,2,8,512]{5,4,3,2,1,0:T(8,128)S(1)} %dynamic-slice_bitcast_fusion.5), channel_id=1, source_target_pairs={{0,16},{16,0},{32,48},{48,32},{1,17},{17,1},{33,49},{49,33},{2,18}... | collective-permute-start | bytes 196616 | tf_op jit(solution)/shard_map/ppermute | solution.py:79
  102.6 5.8 %collective-permute-start.9 = (f32[1,4,1,2,8,768]{5,4,3,1,2,0:T(8,128)S(1)}, f32[1,4,1,2,8,768]{5,4,3,1,2,0:T(8,128)S(1)}, u32[]{:S(2)}, u32[]{:S(2)}) collective-permute-start(f32[1,4,1,2,8,768]{5,4,3,1,2,0:T(8,128)S(1)} %dynamic-slice_bitcast_fusion.3), channel_id=1, source_target_pairs={{0,1},{1,0},{2,3},{3,2},{4,5},{5,4},{6,7},{7,6},{8,9},{9,8},{10,11... | collective-permute-start | bytes 589832 | tf_op jit(solution)/shard_map/ppermute | solution.py:79
  108.4 6.1 %collective-permute-start.10 = (f32[1,2,1,2,8,768]{5,4,3,2,1,0:T(8,128)S(1)}, f32[1,2,1,2,8,768]{5,4,3,2,1,0:T(8,128)S(1)}, u32[]{:S(2)}, u32[]{:S(2)}) collective-permute-start(f32[1,2,1,2,8,768]{5,4,3,2,1,0:T(8,128)S(1)} %dynamic-slice_bitcast_fusion.4), channel_id=1, source_target_pairs={{0,2},{1,3},{2,0},{3,1},{4,6},{5,7},{6,4},{7,5},{8,10},{9,11},{10,... | collective-permute-start | bytes 294920 | tf_op jit(solution)/shard_map/ppermute | solution.py:79
  109.0 6.5 %collective-permute-start.6 = (f32[1,1,1,2,8,512]{5,4,3,2,1,0:T(8,128)S(1)}, f32[1,1,1,2,8,512]{5,4,3,2,1,0:T(8,128)S(1)}, u32[]{:S(2)}, u32[]{:S(2)}) collective-permute-start(f32[1,1,1,2,8,512]{5,4,3,2,1,0:T(8,128)S(1)} %constant_dynamic-slice_fusion.4), channel_id=1, source_target_pairs={{0,32},{16,48},{32,0},{48,16},{1,33},{17,49},{33,1},{49,17},{2,34}... | collective-permute-start | bytes 98312 | tf_op jit(solution)/shard_map/ppermute | solution.py:79
  114.6 8.1 %collective-permute-start.11 = (f32[1,1,1,2,8,768]{5,4,3,2,1,0:T(8,128)S(1)}, f32[1,1,1,2,8,768]{5,4,3,2,1,0:T(8,128)S(1)}, u32[]{:S(2)}, u32[]{:S(2)}) collective-permute-start(f32[1,1,1,2,8,768]{5,4,3,2,1,0:T(8,128)S(1)} %constant_dynamic-slice_fusion.2), channel_id=1, source_target_pairs={{0,4},{1,5},{2,6},{3,7},{4,0},{5,1},{6,2},{7,3},{8,12},{9,13},{10,... | collective-permute-start | bytes 147464 | tf_op jit(solution)/shard_map/ppermute | solution.py:79
  122.7 5.6 %collective-permute-start.12 = (f32[1,1,1,1,8,1280]{5,4,3,2,1,0:T(8,128)S(1)}, f32[1,1,1,1,8,1280]{5,4,3,2,1,0:T(8,128)S(1)}, u32[]{:S(2)}, u32[]{:S(2)}) collective-permute-start(f32[1,1,1,1,8,1280]{5,4,3,2,1,0:T(8,128)S(1)} %fusion.164), channel_id=1, source_target_pairs={{0,8},{8,0},{1,9},{9,1},{2,10},{10,2},{3,11},{11,3},{4,12},{12,4},... | collective-permute-start | bytes 122888 | tf_op jit(solution)/shard_map/ppermute | solution.py:79
  128.3 3.9 %collective-permute-start.13 = (f32[1,1,1,1,1,4,1280]{6,5,4,3,2,1,0:T(4,128)S(1)}, f32[1,1,1,1,1,4,1280]{6,5,4,3,2,1,0:T(4,128)S(1)}, u32[]{:S(2)}, u32[]{:S(2)}) collective-permute-start(f32[1,1,1,1,1,4,1280]{6,5,4,3,2,1,0:T(4,128)S(1)} %dynamic-slice_bitcast_fusion.6), channel_id=1, source_target_pairs={{0,128},{128,0},{1,129},{129,1},{2,130},{130,2},{3,131},{131,3},{4... | collective-permute-start | bytes 61448 | tf_op jit(solution)/shard_map/ppermute | solution.py:79
  132.2 12.8 %collective-permute-start.14 = (f32[1,1,1,1,1,4,1280]{6,5,4,3,2,1,0:T(4,128)S(1)}, f32[1,1,1,1,1,4,1280]{6,5,4,3,2,1,0:T(4,128)S(1)}, u32[]{:S(2)}, u32[]{:S(2)}) collective-permute-start(f32[1,1,1,1,1,4,1280]{6,5,4,3,2,1,0:T(4,128)S(1)} %bitcast_add_fusion.6), channel_id=1, source_target_pairs={{0,0},{1,64},{2,32},{3,96},{4,16},{5,80},{6,48},{7,112},{8,2},{9,6... | collective-permute-start | bytes 61448 | tf_op jit(solution)/shard_map/ppermute | solution.py:184
  (4 other events, 4.3 us)

commit v15 on v14

--- a/solution.py
+++ b/solution.py
@@ -172,7 +172,7 @@
 
     sent = lax.ppermute(core_half(1 - core), "core", [(i, i ^ 1) for i in range(cores)])
     slab = core_half(core) + sent
-    half = (width // 128 * 2 // 5) * 128
+    half = width - (width // 128 * 2 // 5) * 128
     left = exchange_scatter(slab[..., :half], "z", 1)
     right = exchange_scatter(slab[..., half:], "y", 2)
     left = exchange_scatter(left, "y", 2)

time: 149 us -> 153 us (1.027)
  starting transfers between devices: 24.8 us -> 35.8 us
  waiting for transfers between devices: 67.5 us -> 60.1 us
    ppermute x12, starting transfers between devices: 19.7 us -> 29.7 us  [exchange_scatter(): slab = mine + lax.ppermute(other, axis, pairs)]
    ppermute x12, waiting for transfers between devices: 56 us -> 49.8 us  [exchange_scatter(): slab = mine + lax.ppermute(other, axis, pairs)]
where the time goes in v15:
time: 153 us; the launch traced here: 152 us
  waiting for transfers between devices  60.1 us (39%)
  starting transfers between devices  35.8 us (23%)
  matrix products  26.5 us (17%)
  other arithmetic  17.1 us (11%)
  local copies, waits for them, and re-layouts  10.3 us (7%)
  between operations  2.59 us (2%)
    ppermute x12, waiting for transfers between devices, exchange_scatter(): slab = mine + lax.ppermute(other, axis, pairs)  49.8 us
    ppermute x12, starting transfers between devices, exchange_scatter(): slab = mine + lax.ppermute(other, axis, pairs)  29.7 us
    ppermute x1, waiting for transfers between devices, per_device(): slab = lax.ppermute(slab, FINE, owner_pairs(sizes))  9.69 us
    dot_general x10, matrix products, layer_math(): preact = jnp.dot(paired, conv_one, preferred_element_type=jnp.float32)  8.26 us
    dot_general x2, matrix products, core_half(): lax.dot_general(lhs, paired, (((0,), (0,)), ((), ())), preferred_element_...  7.95 us
    convert_element_type x9, other arithmetic, layer_math(): (jnp.tanh(preact[:, :gate_width]) * jax.nn.sigmoid(preact[:, gate_width:]...  7.07 us
    unnamed x35, local copies, waits for them, and re-layouts  6.39 us
    dot_general x1, matrix products, per_device(): skip_sum = jnp.dot(stacked, skip_weight, preferred_element_type=jnp.float32)  5.88 us
  transfers between devices with their start and end apart: 15, of which 11 were waited for; matrix products, arithmetic and copies ran while one was open for 6% of the time, Pallas kernels for 0%

profile of v15, /device:TPU:28, one launch (start us, length us, event | category | flops | bytes accessed | tf_op | source)
XLA Modules:
  0.0 152.4 jit_solution(15847924913354082230)
XLA Ops:
  0.6 1.7 %collective-permute-start = (f32[1,1024]{1,0:T(1,128)}, f32[1,1024]{1,0:T(1,128)S(1)}, u32[]{:S(2)}, u32[]{:S(2)}) collective-permute-start(f32[1,1024]{1,0:T(1,128)} %param.7), channel_id=1, source_target_pairs={{0,64},{64,128},{128,192},{1,65},{65,129},{129,193},{2,66},{66,130... | collective-permute-start | bytes 12296 | tf_op jit(solution)/shard_map/ppermute | solution.py:54
  5.6 1.7 %fusion.69 = f32[2048,512]{0,1:T(8,128)S(1)} fusion(bf16[2047,128]{1,0:T(8,128)(2,1)S(1)} %bitcast.124, bf16[2048,128]{1,0:T(8,128)(2,1)S(1)} %multiply_convert_fusion, bf16[10,256,512]{2,1,0:T(8,128)(2,1)} %param.11), kind=kOutput, calls=%fused_computation.106 | convolution fusion | flops 540016640 | bytes 5504768 | tf_op jit(solution)/shard_map/dot_general | solution.py:91
  29.3 5.9 %broadcast_select_fusion = bf16[1024,1024]{0,1:T(8,128)(2,1)S(1)} fusion(pred[1024]{0:T(1024)(128)(4,1)S(1)} %add_compare_fusion, bf16[1024,2560]{0,1:T(8,128)(2,1)S(1)} %fusion.118, bf16[2560,1024]{1,0:T(8,128)(2,1)S(1)} %bitcast.140), kind=kOutput, calls=%fused_computation.83 | convolution fusion | flops 5371854848 | bytes 12583936 | tf_op jit(solution)/shard_map/dot_general | solution.py:133
  35.2 3.8 %convolution_select_fusion = f32[512,1280]{1,0:T(8,128)} fusion(bf16[1024,256]{0,1:T(8,128)(2,1)S(1)} %fusion.93, bf16[1024,1024]{0,1:T(8,128)(2,1)S(1)} %broadcast_select_fusion, s32[512]{0:T(512)S(1)} %fusion.171, s32[512]{0:T(512)S(1)} %get-tuple-element.18, s32[512]{0:T(512)S(1)} %get-tuple-element.22, f32[]{:T(128)} %convert_reduce_fusion, ...), kind=kOutput, calls=%fused_computation.1 | convolution fusion | flops 1350696960 | bytes 6298120 | tf_op jit(solution)/shard_map/dot_general | solution.py:164
  38.9 1.5 collective-permute-start.1
  40.4 4.2 %convolution_select_fusion.1 = f32[512,1280]{1,0:T(8,128)S(1)} fusion(bf16[1024,256]{0,1:T(8,128)(2,1)S(1)} %fusion.93, bf16[1024,1024]{0,1:T(8,128)(2,1)} %copy-done.10, f32[]{:T(128)} %convert_reduce_fusion, s32[512]{0:T(512)S(1)} %fusion.172, s32[512]{0:T(512)S(1)} %get-tuple-element.19, s32[512]{0:T(512)S(1)} %get-tuple-element.23, ...), kind=kOutput, calls=%fused_computation.2 | convolution fusion | flops 1350696960 | bytes 6298628 | tf_op jit(solution)/shard_map/dot_general | solution.py:164
  45.2 1.5 copy-done.6
  46.6 2.2 %add.359 = f32[1,8,4,2,8,1280]{5,4,3,2,1,0:T(8,128)S(1)} add(f32[1,8,4,2,8,1280]{5,4,3,2,1,0:T(8,128)S(1)} %bitcast.130, f32[1,8,4,2,8,1280]{5,4,3,2,1,0:T(8,128)} %copy-done.6) | non-fusion elementwise | flops 655360 | bytes 7864320 | tf_op jit(solution)/shard_map/add | solution.py:174
  53.8 1.9 %collective-permute-start.2 = (f32[1,4,4,2,8,768]{5,4,3,2,1,0:T(8,128)}, f32[1,4,4,2,8,768]{5,4,3,2,1,0:T(8,128)S(1)}, u32[]{:S(2)}, u32[]{:S(2)}) collective-permute-start(f32[1,4,4,2,8,768]{5,4,3,2,1,0:T(8,128)} %dynamic-slice_bitcast_fusion), channel_id=1, source_target_pairs={{0,1},{1,0},{2,3},{3,2},{4,5},{5,4},{6,7},{7,6},{8,9},{9,8},{10,11... | collective-permute-start | bytes 2359304 | tf_op jit(solution)/shard_map/ppermute | solution.py:79
  55.7 9.6 %collective-permute-done.7 = f32[1,8,2,2,8,512]{5,4,3,2,1,0:T(8,128)} collective-permute-done((f32[1,8,2,2,8,512]{5,4,3,2,1,0:T(8,128)}, f32[1,8,2,2,8,512]{5,4,3,2,1,0:T(8,128)}, u32[]{:S(2)}, u32[]{:S(2)}) %collective-permute-start.7) | collective-permute-done | bytes 524320 | tf_op jit(solution)/shard_map/ppermute | solution.py:79
  66.5 1.3 collective-permute-start.8
  67.8 8.1 %collective-permute-done.8 = f32[1,8,1,2,8,512]{5,4,3,2,1,0:T(8,128)} collective-permute-done((f32[1,8,1,2,8,512]{5,4,3,2,1,0:T(8,128)S(1)}, f32[1,8,1,2,8,512]{5,4,3,2,1,0:T(8,128)}, u32[]{:S(2)}, u32[]{:S(2)}) %collective-permute-start.8) | collective-permute-done | bytes 262176 | tf_op jit(solution)/shard_map/ppermute | solution.py:79
  77.6 1.9 %collective-permute-start.9 = (f32[1,4,1,2,8,512]{5,4,3,1,2,0:T(8,128)}, f32[1,4,1,2,8,512]{5,4,3,1,2,0:T(8,128)S(1)}, u32[]{:S(2)}, u32[]{:S(2)}) collective-permute-start(f32[1,4,1,2,8,512]{5,4,3,1,2,0:T(8,128)} %dynamic-slice_bitcast_fusion.3), channel_id=1, source_target_pairs={{0,1},{1,0},{2,3},{3,2},{4,5},{5,4},{6,7},{7,6},{8,9},{9,8},{10,11... | collective-permute-start | bytes 393224 | tf_op jit(solution)/shard_map/ppermute | solution.py:79
  79.7 3.4 %collective-permute-start.3 = (f32[1,2,4,2,8,768]{5,4,3,2,1,0:T(8,128)S(1)}, f32[1,2,4,2,8,768]{5,4,3,2,1,0:T(8,128)S(1)}, u32[]{:S(2)}, u32[]{:S(2)}) collective-permute-start(f32[1,2,4,2,8,768]{5,4,3,2,1,0:T(8,128)S(1)} %dynamic-slice_bitcast_fusion.2), channel_id=1, source_target_pairs={{0,2},{1,3},{2,0},{3,1},{4,6},{5,7},{6,4},{7,5},{8,10},{9,11},{10,... | collective-permute-start | bytes 1179656 | tf_op jit(solution)/shard_map/ppermute | solution.py:79
  84.0 3.6 %collective-permute-start.10 = (f32[1,2,1,2,8,512]{5,4,3,2,1,0:T(8,128)S(1)}, f32[1,2,1,2,8,512]{5,4,3,2,1,0:T(8,128)S(1)}, u32[]{:S(2)}, u32[]{:S(2)}) collective-permute-start(f32[1,2,1,2,8,512]{5,4,3,2,1,0:T(8,128)S(1)} %dynamic-slice_bitcast_fusion.5), channel_id=1, source_target_pairs={{0,2},{1,3},{2,0},{3,1},{4,6},{5,7},{6,4},{7,5},{8,10},{9,11},{10,... | collective-permute-start | bytes 196616 | tf_op jit(solution)/shard_map/ppermute | solution.py:79
  87.6 13.7 %collective-permute-done.3 = f32[1,2,4,2,8,768]{5,4,3,2,1,0:T(8,128)S(1)} collective-permute-done((f32[1,2,4,2,8,768]{5,4,3,2,1,0:T(8,128)S(1)}, f32[1,2,4,2,8,768]{5,4,3,2,1,0:T(8,128)S(1)}, u32[]{:S(2)}, u32[]{:S(2)}) %collective-permute-start.3) | collective-permute-done | bytes 393248 | tf_op jit(solution)/shard_map/ppermute | solution.py:79
  101.3 5.8 %collective-permute-start.4 = (f32[1,1,4,2,8,768]{5,4,3,2,1,0:T(8,128)S(1)}, f32[1,1,4,2,8,768]{5,4,3,2,1,0:T(8,128)S(1)}, u32[]{:S(2)}, u32[]{:S(2)}) collective-permute-start(f32[1,1,4,2,8,768]{5,4,3,2,1,0:T(8,128)S(1)} %constant_dynamic-slice_fusion.5), channel_id=1, source_target_pairs={{0,4},{1,5},{2,6},{3,7},{4,0},{5,1},{6,2},{7,3},{8,12},{9,13},{10,... | collective-permute-start | bytes 589832 | tf_op jit(solution)/shard_map/ppermute | solution.py:79
  107.2 5.6 %collective-permute-done.4 = f32[1,1,4,2,8,768]{5,4,3,2,1,0:T(8,128)S(1)} collective-permute-done((f32[1,1,4,2,8,768]{5,4,3,2,1,0:T(8,128)S(1)}, f32[1,1,4,2,8,768]{5,4,3,2,1,0:T(8,128)S(1)}, u32[]{:S(2)}, u32[]{:S(2)}) %collective-permute-start.4) | collective-permute-done | bytes 196640 | tf_op jit(solution)/shard_map/ppermute | solution.py:79
  113.7 7.0 %collective-permute-start.11 = (f32[1,1,1,2,8,512]{5,4,3,2,1,0:T(8,128)S(1)}, f32[1,1,1,2,8,512]{5,4,3,2,1,0:T(8,128)S(1)}, u32[]{:S(2)}, u32[]{:S(2)}) collective-permute-start(f32[1,1,1,2,8,512]{5,4,3,2,1,0:T(8,128)S(1)} %constant_dynamic-slice_fusion.2), channel_id=1, source_target_pairs={{0,4},{1,5},{2,6},{3,7},{4,0},{5,1},{6,2},{7,3},{8,12},{9,13},{10,... | collective-permute-start | bytes 98312 | tf_op jit(solution)/shard_map/ppermute | solution.py:79
  122.6 3.8 %collective-permute-done.6 = f32[1,1,1,2,8,768]{5,4,3,2,1,0:T(8,128)S(1)} collective-permute-done((f32[1,1,1,2,8,768]{5,4,3,2,1,0:T(8,128)S(1)}, f32[1,1,1,2,8,768]{5,4,3,2,1,0:T(8,128)S(1)}, u32[]{:S(2)}, u32[]{:S(2)}) %collective-permute-start.6) | collective-permute-done | bytes 49184 | tf_op jit(solution)/shard_map/ppermute | solution.py:79
  127.3 4.7 %collective-permute-done.12 = f32[1,1,1,1,8,1280]{5,4,3,2,1,0:T(8,128)S(1)} collective-permute-done((f32[1,1,1,1,8,1280]{5,4,3,2,1,0:T(8,128)S(1)}, f32[1,1,1,1,8,1280]{5,4,3,2,1,0:T(8,128)S(1)}, u32[]{:S(2)}, u32[]{:S(2)}) %collective-permute-start.12) | collective-permute-done | bytes 40992 | tf_op jit(solution)/shard_map/ppermute | solution.py:79
  133.4 2.6 %collective-permute-done.13 = f32[1,1,1,1,1,4,1280]{6,5,4,3,2,1,0:T(4,128)S(1)} collective-permute-done((f32[1,1,1,1,1,4,1280]{6,5,4,3,2,1,0:T(4,128)S(1)}, f32[1,1,1,1,1,4,1280]{6,5,4,3,2,1,0:T(4,128)S(1)}, u32[]{:S(2)}, u32[]{:S(2)}) %collective-permute-start.13) | collective-permute-done | bytes 20512 | tf_op jit(solution)/shard_map/ppermute | solution.py:79
  136.0 2.9 %collective-permute-start.14 = (f32[1,1,1,1,1,4,1280]{6,5,4,3,2,1,0:T(4,128)S(1)}, f32[1,1,1,1,1,4,1280]{6,5,4,3,2,1,0:T(4,128)S(1)}, u32[]{:S(2)}, u32[]{:S(2)}) collective-permute-start(f32[1,1,1,1,1,4,1280]{6,5,4,3,2,1,0:T(4,128)S(1)} %bitcast_add_fusion.6), channel_id=1, source_target_pairs={{0,0},{1,64},{2,32},{3,96},{4,16},{5,80},{6,48},{7,112},{8,2},{9,6... | collective-permute-start | bytes 61448 | tf_op jit(solution)/shard_map/ppermute | solution.py:184
  138.9 9.7 %collective-permute-done.14 = f32[1,1,1,1,1,4,1280]{6,5,4,3,2,1,0:T(4,128)S(1)} collective-permute-done((f32[1,1,1,1,1,4,1280]{6,5,4,3,2,1,0:T(4,128)S(1)}, f32[1,1,1,1,1,4,1280]{6,5,4,3,2,1,0:T(4,128)S(1)}, u32[]{:S(2)}, u32[]{:S(2)}) %collective-permute-start.14) | collective-permute-done | bytes 20512 | tf_op jit(solution)/shard_map/ppermute | solution.py:184
  (126 shorter events, 41.9 us)
Async XLA Ops:
  0.6 1.8 %copy-start = (s32[1,8]{1,0:T(1,128)S(1)}, s32[1,8]{1,0:T(1,128)}, u32[]{:S(2)}) copy-start(s32[1,8]{1,0:T(1,128)} %param.9) | copy-start | bytes 100
  0.6 3.3 %collective-permute-start = (f32[1,1024]{1,0:T(1,128)}, f32[1,1024]{1,0:T(1,128)S(1)}, u32[]{:S(2)}, u32[]{:S(2)}) collective-permute-start(f32[1,1024]{1,0:T(1,128)} %param.7), channel_id=1, source_target_pairs={{0,64},{64,128},{128,192},{1,65},{65,129},{129,193},{2,66},{66,130... | collective-permute-start | bytes 12296 | tf_op jit(solution)/shard_map/ppermute | solution.py:54
  8.2 1.8 %copy-start.7 = (bf16[10,256,512]{2,1,0:T(8,128)(2,1)S(1)}, bf16[10,256,512]{2,1,0:T(8,128)(2,1)}, u32[]{:S(2)}) copy-start(bf16[10,256,512]{2,1,0:T(8,128)(2,1)} %param.11) | copy-start | bytes 7864324
  26.5 2.2 %slice-start = ((s8[5242880]{0:T(1024)(128)(4,1)}), s8[4194304]{0:T(1024)(128)(4,1)S(1)}, s32[]{:S(2)}) async-start(s8[5242880]{0:T(1024)(128)(4,1)} %bitcast.139), calls=%async_computation | async-start | bytes 8388608
  27.6 1.7 %slice-start.1 = ((s8[5242880]{0:T(1024)(128)(4,1)}), s8[1048576]{0:T(1024)(128)(4,1)S(1)}, s32[]{:S(2)}) async-start(s8[5242880]{0:T(1024)(128)(4,1)} %bitcast.139), calls=%async_computation.1 | async-start | bytes 2097152
  35.1 3.8 %copy-start.10 = (bf16[1024,1024]{0,1:T(8,128)(2,1)}, bf16[1024,1024]{0,1:T(8,128)(2,1)S(1)}, u32[]{:S(2)}) copy-start(bf16[1024,1024]{0,1:T(8,128)(2,1)S(1)} %broadcast_select_fusion) | copy-start | bytes 6291460
  38.9 6.2 %collective-permute-start.1 = (f32[1,8,4,2,8,1280]{5,4,3,2,1,0:T(8,128)}, f32[1,8,4,2,8,1280]{5,4,3,2,1,0:T(8,128)S(1)}, u32[]{:S(2)}, u32[]{:S(2)}) collective-permute-start(f32[1,8,4,2,8,1280]{5,4,3,2,1,0:T(8,128)} %bitcast.24), channel_id=1, source_target_pairs={{0,64},{64,0},{1,65},{65,1},{2,66},{66,2},{3,67},{67,3},{4,68},{68... | collective-permute-start | bytes 7864328 | tf_op jit(solution)/shard_map/ppermute | solution.py:173
  45.2 1.5 copy-start.6
  50.8 14.5 %collective-permute-start.7 = (f32[1,8,2,2,8,512]{5,4,3,2,1,0:T(8,128)}, f32[1,8,2,2,8,512]{5,4,3,2,1,0:T(8,128)}, u32[]{:S(2)}, u32[]{:S(2)}) collective-permute-start(f32[1,8,2,2,8,512]{5,4,3,2,1,0:T(8,128)} %dynamic-slice_bitcast_fusion.1), channel_id=1, source_target_pairs={{0,16},{16,0},{32,48},{48,32},{1,17},{17,1},{33,49},{49,33},{2,18}... | collective-permute-start | bytes 1572872 | tf_op jit(solution)/shard_map/ppermute | solution.py:79
  51.6 13.8 %copy-start.5 = (f32[1,8,4,2,8,512]{5,4,3,2,1,0:T(8,128)S(1)}, f32[1,8,4,2,8,512]{5,4,3,2,1,0:T(8,128)}, u32[]{:S(2)}) copy-start(f32[1,8,4,2,8,512]{5,4,3,2,1,0:T(8,128)} %copy-done.4) | copy-start | bytes 3145732
  53.8 25.7 %copy-start.3 = (f32[1,8,4,2,8,768]{5,4,3,2,1,0:T(8,128)S(1)}, f32[1,8,4,2,8,768]{5,4,3,2,1,0:T(8,128)}, u32[]{:S(2)}) copy-start(f32[1,8,4,2,8,768]{5,4,3,2,1,0:T(8,128)} %copy-done.2) | copy-start | bytes 4718596
  53.8 25.7 %collective-permute-start.2 = (f32[1,4,4,2,8,768]{5,4,3,2,1,0:T(8,128)}, f32[1,4,4,2,8,768]{5,4,3,2,1,0:T(8,128)S(1)}, u32[]{:S(2)}, u32[]{:S(2)}) collective-permute-start(f32[1,4,4,2,8,768]{5,4,3,2,1,0:T(8,128)} %dynamic-slice_bitcast_fusion), channel_id=1, source_target_pairs={{0,1},{1,0},{2,3},{3,2},{4,5},{5,4},{6,7},{7,6},{8,9},{9,8},{10,11... | collective-permute-start | bytes 2359304 | tf_op jit(solution)/shard_map/ppermute | solution.py:79
  66.5 9.4 %collective-permute-start.8 = (f32[1,8,1,2,8,512]{5,4,3,2,1,0:T(8,128)S(1)}, f32[1,8,1,2,8,512]{5,4,3,2,1,0:T(8,128)}, u32[]{:S(2)}, u32[]{:S(2)}) collective-permute-start(f32[1,8,1,2,8,512]{5,4,3,2,1,0:T(8,128)S(1)} %constant_dynamic-slice_fusion.3), channel_id=1, source_target_pairs={{0,32},{16,48},{32,0},{48,16},{1,33},{17,49},{33,1},{49,17},{2,34}... | collective-permute-start | bytes 786440 | tf_op jit(solution)/shard_map/ppermute | solution.py:79
  77.6 6.3 %collective-permute-start.9 = (f32[1,4,1,2,8,512]{5,4,3,1,2,0:T(8,128)}, f32[1,4,1,2,8,512]{5,4,3,1,2,0:T(8,128)S(1)}, u32[]{:S(2)}, u32[]{:S(2)}) collective-permute-start(f32[1,4,1,2,8,512]{5,4,3,1,2,0:T(8,128)} %dynamic-slice_bitcast_fusion.3), channel_id=1, source_target_pairs={{0,1},{1,0},{2,3},{3,2},{4,5},{5,4},{6,7},{7,6},{8,9},{9,8},{10,11... | collective-permute-start | bytes 393224 | tf_op jit(solution)/shard_map/ppermute | solution.py:79
  79.7 21.6 %collective-permute-start.3 = (f32[1,2,4,2,8,768]{5,4,3,2,1,0:T(8,128)S(1)}, f32[1,2,4,2,8,768]{5,4,3,2,1,0:T(8,128)S(1)}, u32[]{:S(2)}, u32[]{:S(2)}) collective-permute-start(f32[1,2,4,2,8,768]{5,4,3,2,1,0:T(8,128)S(1)} %dynamic-slice_bitcast_fusion.2), channel_id=1, source_target_pairs={{0,2},{1,3},{2,0},{3,1},{4,6},{5,7},{6,4},{7,5},{8,10},{9,11},{10,... | collective-permute-start | bytes 1179656 | tf_op jit(solution)/shard_map/ppermute | solution.py:79
  83.9 68.5 %copy-start.1 = (s32[1,8]{1,0:T(1,128)S(1)}, s32[1,8]{1,0:T(1,128)}, u32[]{:S(2)}) copy-start(s32[1,8]{1,0:T(1,128)} %param.9) | copy-start | bytes 100
  84.0 23.2 %collective-permute-start.10 = (f32[1,2,1,2,8,512]{5,4,3,2,1,0:T(8,128)S(1)}, f32[1,2,1,2,8,512]{5,4,3,2,1,0:T(8,128)S(1)}, u32[]{:S(2)}, u32[]{:S(2)}) collective-permute-start(f32[1,2,1,2,8,512]{5,4,3,2,1,0:T(8,128)S(1)} %dynamic-slice_bitcast_fusion.5), channel_id=1, source_target_pairs={{0,2},{1,3},{2,0},{3,1},{4,6},{5,7},{6,4},{7,5},{8,10},{9,11},{10,... | collective-permute-start | bytes 196616 | tf_op jit(solution)/shard_map/ppermute | solution.py:79
  101.3 11.5 %collective-permute-start.4 = (f32[1,1,4,2,8,768]{5,4,3,2,1,0:T(8,128)S(1)}, f32[1,1,4,2,8,768]{5,4,3,2,1,0:T(8,128)S(1)}, u32[]{:S(2)}, u32[]{:S(2)}) collective-permute-start(f32[1,1,4,2,8,768]{5,4,3,2,1,0:T(8,128)S(1)} %constant_dynamic-slice_fusion.5), channel_id=1, source_target_pairs={{0,4},{1,5},{2,6},{3,7},{4,0},{5,1},{6,2},{7,3},{8,12},{9,13},{10,... | collective-permute-start | bytes 589832 | tf_op jit(solution)/shard_map/ppermute | solution.py:79
  112.9 7.8 %collective-permute-start.5 = (f32[1,1,2,2,8,768]{5,4,3,2,1,0:T(8,128)S(1)}, f32[1,1,2,2,8,768]{5,4,3,2,1,0:T(8,128)S(1)}, u32[]{:S(2)}, u32[]{:S(2)}) collective-permute-start(f32[1,1,2,2,8,768]{5,4,3,2,1,0:T(8,128)S(1)} %dynamic-slice_bitcast_fusion.4), channel_id=1, source_target_pairs={{0,16},{16,0},{32,48},{48,32},{1,17},{17,1},{33,49},{49,33},{2,18}... | collective-permute-start | bytes 294920 | tf_op jit(solution)/shard_map/ppermute | solution.py:79
  113.7 8.9 %collective-permute-start.11 = (f32[1,1,1,2,8,512]{5,4,3,2,1,0:T(8,128)S(1)}, f32[1,1,1,2,8,512]{5,4,3,2,1,0:T(8,128)S(1)}, u32[]{:S(2)}, u32[]{:S(2)}) collective-permute-start(f32[1,1,1,2,8,512]{5,4,3,2,1,0:T(8,128)S(1)} %constant_dynamic-slice_fusion.2), channel_id=1, source_target_pairs={{0,4},{1,5},{2,6},{3,7},{4,0},{5,1},{6,2},{7,3},{8,12},{9,13},{10,... | collective-permute-start | bytes 98312 | tf_op jit(solution)/shard_map/ppermute | solution.py:79
  120.7 5.7 %collective-permute-start.6 = (f32[1,1,1,2,8,768]{5,4,3,2,1,0:T(8,128)S(1)}, f32[1,1,1,2,8,768]{5,4,3,2,1,0:T(8,128)S(1)}, u32[]{:S(2)}, u32[]{:S(2)}) collective-permute-start(f32[1,1,1,2,8,768]{5,4,3,2,1,0:T(8,128)S(1)} %constant_dynamic-slice_fusion.4), channel_id=1, source_target_pairs={{0,32},{16,48},{32,0},{48,16},{1,33},{17,49},{33,1},{49,17},{2,34}... | collective-permute-start | bytes 147464 | tf_op jit(solution)/shard_map/ppermute | solution.py:79
  126.4 5.6 %collective-permute-start.12 = (f32[1,1,1,1,8,1280]{5,4,3,2,1,0:T(8,128)S(1)}, f32[1,1,1,1,8,1280]{5,4,3,2,1,0:T(8,128)S(1)}, u32[]{:S(2)}, u32[]{:S(2)}) collective-permute-start(f32[1,1,1,1,8,1280]{5,4,3,2,1,0:T(8,128)S(1)} %fusion.164), channel_id=1, source_target_pairs={{0,8},{8,0},{1,9},{9,1},{2,10},{10,2},{3,11},{11,3},{4,12},{12,4},... | collective-permute-start | bytes 122888 | tf_op jit(solution)/shard_map/ppermute | solution.py:79
  132.1 3.9 %collective-permute-start.13 = (f32[1,1,1,1,1,4,1280]{6,5,4,3,2,1,0:T(4,128)S(1)}, f32[1,1,1,1,1,4,1280]{6,5,4,3,2,1,0:T(4,128)S(1)}, u32[]{:S(2)}, u32[]{:S(2)}) collective-permute-start(f32[1,1,1,1,1,4,1280]{6,5,4,3,2,1,0:T(4,128)S(1)} %dynamic-slice_bitcast_fusion.6), channel_id=1, source_target_pairs={{0,128},{128,0},{1,129},{129,1},{2,130},{130,2},{3,131},{131,3},{4... | collective-permute-start | bytes 61448 | tf_op jit(solution)/shard_map/ppermute | solution.py:79
  136.0 12.6 %collective-permute-start.14 = (f32[1,1,1,1,1,4,1280]{6,5,4,3,2,1,0:T(4,128)S(1)}, f32[1,1,1,1,1,4,1280]{6,5,4,3,2,1,0:T(4,128)S(1)}, u32[]{:S(2)}, u32[]{:S(2)}) collective-permute-start(f32[1,1,1,1,1,4,1280]{6,5,4,3,2,1,0:T(4,128)S(1)} %bitcast_add_fusion.6), channel_id=1, source_target_pairs={{0,0},{1,64},{2,32},{3,96},{4,16},{5,80},{6,48},{7,112},{8,2},{9,6... | collective-permute-start | bytes 61448 | tf_op jit(solution)/shard_map/ppermute | solution.py:184
  (4 other events, 4.3 us)
